TPU v7x, 128 devices: a whole 4x4x4 slice. The times are simulated.
128 devices in a mesh: ctl: 32 (over y, z_lo, x), side: 2 (over core), tp: 2 (over z_hi).
Axes of the slice: x: 4, y: 4, z: 4 (z_hi: 2, z_lo: 2; z = z_hi * 2 + z_lo), core: 2. Of those that a mesh axis runs over, the one named last changes fastest.
Arguments:
- image_latent: bfloat16 [64, 256, 3072], P('ctl'), may hold values from -6 to 6
- control_latent: bfloat16 [64, 256, 3072], P('ctl'), may hold values from -6 to 6
- control_order: int32 [64, 256], P('ctl'), may hold values from 0 to 255, each once within a row
- captions: bfloat16 [128, 128, 3072], P('ctl'), may hold values from -6 to 6
- caption_ids: int32 [64], P('ctl'), may hold values from 0 to 3
- modulation: float32 [2, 64, 3, 3072], P('side', 'ctl'), may hold values from -3 to 3
- qkv_weight: bfloat16 [2, 3072, 3, 1536], P('side', 'ctl', None, 'tp'), may hold values from -1 to 1
- qk_gain: float32 [2, 2, 128], P('side'), may hold values from 1 to 6
- out_weight: bfloat16 [2, 1536, 3072], P('side', 'tp', 'ctl'), may hold values from -0.5 to 0.5
- zero_weight: bfloat16 [3072, 3072], P('ctl', 'tp'), may hold values from -0.109375 to 0.109375
- proj_weight: bfloat16 [3072, 64], P('tp'), may hold values from -1 to 1
- final_mod: float32 [64, 2, 3072], P('ctl'), may hold values from -3 to 3
- velocity_target: float32 [64, 256, 64], P('ctl'), may hold values from -6 to 6
Outputs:
- hidden_out: bfloat16 [2, 64, 256, 3072], P('side', 'ctl', None, 'tp')
- zero_grad: float32 [3072, 3072], P(('ctl', 'side'), 'tp')
Inputs may be any that keep to these rules, and one draw needn't show every extreme that they name: caption_ids counts from the first caption held by the sample's own index of ctl. Each sample's row of control_order is a permutation.
All inputs are finite; a program needn't handle non-finite values.
Results may differ from a plain program's by a relative error of at most 0.03.
Values may be sent and summed in bfloat16 or wider, within the bound.
No kernel may reach another device: no remote copies, remote signals or barrier semaphores. Data moves between devices by JAX's collectives and lax.ppermute only.
A program may use at most 192 MiB of HBM per device.

v0:
```python
import math

import jax
import jax.numpy as jnp
from jax import lax
from jax.sharding import PartitionSpec as P

HEAD_DIM = 128


EPS = 1e-06


def passed_along(shard, axis, by):
    length = lax.axis_size(axis)
    pairs = [(i, i + by) for i in range(length) if 0 <= i + by < length]
    return lax.ppermute(shard, axis, pairs)


def partner(value, axis, bit):
    mask = 2**bit
    pairs = [(source, source ^ mask) for source in range(lax.axis_size(axis))]
    return lax.ppermute(value, axis, pairs)


def layer_norm(values):
    center = values - jnp.mean(values, axis=-1, keepdims=True)
    spread = jnp.mean(center * center, axis=-1, keepdims=True)
    return center * lax.rsqrt(spread + EPS)


def head_norm(values, gain_row):
    power_mean = jnp.mean(values * values, axis=-1, keepdims=True)
    return (values * lax.rsqrt(power_mean + EPS) * gain_row).astype(jnp.bfloat16)


def rounded(values):
    narrow = lax.optimization_barrier(values.astype(jnp.bfloat16))
    return narrow.astype(jnp.float32)


def local(
    image_latent,
    control_latent,
    control_order,
    captions,
    caption_ids,
    modulation,
    qkv_weight,
    qk_gain,
    out_weight,
    zero_weight,
    proj_weight,
    final_mod,
    velocity_target,
):
    side_index = lax.axis_index("side")
    tp_index = lax.axis_index("tp")
    ctl_count = lax.axis_size("ctl")
    tp_count = lax.axis_size("tp")
    is_control = side_index == 0
    micro_count, img_rows, width_full = image_latent.shape
    text_rows = captions.shape[1]
    seq_rows = text_rows + img_rows
    local_heads = qkv_weight.shape[3]
    head_count = local_heads // HEAD_DIM
    half_width = width_full // tp_count
    quarter_width = half_width // 2
    flat_rows = micro_count * img_rows
    block_rows = width_full // (2 * ctl_count)
    aligned = jax.vmap(lambda latent, order_row: jnp.take(latent, order_row, axis=0))(
        control_latent, control_order
    )
    plain_rows = image_latent.astype(jnp.float32)
    hidden = plain_rows + jnp.where(is_control, 1.0, 0.0) * aligned.astype(jnp.float32)
    chosen = jnp.take(captions, caption_ids, axis=0).astype(jnp.float32)
    sequence = jnp.concatenate([chosen, hidden], axis=1)
    modulate = modulation[0]
    normed = (layer_norm(sequence) * (1.0 + modulate[:, 1:2]) + modulate[:, 0:1]).astype(
        jnp.bfloat16
    )
    text_flat = normed.reshape(micro_count * seq_rows, width_full)
    image_flat = normed[:, text_rows:].reshape(flat_rows, width_full)
    shard_piece = lax.all_gather(qkv_weight, "ctl", axis=1, tiled=True)
    count_rows = shard_piece.shape[1]
    query_acc = jnp.dot(image_flat, shard_piece[0, :, 0], preferred_element_type=jnp.float32)
    pair_weight = shard_piece[0, :, 1:].reshape(count_rows, 2 * local_heads)
    pair_acc = jnp.dot(text_flat, pair_weight, preferred_element_type=jnp.float32)
    query_acc, pair_acc = (query_acc, pair_acc)
    gain_pair = qk_gain[0]
    queries = head_norm(
        query_acc.reshape(micro_count, img_rows, head_count, HEAD_DIM), gain_pair[0]
    )
    pair_acc = pair_acc.reshape(micro_count, seq_rows, 2, head_count, HEAD_DIM)
    keys_all = head_norm(pair_acc[:, :, 0], gain_pair[1])
    values_all = pair_acc[:, :, 1].astype(jnp.bfloat16)
    scores = jnp.einsum(
        "bihd,bjhd->bhij", queries, keys_all, preferred_element_type=jnp.float32
    ) / math.sqrt(HEAD_DIM)
    attend = jax.nn.softmax(scores, axis=-1).astype(jnp.bfloat16)
    mixed_heads = jnp.einsum(
        "bhij,bjhd->bihd", attend, values_all, preferred_element_type=jnp.float32
    )
    mixed_heads = mixed_heads.astype(jnp.bfloat16).reshape(flat_rows, local_heads)
    partial_value = rounded(
        jnp.dot(
            mixed_heads,
            lax.all_gather(out_weight, "ctl", axis=2, tiled=True)[0],
            preferred_element_type=jnp.float32,
        )
    )
    head_sum = lax.psum_scatter(
        partial_value.astype(jnp.bfloat16), "tp", scatter_dimension=1, tiled=True
    ).astype(jnp.float32)
    hid_half = lax.dynamic_slice_in_dim(hidden, tp_index * half_width, half_width, 2)
    gate_half = lax.dynamic_slice_in_dim(modulate[:, 2:3], tp_index * half_width, half_width, 2)
    act_half = hid_half + gate_half * head_sum.reshape(micro_count, img_rows, half_width)
    act_half = act_half.reshape(flat_rows, half_width)
    act_narrow = lax.all_gather(act_half.astype(jnp.bfloat16), "tp", axis=1, tiled=True)
    act_other = passed_along(act_narrow, "side", 1)
    control_rows = jnp.where(is_control, act_narrow, act_other)
    own_cols = lax.dynamic_slice_in_dim(zero_weight, side_index * quarter_width, quarter_width, 1)
    columns = control_rows
    own_part = jnp.dot(
        columns,
        lax.all_gather(own_cols, "ctl", axis=0, tiled=True),
        preferred_element_type=jnp.float32,
    )
    own_narrow = own_part.astype(jnp.bfloat16)
    other_narrow = partner(own_narrow, "side", 0)
    residual_narrow = jnp.where(
        is_control,
        jnp.concatenate([own_narrow, other_narrow], axis=1),
        jnp.concatenate([other_narrow, own_narrow], axis=1),
    )
    merged = act_half + residual_narrow.astype(jnp.float32)
    section_out = jnp.where(is_control, residual_narrow, merged.astype(jnp.bfloat16))
    final_half = lax.dynamic_slice_in_dim(final_mod, tp_index * half_width, half_width, 2)
    merged_rows = merged.reshape(micro_count, img_rows, half_width)
    row_total, squares = lax.psum(
        (
            jnp.sum(merged_rows, axis=-1, keepdims=True),
            jnp.sum(merged_rows * merged_rows, axis=-1, keepdims=True),
        ),
        "tp",
    )
    mean_val = row_total / width_full
    spread = squares / width_full - mean_val * mean_val
    scale_inv = lax.rsqrt(spread + EPS)
    unit_rows = (merged_rows - mean_val) * scale_inv
    final_in = (unit_rows * (1.0 + final_half[:, 1:2]) + final_half[:, 0:1]).astype(jnp.bfloat16)
    prediction = lax.psum(
        jnp.dot(
            final_in.reshape(flat_rows, half_width), proj_weight, preferred_element_type=jnp.float32
        ).astype(jnp.bfloat16),
        "tp",
    ).astype(jnp.float32)
    loss_factor = 4.0 / math.sqrt(micro_count * ctl_count * img_rows)
    grad_pred = (loss_factor * (prediction - velocity_target.reshape(flat_rows, -1))).astype(
        jnp.bfloat16
    )
    grad_unit = lax.dot_general(
        grad_pred, proj_weight, (((1,), (1,)), ((), ())), preferred_element_type=jnp.float32
    )
    grad_unit = grad_unit.reshape(micro_count, img_rows, half_width) * (1.0 + final_half[:, 1:2])
    first_sum, second_sum = lax.psum(
        (
            jnp.sum(grad_unit, axis=-1, keepdims=True),
            jnp.sum(grad_unit * unit_rows, axis=-1, keepdims=True),
        ),
        "tp",
    )
    grad_narrow = (
        (grad_unit - first_sum / width_full - unit_rows * (second_sum / width_full)) * scale_inv
    ).astype(jnp.bfloat16)
    grad_narrow = grad_narrow.reshape(flat_rows, half_width)
    returned = passed_along(grad_narrow, "side", -1)
    grad_rows_all = jnp.where(is_control, returned, grad_narrow)
    own_act = lax.dynamic_index_in_dim(
        control_rows.reshape(flat_rows, ctl_count, 2, block_rows), side_index, 2, keepdims=False
    )
    own_act = own_act.reshape(flat_rows, ctl_count * block_rows)
    columns = own_act
    product = lax.dot_general(
        columns, grad_rows_all, (((0,), (0,)), ((), ())), preferred_element_type=jnp.float32
    )
    zero_grad = lax.psum_scatter(
        rounded(product).astype(jnp.bfloat16), "ctl", scatter_dimension=0, tiled=True
    ).astype(jnp.float32)
    return (section_out.reshape(1, micro_count, img_rows, half_width), zero_grad)


def solution(mesh):
    return jax.shard_map(
        local,
        mesh=mesh,
        in_specs=(
            P("ctl", None, None),
            P("ctl", None, None),
            P("ctl", None),
            P("ctl", None, None),
            P("ctl"),
            P("side", "ctl", None, None),
            P("side", "ctl", None, "tp"),
            P("side", None, None),
            P("side", "tp", "ctl"),
            P("ctl", "tp"),
            P("tp", None),
            P("ctl", None, None),
            P("ctl", None, None),
        ),
        out_specs=(P("side", "ctl", None, "tp"), P(("ctl", "side"), "tp")),
        check_vma=False,
    )
```

profile of v0, /device:TPU:0, one launch (start us, length us, event | category | flops | bytes accessed | tf_op | source)
XLA Modules:
  0.0 868.4 jit_solution(13904714863020489514)
XLA Ops:
  12.2 14.7 %gather_fusion.1 = bf16[512,3072]{1,0:T(8,128)(2,1)} fusion(bf16[2,256,3072]{2,1,0:T(8,128)(2,1)S(1)} %copy-done, s32[512]{0:T(512)S(1)} %bitcast.114), kind=kCustom, calls=%fused_computation.1 | custom fusion | bytes 6295552 | tf_op jit(solution)/shard_map/vmap(jit(_take))/gather | solution.py:71
  26.9 7.2 multiply_add_fusion
  46.4 144.6 %all-gather.5.cloned.1.call-done = bf16[1,3072,3,768]{3,1,2,0:T(8,128)(2,1)} async-done(((bf16[1,96,3,768]{3,1,2,0:T(8,128)(2,1)}), bf16[1,3072,3,768]{3,1,2,0:T(8,128)(2,1)}) %all-gather.5.cloned.1.call-update) | async-done | bytes 14155792 | tf_op jit(solution)/shard_map/all_gather | solution.py:84
  191.0 7.8 slice.59
  198.9 12.7 %copy.37 = bf16[1,3072,2,768]{1,3,2,0:T(8,128)(2,1)} copy(bf16[1,3072,2,768]{3,1,2,0:T(8,128)(2,1)} %slice.59) | data formatting | bytes 18874368
  211.5 4.8 slice_bitcast_fusion
  216.3 6.7 copy.25
  223.0 11.8 %fusion.2 = f32[2,384,2,6,128]{1,4,3,2,0:T(8,128)S(1)} fusion(bf16[2,6,128,3072,1]{3,2,1,0,4:T(8,128)(2,1)} %bitcast.117, bf16[2,384,3072]{2,1,0:T(8,128)(2,1)} %add_convert_fusion), kind=kOutput, calls=%fused_computation.10 | convolution fusion | flops 7247757312 | bytes 18874368 | tf_op jit(solution)/shard_map/dot_general | solution.py:88
  235.1 6.0 multiply_reduce_fusion.5
  245.9 10.0 %fusion.21 = bf16[2,256,6,128]{1,3,2,0:T(8,128)(2,1)S(1)} fusion(f32[2,6,256]{2,1,0:T(8,128)S(1)} %fusion.44, f32[2,384,2,6,128]{1,4,3,2,0:T(8,128)} %copy-done.7, f32[2,6,256,384]{3,2,1,0:T(8,128)} %copy-done.3), kind=kOutput, calls=%fused_computation.48 | convolution fusion | flops 308284800 | bytes 11415552 | tf_op jit(solution)/shard_map/bhij,bjhd->bihd/dot_general | solution.py:101
  257.0 91.9 %all-gather.7.cloned.1.call-done = bf16[1,768,3072]{1,2,0:T(8,128)(2,1)} async-done(((bf16[1,768,96]{1,2,0:T(8,128)(2,1)}), bf16[1,768,3072]{1,2,0:T(8,128)(2,1)}) %all-gather.7.cloned.1.call-update) | async-done | bytes 4718608 | tf_op jit(solution)/shard_map/all_gather | solution.py:108
  348.9 6.4 fusion.6
  355.4 47.4 %reduce-scatter.3.cloned.1.call-done = bf16[512,1536]{1,0:T(8,128)(2,1)} async-done(((bf16[512,3072]{1,0:T(8,128)(2,1)}), bf16[512,1536]{1,0:T(8,128)(2,1)}) %reduce-scatter.3.cloned.1.call-update) | async-done | bytes 1572880 | tf_op jit(solution)/shard_map/reduce_scatter | solution.py:112
  408.3 47.6 %all-gather.9.cloned.1.call-done = bf16[512,3072]{0,1:T(8,128)(2,1)} async-done(((bf16[512,1536]{0,1:T(8,128)(2,1)}), bf16[512,3072]{0,1:T(8,128)(2,1)}) %all-gather.9.cloned.1.call-update) | async-done | bytes 3145744 | tf_op jit(solution)/shard_map/all_gather | solution.py:119
  457.7 5.3 collective-permute-done
  465.3 149.6 %all-gather.11.cloned.1.call-done = bf16[3072,768]{1,0:T(8,128)(2,1)} async-done(((bf16[96,768]{1,0:T(8,128)(2,1)}), bf16[3072,768]{1,0:T(8,128)(2,1)}) %all-gather.11.cloned.1.call-update) | async-done | bytes 4718608 | tf_op jit(solution)/shard_map/all_gather | solution.py:126
  614.9 5.9 convolution_convert_fusion.1
  627.3 6.6 all-reduce.1
  636.8 28.0 %all-reduce.4.cloned.1.call-done = bf16[512,64]{0,1:T(8,128)(2,1)} async-done(((bf16[512,64]{0,1:T(8,128)(2,1)}), bf16[512,64]{0,1:T(8,128)(2,1)}) %all-reduce.4.cloned.1.call-update) | async-done | bytes 65552 | tf_op jit(solution)/shard_map/psum | solution.py:152
  668.0 6.4 all-reduce
  674.4 4.0 multiply_convert_fusion
  683.9 4.2 convolution_convert_fusion
  688.2 4.7 select_bitcast_fusion
  692.8 167.0 %reduce-scatter.5.cloned.1.call-done = bf16[48,1536]{1,0:T(8,128)(2,1)} async-done(((bf16[1536,1536]{1,0:T(8,128)(2,1)}), bf16[48,1536]{1,0:T(8,128)(2,1)}) %reduce-scatter.5.cloned.1.call-update) | async-done | bytes 147472 | tf_op jit(solution)/shard_map/reduce_scatter | solution.py:187
  (91 shorter events, 52.5 us)
Async XLA Ops:
  7.2 5.0 copy-start
  7.2 183.8 %all-gather.5.cloned.1.call-start = ((), (), s32[]{:S(2)}) async-start(), calls=%async_computation.2 | async-start | bytes 14598144 | tf_op jit(solution)/shard_map/all_gather | solution.py:84
  7.9 340.9 %all-gather.7.cloned.1.call-start = ((), (), s32[]{:S(2)}) async-start(), calls=%async_computation.3 | async-start | bytes 4866048 | tf_op jit(solution)/shard_map/all_gather | solution.py:108
  8.7 394.1 %reduce-scatter.3.cloned.1.call-start = ((), (), s32[]{:S(2)}) async-start(), calls=%async_computation.4 | async-start | bytes 4718592 | tf_op jit(solution)/shard_map/reduce_scatter | solution.py:112
  26.9 7.2 copy-start.8
  35.9 5.4 slice-start
  37.8 3.7 slice-start.1
  223.0 12.1 %copy-start.6 = (bf16[768,3072]{1,0:T(8,128)(2,1)S(1)}, bf16[768,3072]{1,0:T(8,128)(2,1)}, u32[]{:S(2)}) copy-start(bf16[768,3072]{1,0:T(8,128)(2,1)} %copy.25) | copy-start | bytes 14155780
  234.9 6.3 copy-start.7
  242.1 2.1 copy-start.3
  355.3 100.6 %all-gather.9.cloned.1.call-start = ((), (), s32[]{:S(2)}) async-start(), calls=%async_computation.5 | async-start | bytes 4718592 | tf_op jit(solution)/shard_map/all_gather | solution.py:119
  405.6 1.9 copy-start.10
  407.5 207.4 %all-gather.11.cloned.1.call-start = ((), (), s32[]{:S(2)}) async-start(), calls=%async_computation.6 | async-start | bytes 4866048 | tf_op jit(solution)/shard_map/all_gather | solution.py:126
  408.2 256.6 %all-reduce.4.cloned.1.call-start = ((), (), s32[]{:S(2)}) async-start(), calls=%async_computation.7 | async-start | bytes 131072 | tf_op jit(solution)/shard_map/psum | solution.py:152
  455.9 7.0 collective-permute-start
  465.3 155.5 %copy-start.5 = (bf16[512,3072]{0,1:T(8,128)(2,1)}, bf16[512,3072]{0,1:T(8,128)(2,1)S(1)}, u32[]{:S(2)}) copy-start(bf16[512,3072]{0,1:T(8,128)(2,1)S(1)} %broadcast_select_fusion) | copy-start | bytes 9437188
  465.3 155.5 %copy-start.12 = (f32[2,2,3072]{2,1,0:T(2,128)S(1)}, f32[2,2,3072]{2,1,0:T(2,128)}, u32[]{:S(2)}) copy-start(f32[2,2,3072]{2,1,0:T(2,128)} %param.24) | copy-start | bytes 147460
  620.8 2.6 collective-permute-start.1
  627.3 47.1 %copy-start.2 = (f32[2,256,1536]{2,1,0:T(8,128)}, f32[2,256,1536]{2,1,0:T(8,128)S(1)}, u32[]{:S(2)}) copy-start(f32[2,256,1536]{2,1,0:T(8,128)S(1)} %get-tuple-element.8) | copy-start | bytes 9437188
  627.3 7.2 copy-start.9
  635.8 224.0 %reduce-scatter.5.cloned.1.call-start = ((), (), s32[]{:S(2)}) async-start(), calls=%async_computation.8 | async-start | bytes 4866048 | tf_op jit(solution)/shard_map/reduce_scatter | solution.py:187
  666.3 1.7 copy-start.4
  678.4 5.5 collective-permute-start.2
  688.1 173.4 %copy-start.1 = (bf16[2,256,3072]{2,1,0:T(8,128)(2,1)S(1)}, bf16[2,256,3072]{2,1,0:T(8,128)(2,1)}, u32[]{:S(2)}) copy-start(bf16[2,256,3072]{2,1,0:T(8,128)(2,1)} %param.14) | copy-start | bytes 9437188
  (1 other events, 1.3 us)
Sparse Core Ops, SparseCore 0:
  9.6 181.3 all-gather.4
  192.7 156.1 all-gather.6
  355.4 47.3 reduce-scatter.2
  407.6 48.2 all-gather.8
  458.0 156.8 all-gather.10
  635.9 28.8 all-reduce.3
  688.3 171.5 reduce-scatter.4
where the time goes:
time: 869 us; the launch traced here: 868 us
  waiting for transfers between devices  688 us (79%)
  local copies, waits for them, and re-layouts  58.5 us (7%)
  matrix products  48.1 us (6%)
  other arithmetic  42.8 us (5%)
  between operations  14.5 us (2%)
  blocking collectives  13 us (1%)
    reduce_scatter x1, waiting for transfers between devices, local(): lax.psum_scatter(rounded(product).astype(jnp.bfloat16), 'ctl', scatter_di...  167 us
    all_gather x1, waiting for transfers between devices, local(): lax.all_gather(own_cols, 'ctl', axis=0, tiled=True)  150 us
    all_gather x1, waiting for transfers between devices, local(): shard_piece = lax.all_gather(qkv_weight, 'ctl', axis=1, tiled=True)  145 us
    all_gather x1, waiting for transfers between devices, local(): lax.all_gather(out_weight, 'ctl', axis=2, tiled=True)[0]  91.9 us
    all_gather x1, waiting for transfers between devices, local(): lax.all_gather(act_half.astype(jnp.bfloat16), 'tp', axis=1, tiled=True)  47.6 us
    reduce_scatter x1, waiting for transfers between devices, local(): lax.psum_scatter(partial_value.astype(jnp.bfloat16), 'tp', scatter_dimens...  47.4 us
    psum x1, waiting for transfers between devices, local(): lax.psum(jnp.dot(final_in.reshape(flat_rows, half_width), proj_weight, pr...  28 us
  transfers between devices with their start and end apart: 10, of which 10 were waited for; matrix products, arithmetic and copies ran while one was open for 13% of the time, Pallas kernels for 0%

commit v1 on v0

--- a/solution.py
+++ b/solution.py
@@ -21,6 +21,10 @@
     mask = 2**bit
     pairs = [(source, source ^ mask) for source in range(lax.axis_size(axis))]
     return lax.ppermute(value, axis, pairs)
+
+
+def swap(value, axis):
+    return lax.ppermute(value, axis, [(0, 1), (1, 0)])
 
 
 def layer_norm(values):
@@ -81,12 +85,24 @@
     )
     text_flat = normed.reshape(micro_count * seq_rows, width_full)
     image_flat = normed[:, text_rows:].reshape(flat_rows, width_full)
-    shard_piece = lax.all_gather(qkv_weight, "ctl", axis=1, tiled=True)
-    count_rows = shard_piece.shape[1]
-    query_acc = jnp.dot(image_flat, shard_piece[0, :, 0], preferred_element_type=jnp.float32)
-    pair_weight = shard_piece[0, :, 1:].reshape(count_rows, 2 * local_heads)
+    local_rows = qkv_weight.shape[1]
+    own_cols = lax.dynamic_slice_in_dim(zero_weight, side_index * quarter_width, quarter_width, 1)
+    packed = jnp.concatenate(
+        [
+            qkv_weight[0].reshape(local_rows, 3 * local_heads),
+            out_weight[0].T,
+            own_cols,
+        ],
+        axis=1,
+    )
+    gathered = lax.all_gather(packed, "ctl", axis=0, tiled=True)
+    count_rows = gathered.shape[0]
+    query_weight = gathered[:, :local_heads]
+    pair_weight = gathered[:, local_heads : 3 * local_heads]
+    out_cols = gathered[:, 3 * local_heads : 4 * local_heads]
+    zero_cols = gathered[:, 4 * local_heads :]
+    query_acc = jnp.dot(image_flat, query_weight, preferred_element_type=jnp.float32)
     pair_acc = jnp.dot(text_flat, pair_weight, preferred_element_type=jnp.float32)
-    query_acc, pair_acc = (query_acc, pair_acc)
     gain_pair = qk_gain[0]
     queries = head_norm(
         query_acc.reshape(micro_count, img_rows, head_count, HEAD_DIM), gain_pair[0]
@@ -102,30 +118,31 @@
         "bhij,bjhd->bihd", attend, values_all, preferred_element_type=jnp.float32
     )
     mixed_heads = mixed_heads.astype(jnp.bfloat16).reshape(flat_rows, local_heads)
-    partial_value = rounded(
-        jnp.dot(
-            mixed_heads,
-            lax.all_gather(out_weight, "ctl", axis=2, tiled=True)[0],
-            preferred_element_type=jnp.float32,
-        )
-    )
-    head_sum = lax.psum_scatter(
-        partial_value.astype(jnp.bfloat16), "tp", scatter_dimension=1, tiled=True
-    ).astype(jnp.float32)
+    contract_last = (((1,), (1,)), ((), ()))
+    other_out = lax.dynamic_slice_in_dim(out_cols, (1 - tp_index) * half_width, half_width, 0)
+    own_out = lax.dynamic_slice_in_dim(out_cols, tp_index * half_width, half_width, 0)
+    other_part = lax.dot_general(
+        mixed_heads, other_out, contract_last, preferred_element_type=jnp.float32
+    ).astype(jnp.bfloat16)
+    got_part = swap(other_part, "tp")
+    own_part_heads = rounded(
+        lax.dot_general(mixed_heads, own_out, contract_last, preferred_element_type=jnp.float32)
+    )
+    head_sum = own_part_heads + got_part.astype(jnp.float32)
     hid_half = lax.dynamic_slice_in_dim(hidden, tp_index * half_width, half_width, 2)
     gate_half = lax.dynamic_slice_in_dim(modulate[:, 2:3], tp_index * half_width, half_width, 2)
     act_half = hid_half + gate_half * head_sum.reshape(micro_count, img_rows, half_width)
     act_half = act_half.reshape(flat_rows, half_width)
-    act_narrow = lax.all_gather(act_half.astype(jnp.bfloat16), "tp", axis=1, tiled=True)
+    act_own = act_half.astype(jnp.bfloat16)
+    act_got = swap(act_own, "tp")
+    act_narrow = jnp.where(
+        tp_index == 0,
+        jnp.concatenate([act_own, act_got], axis=1),
+        jnp.concatenate([act_got, act_own], axis=1),
+    )
     act_other = passed_along(act_narrow, "side", 1)
     control_rows = jnp.where(is_control, act_narrow, act_other)
-    own_cols = lax.dynamic_slice_in_dim(zero_weight, side_index * quarter_width, quarter_width, 1)
-    columns = control_rows
-    own_part = jnp.dot(
-        columns,
-        lax.all_gather(own_cols, "ctl", axis=0, tiled=True),
-        preferred_element_type=jnp.float32,
-    )
+    own_part = jnp.dot(control_rows, zero_cols, preferred_element_type=jnp.float32)
     own_narrow = own_part.astype(jnp.bfloat16)
     other_narrow = partner(own_narrow, "side", 0)
     residual_narrow = jnp.where(
@@ -149,12 +166,10 @@
     scale_inv = lax.rsqrt(spread + EPS)
     unit_rows = (merged_rows - mean_val) * scale_inv
     final_in = (unit_rows * (1.0 + final_half[:, 1:2]) + final_half[:, 0:1]).astype(jnp.bfloat16)
-    prediction = lax.psum(
-        jnp.dot(
-            final_in.reshape(flat_rows, half_width), proj_weight, preferred_element_type=jnp.float32
-        ).astype(jnp.bfloat16),
-        "tp",
-    ).astype(jnp.float32)
+    pred_part = jnp.dot(
+        final_in.reshape(flat_rows, half_width), proj_weight, preferred_element_type=jnp.float32
+    )
+    prediction = pred_part + swap(pred_part, "tp")
     loss_factor = 4.0 / math.sqrt(micro_count * ctl_count * img_rows)
     grad_pred = (loss_factor * (prediction - velocity_target.reshape(flat_rows, -1))).astype(
         jnp.bfloat16
@@ -180,13 +195,12 @@
         control_rows.reshape(flat_rows, ctl_count, 2, block_rows), side_index, 2, keepdims=False
     )
     own_act = own_act.reshape(flat_rows, ctl_count * block_rows)
-    columns = own_act
     product = lax.dot_general(
-        columns, grad_rows_all, (((0,), (0,)), ((), ())), preferred_element_type=jnp.float32
-    )
-    zero_grad = lax.psum_scatter(
-        rounded(product).astype(jnp.bfloat16), "ctl", scatter_dimension=0, tiled=True
-    ).astype(jnp.float32)
+        own_act, grad_rows_all, (((0,), (0,)), ((), ())), preferred_element_type=jnp.float32
+    )
+    group_parts = rounded(product).astype(jnp.bfloat16).reshape(ctl_count, block_rows, half_width)
+    received = lax.all_to_all(group_parts, "ctl", 0, 0, tiled=True)
+    zero_grad = jnp.sum(received.astype(jnp.float32), axis=0)
     return (section_out.reshape(1, micro_count, img_rows, half_width), zero_grad)
 
 

time: 869 us -> 595 us (0.68)
  the two profiles are of different devices: /device:TPU:0 before, /device:TPU:5 now
where the time goes in v1:
time: 595 us; the launch traced here: 583 us
  waiting for transfers between devices  370 us (62%)
  local copies, waits for them, and re-layouts  68.5 us (12%)
  matrix products  49.4 us (8%)
  other arithmetic  44.2 us (7%)
  starting transfers between devices  25.7 us (4%)
  between operations  14.7 us (2%)
  blocking collectives  10.7 us (2%)
    all_gather x1, waiting for transfers between devices, local(): gathered = lax.all_gather(packed, 'ctl', axis=0, tiled=True)  228 us
    ppermute x3, waiting for transfers between devices, swap(): return lax.ppermute(value, axis, [(0, 1), (1, 0)])  66.2 us
    all_to_all x1, waiting for transfers between devices, local(): received = lax.all_to_all(group_parts, 'ctl', 0, 0, tiled=True)  64.7 us
    dot_general x2, local copies, waits for them, and re-layouts, local(): jnp.dot(text_flat, pair_weight, preferred_element_type=jnp.float32)  20.7 us
    gather x1, local copies, waits for them, and re-layouts, local(): jnp.take(latent, order_row, axis=0)  14.8 us
  transfers between devices with their start and end apart: 8, of which 8 were waited for; matrix products, arithmetic and copies ran while one was open for 7% of the time, Pallas kernels for 0%

profile of v1, /device:TPU:5, one launch (start us, length us, event | category | flops | bytes accessed | tf_op | source)
XLA Modules:
  0.0 583.2 jit_solution(12119574096527699242)
XLA Ops:
  12.6 14.8 %gather_fusion.1 = bf16[512,3072]{1,0:T(8,128)(2,1)} fusion(bf16[2,256,3072]{2,1,0:T(8,128)(2,1)S(1)} %copy-done, s32[512]{0:T(512)S(1)} %bitcast.109), kind=kCustom, calls=%fused_computation.1 | custom fusion | bytes 6295552 | tf_op jit(solution)/shard_map/vmap(jit(_take))/gather | solution.py:75
  32.9 4.4 multiply_add_fusion
  43.6 227.9 %all-gather.2.cloned.1.call-done = bf16[3072,3840]{1,0:T(8,128)(2,1)} async-done(((bf16[96,3840]{1,0:T(8,128)(2,1)}), bf16[3072,3840]{1,0:T(8,128)(2,1)}) %all-gather.2.cloned.1.call-update) | async-done | bytes 23592976 | tf_op jit(solution)/shard_map/all_gather | solution.py:98
  271.5 8.0 %slice_bitcast_fusion = bf16[1536,3072]{0,1:T(8,128)(2,1)} fusion(bf16[3072,3840]{1,0:T(8,128)(2,1)} %all-gather.2.cloned.1.call-done), kind=kLoop, calls=%fused_computation.3 | loop fusion | bytes 18874368 | tf_op jit(solution)/shard_map/dot_general | solution.py:105
  279.5 12.6 %copy.21 = bf16[1536,3072]{1,0:T(8,128)(2,1)} copy(bf16[1536,3072]{0,1:T(8,128)(2,1)} %slice_bitcast_fusion) | data formatting | bytes 18874368 | tf_op jit(solution)/shard_map/dot_general | solution.py:105
  292.1 11.5 %fusion.4 = f32[2,384,2,6,128]{1,4,3,2,0:T(8,128)S(1)} fusion(bf16[2,6,128,3072,1]{3,2,1,0,4:T(8,128)(2,1)} %bitcast.113, bf16[2,384,3072]{2,1,0:T(8,128)(2,1)} %add_convert_fusion), kind=kOutput, calls=%fused_computation.14 | convolution fusion | flops 7247757312 | bytes 18874368 | tf_op jit(solution)/shard_map/dot_general | solution.py:105
  306.0 8.2 %fusion.46 = (bf16[3072,768]{1,0:T(8,128)(2,1)}, bf16[768,3072]{0,1:T(8,128)(2,1)}) fusion(bf16[3072,3840]{1,0:T(8,128)(2,1)} %all-gather.2.cloned.1.call-done), kind=kLoop, calls=%fused_computation.99 | loop fusion | bytes 18874368 | tf_op jit(solution)/shard_map/slice | solution.py:102
  314.2 6.7 %copy.22 = bf16[768,3072]{1,0:T(8,128)(2,1)} copy(bf16[768,3072]{0,1:T(8,128)(2,1)} %get-tuple-element.10) | data formatting | bytes 9437184 | tf_op jit(solution)/shard_map/dot_general | solution.py:104
  320.8 6.0 %multiply_reduce_fusion.5 = (f32[2,256,6]{1,2,0:T(8,128)S(1)}, f32[2,256,6,128]{1,3,2,0:T(8,128)S(1)}) fusion(bf16[6,128,3072,1]{2,1,0,3:T(8,128)(2,1)} %bitcast.118, bf16[2,384,3072]{2,1,0:T(8,128)(2,1)} %add_convert_fusion), kind=kOutput, calls=%fused_computation.48 | convolution fusion | flops 2416702464 | bytes 9449472 | tf_op jit(solution)/shard_map/dot_general | solution.py:104
  333.3 10.0 %fusion.21 = bf16[2,256,6,128]{1,3,2,0:T(8,128)(2,1)S(1)} fusion(f32[2,6,256]{2,1,0:T(8,128)S(1)} %fusion.48, f32[2,384,2,6,128]{1,4,3,2,0:T(8,128)} %copy-done.9, f32[2,6,256,384]{3,2,1,0:T(8,128)} %copy-done.4), kind=kOutput, calls=%fused_computation.53 | convolution fusion | flops 308284800 | bytes 11415552 | tf_op jit(solution)/shard_map/bhij,bjhd->bihd/dot_general | solution.py:117
  353.7 30.7 %collective-permute-done = bf16[512,1536]{1,0:T(8,128)(2,1)} collective-permute-done((bf16[512,1536]{1,0:T(8,128)(2,1)S(1)}, bf16[512,1536]{1,0:T(8,128)(2,1)}, u32[]{:S(2)}, u32[]{:S(2)}) %collective-permute-start) | collective-permute-done | bytes 1572896 | tf_op jit(solution)/shard_map/ppermute | solution.py:27
  386.3 4.9 fusion.27
  395.9 33.0 %collective-permute-done.1 = bf16[512,1536]{0,1:T(8,128)(2,1)} collective-permute-done((bf16[512,1536]{0,1:T(8,128)(2,1)S(1)}, bf16[512,1536]{0,1:T(8,128)(2,1)}, u32[]{:S(2)}, u32[]{:S(2)}) %collective-permute-start.1) | collective-permute-done | bytes 1572896 | tf_op jit(solution)/shard_map/ppermute | solution.py:27
  433.4 7.7 %collective-permute-done.2 = bf16[512,3072]{0,1:T(8,128)(2,1)S(1)} collective-permute-done((bf16[512,3072]{0,1:T(8,128)(2,1)S(1)}, bf16[512,3072]{0,1:T(8,128)(2,1)S(1)}, u32[]{:S(2)}, u32[]{:S(2)}) %collective-permute-start.2) | collective-permute-done | bytes 3145760 | tf_op jit(solution)/shard_map/ppermute | solution.py:17
  441.5 6.1 %fusion.18 = bf16[512,768]{1,0:T(8,128)(2,1)S(1)} fusion(bf16[512,3072]{0,1:T(8,128)(2,1)S(1)} %broadcast_select_fusion, bf16[3072,3840]{1,0:T(8,128)(2,1)} %all-gather.2.cloned.1.call-done), kind=kOutput, calls=%fused_computation.52 | convolution fusion | flops 2416312320 | bytes 8650752 | tf_op jit(solution)/shard_map/dot_general | solution.py:145
  450.9 4.4 fusion.45
  455.4 5.4 all-reduce.1
  469.9 5.3 all-reduce
  475.1 4.0 multiply_convert_fusion
  479.1 5.8 collective-permute-start.5
  487.8 5.7 convolution_convert_fusion
  493.5 9.4 %all-to-all-start = ((bf16[32,48,1536]{2,1,0:T(8,128)(2,1)}), bf16[32,48,1536]{2,1,0:T(8,128)(2,1)}, u32[]{:S(2)}, u32[]{:S(2)}) async-start(bf16[32,48,1536]{2,1,0:T(8,128)(2,1)} %bitcast.117), calls=%async_computation | async-start | bytes 9437184 | tf_op jit(solution)/shard_map/all_to_all | solution.py:202
  503.0 4.7 select_bitcast_fusion
  507.6 64.7 %all-to-all-done = bf16[32,48,1536]{2,1,0:T(8,128)(2,1)} async-done(((bf16[32,48,1536]{2,1,0:T(8,128)(2,1)}), bf16[32,48,1536]{2,1,0:T(8,128)(2,1)}, u32[]{:S(2)}, u32[]{:S(2)}) %all-to-all-start) | async-done | bytes 4718624 | tf_op jit(solution)/shard_map/all_to_all | solution.py:202
  (94 shorter events, 66.6 us)
Async XLA Ops:
  7.2 5.5 copy-start
  7.2 5.4 copy-start.16
  7.2 264.3 %all-gather.2.cloned.1.call-start = ((), (), s32[]{:S(2)}) async-start(), calls=%async_computation.1 | async-start | bytes 24330240 | tf_op jit(solution)/shard_map/all_gather | solution.py:98
  12.6 14.8 %copy-start.18 = (s32[2]{0:T(128)S(1)}, s32[2]{0:T(128)}, u32[]{:S(2)}) copy-start(s32[2]{0:T(128)} %param.17) | copy-start | bytes 28
  27.4 3.8 copy-start.17
  37.3 2.7 copy-start.2
  303.7 2.2 copy-start.9
  329.4 2.2 copy-start.4
  347.5 37.0 %collective-permute-start = (bf16[512,1536]{1,0:T(8,128)(2,1)S(1)}, bf16[512,1536]{1,0:T(8,128)(2,1)}, u32[]{:S(2)}, u32[]{:S(2)}) collective-permute-start(bf16[512,1536]{1,0:T(8,128)(2,1)S(1)} %convolution_convert_fusion.1), channel_id=1, source_target_pairs={{0,1},{1,0},{2,3},{3,2},{4,5},{5,4},{6,7},{7,6},{8,9},{9,8},{10,11... | collective-permute-start | bytes 4718600 | tf_op jit(solution)/shard_map/ppermute | solution.py:27
  386.3 4.9 copy-start.6
  393.0 3.0 copy-start.8
  393.0 35.9 %collective-permute-start.1 = (bf16[512,1536]{0,1:T(8,128)(2,1)S(1)}, bf16[512,1536]{0,1:T(8,128)(2,1)}, u32[]{:S(2)}, u32[]{:S(2)}) collective-permute-start(bf16[512,1536]{0,1:T(8,128)(2,1)S(1)} %copy.27), channel_id=1, source_target_pairs={{0,1},{1,0},{2,3},{3,2},{4,5},{5,4},{6,7},{7,6},{8,9},{9,8},{10,11... | collective-permute-start | bytes 4718600 | tf_op jit(solution)/shard_map/ppermute | solution.py:27
  432.1 9.0 %collective-permute-start.2 = (bf16[512,3072]{0,1:T(8,128)(2,1)S(1)}, bf16[512,3072]{0,1:T(8,128)(2,1)S(1)}, u32[]{:S(2)}, u32[]{:S(2)}) collective-permute-start(bf16[512,3072]{0,1:T(8,128)(2,1)S(1)} %maximum_select_fusion), channel_id=1, source_target_pairs={{0,2},{1,3},{4,6},{5,7},{8,10},{9,11},{12,14},{13,15},{16,18},{17,... | collective-permute-start | bytes 9437192 | tf_op jit(solution)/shard_map/ppermute | solution.py:17
  441.5 6.2 %copy-start.7 = (bf16[512,3072]{0,1:T(8,128)(2,1)}, bf16[512,3072]{0,1:T(8,128)(2,1)S(1)}, u32[]{:S(2)}) copy-start(bf16[512,3072]{0,1:T(8,128)(2,1)S(1)} %broadcast_select_fusion) | copy-start | bytes 9437188
  441.5 6.4 %copy-start.15 = (f32[2,2,3072]{2,1,0:T(2,128)S(1)}, f32[2,2,3072]{2,1,0:T(2,128)}, u32[]{:S(2)}) copy-start(f32[2,2,3072]{2,1,0:T(2,128)} %param.24) | copy-start | bytes 147460
  447.7 2.4 copy-start.10
  447.7 2.4 collective-permute-start.3
  455.4 19.8 %copy-start.3 = (f32[2,256,1536]{2,1,0:T(8,128)}, f32[2,256,1536]{2,1,0:T(8,128)S(1)}, u32[]{:S(2)}) copy-start(f32[2,256,1536]{2,1,0:T(8,128)S(1)} %get-tuple-element.8) | copy-start | bytes 9437188
  455.4 6.1 %copy-start.12 = (bf16[1536,64]{0,1:T(8,128)(2,1)S(1)}, bf16[1536,64]{0,1:T(8,128)(2,1)}, u32[]{:S(2)}) copy-start(bf16[1536,64]{0,1:T(8,128)(2,1)} %param.23) | copy-start | bytes 589828
  460.8 4.2 copy-start.13
  462.1 5.4 collective-permute-start.4
  479.1 8.7 %collective-permute-start.5 = (bf16[512,1536]{1,0:T(8,128)(2,1)}, bf16[512,1536]{1,0:T(8,128)(2,1)S(1)}, u32[]{:S(2)}, u32[]{:S(2)}) collective-permute-start(bf16[512,1536]{1,0:T(8,128)(2,1)} %bitcast.40), channel_id=1, source_target_pairs={{2,0},{3,1},{6,4},{7,5},{10,8},{11,9},{14,12},{15,13},{18,16},{19,... | collective-permute-start | bytes 4718600 | tf_op jit(solution)/shard_map/ppermute | solution.py:17
  493.5 78.8 %all-to-all-start = ((bf16[32,48,1536]{2,1,0:T(8,128)(2,1)}), bf16[32,48,1536]{2,1,0:T(8,128)(2,1)}, u32[]{:S(2)}, u32[]{:S(2)}) async-start(bf16[32,48,1536]{2,1,0:T(8,128)(2,1)} %bitcast.117), calls=%async_computation | async-start | bytes 9437184 | tf_op jit(solution)/shard_map/all_to_all | solution.py:202
  502.9 73.1 %copy-start.1 = (bf16[2,256,3072]{2,1,0:T(8,128)(2,1)S(1)}, bf16[2,256,3072]{2,1,0:T(8,128)(2,1)}, u32[]{:S(2)}) copy-start(bf16[2,256,3072]{2,1,0:T(8,128)(2,1)} %param.14) | copy-start | bytes 9437188
  (3 other events, 3.9 us)
Sparse Core Ops, SparseCore 0:
  12.7 258.7 all-gather.1

commit v2 on v1

--- a/solution.py
+++ b/solution.py
@@ -87,20 +87,17 @@
     image_flat = normed[:, text_rows:].reshape(flat_rows, width_full)
     local_rows = qkv_weight.shape[1]
     own_cols = lax.dynamic_slice_in_dim(zero_weight, side_index * quarter_width, quarter_width, 1)
-    packed = jnp.concatenate(
-        [
-            qkv_weight[0].reshape(local_rows, 3 * local_heads),
-            out_weight[0].T,
-            own_cols,
-        ],
-        axis=1,
-    )
-    gathered = lax.all_gather(packed, "ctl", axis=0, tiled=True)
-    count_rows = gathered.shape[0]
-    query_weight = gathered[:, :local_heads]
-    pair_weight = gathered[:, local_heads : 3 * local_heads]
-    out_cols = gathered[:, 3 * local_heads : 4 * local_heads]
-    zero_cols = gathered[:, 4 * local_heads :]
+    qkv_cols = lax.all_gather(
+        qkv_weight[0].reshape(local_rows, 3 * local_heads), "ctl", axis=0, tiled=True
+    )
+    count_rows = qkv_cols.shape[0]
+    packed = jnp.concatenate([out_weight[0].T, own_cols], axis=1)
+    spread_out = jnp.broadcast_to(packed[None], (ctl_count,) + packed.shape)
+    gathered = lax.all_to_all(spread_out, "ctl", 0, 0, tiled=True).reshape(count_rows, -1)
+    query_weight = qkv_cols[:, :local_heads]
+    pair_weight = qkv_cols[:, local_heads:]
+    out_cols = gathered[:, :local_heads]
+    zero_cols = gathered[:, local_heads:]
     query_acc = jnp.dot(image_flat, query_weight, preferred_element_type=jnp.float32)
     pair_acc = jnp.dot(text_flat, pair_weight, preferred_element_type=jnp.float32)
     gain_pair = qk_gain[0]

time: 595 us -> 623 us (1.047)
  waiting for transfers between devices: 370 us -> 390 us
    all_to_all x0 -> x1, waiting for transfers between devices: none -> 147 us  [local(): lax.all_to_all(spread_out, 'ctl', 0, 0, tiled=True).reshape(count_rows, -1)]
    all_gather x1, waiting for transfers between devices: 228 us -> 98 us  [local(): lax.all_gather(qkv_weight[0].reshape(local_rows, 3 * local_heads), 'ctl',...]
    ppermute x3, waiting for transfers between devices: 66.2 us -> 55.2 us  [swap(): return lax.ppermute(value, axis, [(0, 1), (1, 0)])]
    ppermute x2, waiting for transfers between devices: 9.07 us -> 17.8 us  [passed_along(): return lax.ppermute(shard, axis, pairs)]
    all_to_all x0 -> x1, starting transfers between devices: none -> 8.56 us  [local(): lax.all_to_all(spread_out, 'ctl', 0, 0, tiled=True).reshape(count_rows, -1)]
    ppermute x3, starting transfers between devices: 8.98 us -> 2.18 us  [swap(): return lax.ppermute(value, axis, [(0, 1), (1, 0)])]
  transfers between devices with their start and end apart: 8 -> 9, of which waited for: 8 -> 9; matrix products, arithmetic and copies ran while one was open for 7% -> 8% of each run, Pallas kernels for 0% -> 0%
where the time goes in v2:
time: 623 us; the launch traced here: 612 us
  waiting for transfers between devices  390 us (63%)
  local copies, waits for them, and re-layouts  74.7 us (12%)
  matrix products  49.1 us (8%)
  other arithmetic  43.3 us (7%)
  starting transfers between devices  28.8 us (5%)
  between operations  14.9 us (2%)
  blocking collectives  10.7 us (2%)
    all_to_all x1, waiting for transfers between devices, local(): lax.all_to_all(spread_out, 'ctl', 0, 0, tiled=True).reshape(count_rows, -1)  147 us
    all_gather x1, waiting for transfers between devices, local(): lax.all_gather(qkv_weight[0].reshape(local_rows, 3 * local_heads), 'ctl',...  98 us
    all_to_all x1, waiting for transfers between devices, local(): received = lax.all_to_all(group_parts, 'ctl', 0, 0, tiled=True)  69.6 us
    ppermute x3, waiting for transfers between devices, swap(): return lax.ppermute(value, axis, [(0, 1), (1, 0)])  55.2 us
    dot_general x2, local copies, waits for them, and re-layouts, local(): jnp.dot(text_flat, pair_weight, preferred_element_type=jnp.float32)  20.5 us
    ppermute x2, waiting for transfers between devices, passed_along(): return lax.ppermute(shard, axis, pairs)  17.8 us
    gather x1, local copies, waits for them, and re-layouts, local(): jnp.take(latent, order_row, axis=0)  14.8 us
  transfers between devices with their start and end apart: 9, of which 9 were waited for; matrix products, arithmetic and copies ran while one was open for 8% of the time, Pallas kernels for 0%

profile of v2, /device:TPU:5, one launch (start us, length us, event | category | flops | bytes accessed | tf_op | source)
XLA Modules:
  0.0 611.6 jit_solution(16946621144856477652)
XLA Ops:
  16.1 8.6 %all-to-all-start = ((bf16[32,96,1536]{2,1,0:T(8,128)(2,1)}), bf16[32,96,1536]{2,1,0:T(8,128)(2,1)}, u32[]{:S(2)}, u32[]{:S(2)}) async-start(bf16[32,96,1536]{2,1,0:T(8,128)(2,1)} %broadcast_in_dim.54), calls=%async_computation | async-start | bytes 18874368 | tf_op jit(solution)/shard_map/all_to_all | solution.py:96
  24.8 14.8 %gather_fusion.1 = bf16[512,3072]{1,0:T(8,128)(2,1)} fusion(bf16[2,256,3072]{2,1,0:T(8,128)(2,1)S(1)} %copy-done, s32[512]{0:T(512)S(1)} %bitcast.110), kind=kCustom, calls=%fused_computation.1 | custom fusion | bytes 6295552 | tf_op jit(solution)/shard_map/vmap(jit(_take))/gather | solution.py:75
  55.7 147.4 %all-to-all-done = bf16[32,96,1536]{2,1,0:T(8,128)(2,1)} async-done(((bf16[32,96,1536]{2,1,0:T(8,128)(2,1)}), bf16[32,96,1536]{2,1,0:T(8,128)(2,1)}, u32[]{:S(2)}, u32[]{:S(2)}) %all-to-all-start) | async-done | bytes 9437216 | tf_op jit(solution)/shard_map/all_to_all | solution.py:96
  203.1 4.7 slice.72
  207.8 98.0 %all-gather.2.cloned.1.call-done = bf16[3072,2304]{1,0:T(8,128)(2,1)} async-done(((bf16[96,2304]{1,0:T(8,128)(2,1)}), bf16[3072,2304]{1,0:T(8,128)(2,1)}) %all-gather.2.cloned.1.call-update) | async-done | bytes 14155792 | tf_op jit(solution)/shard_map/all_gather | solution.py:90
  305.8 7.9 %slice_bitcast_fusion = bf16[1536,3072]{0,1:T(8,128)(2,1)} fusion(bf16[3072,2304]{1,0:T(8,128)(2,1)} %all-gather.2.cloned.1.call-done), kind=kLoop, calls=%fused_computation.3 | loop fusion | bytes 18874368 | tf_op jit(solution)/shard_map/dot_general | solution.py:102
  313.7 12.6 %copy.19 = bf16[1536,3072]{1,0:T(8,128)(2,1)} copy(bf16[1536,3072]{0,1:T(8,128)(2,1)} %slice_bitcast_fusion) | data formatting | bytes 18874368 | tf_op jit(solution)/shard_map/dot_general | solution.py:102
  326.3 11.5 %fusion.4 = f32[2,384,2,6,128]{1,4,3,2,0:T(8,128)S(1)} fusion(bf16[2,6,128,3072,1]{3,2,1,0,4:T(8,128)(2,1)} %bitcast.114, bf16[2,384,3072]{2,1,0:T(8,128)(2,1)} %add_convert_fusion), kind=kOutput, calls=%fused_computation.14 | convolution fusion | flops 7247757312 | bytes 18874368 | tf_op jit(solution)/shard_map/dot_general | solution.py:102
  340.3 4.8 slice_bitcast_fusion.1
  345.1 6.7 %copy.20 = bf16[768,3072]{1,0:T(8,128)(2,1)} copy(bf16[768,3072]{0,1:T(8,128)(2,1)} %slice_bitcast_fusion.1) | data formatting | bytes 9437184 | tf_op jit(solution)/shard_map/dot_general | solution.py:101
  351.8 5.7 multiply_reduce_fusion.5
  363.9 10.0 %fusion.21 = bf16[2,256,6,128]{1,3,2,0:T(8,128)(2,1)S(1)} fusion(f32[2,6,256]{2,1,0:T(8,128)S(1)} %fusion.47, f32[2,384,2,6,128]{1,4,3,2,0:T(8,128)} %copy-done.9, f32[2,6,256,384]{3,2,1,0:T(8,128)} %copy-done.4), kind=kOutput, calls=%fused_computation.53 | convolution fusion | flops 308284800 | bytes 11415552 | tf_op jit(solution)/shard_map/bhij,bjhd->bihd/dot_general | solution.py:114
  381.7 24.6 %collective-permute-done = bf16[512,1536]{1,0:T(8,128)(2,1)} collective-permute-done((bf16[512,1536]{1,0:T(8,128)(2,1)S(1)}, bf16[512,1536]{1,0:T(8,128)(2,1)}, u32[]{:S(2)}, u32[]{:S(2)}) %collective-permute-start) | collective-permute-done | bytes 1572896 | tf_op jit(solution)/shard_map/ppermute | solution.py:27
  408.2 4.9 fusion.27
  415.9 26.0 %collective-permute-done.1 = bf16[512,1536]{0,1:T(8,128)(2,1)} collective-permute-done((bf16[512,1536]{0,1:T(8,128)(2,1)S(1)}, bf16[512,1536]{0,1:T(8,128)(2,1)}, u32[]{:S(2)}, u32[]{:S(2)}) %collective-permute-start.1) | collective-permute-done | bytes 1572896 | tf_op jit(solution)/shard_map/ppermute | solution.py:27
  446.7 16.5 %collective-permute-done.2 = bf16[512,3072]{0,1:T(8,128)(2,1)S(1)} collective-permute-done((bf16[512,3072]{0,1:T(8,128)(2,1)S(1)}, bf16[512,3072]{0,1:T(8,128)(2,1)S(1)}, u32[]{:S(2)}, u32[]{:S(2)}) %collective-permute-start.2) | collective-permute-done | bytes 3145760 | tf_op jit(solution)/shard_map/ppermute | solution.py:17
  463.6 6.1 %fusion.18 = bf16[512,768]{1,0:T(8,128)(2,1)S(1)} fusion(bf16[512,3072]{0,1:T(8,128)(2,1)S(1)} %broadcast_select_fusion, bf16[3072,1536]{1,0:T(8,128)(2,1)} %bitcast.23), kind=kOutput, calls=%fused_computation.52 | convolution fusion | flops 2416312320 | bytes 8650752 | tf_op jit(solution)/shard_map/dot_general | solution.py:142
  477.4 5.4 all-reduce.1
  491.9 5.3 all-reduce
  501.2 5.8 collective-permute-start.5
  509.9 5.7 convolution_convert_fusion
  515.5 10.7 %all-to-all-start.1 = ((bf16[32,48,1536]{2,1,0:T(8,128)(2,1)}), bf16[32,48,1536]{2,1,0:T(8,128)(2,1)}, u32[]{:S(2)}, u32[]{:S(2)}) async-start(bf16[32,48,1536]{2,1,0:T(8,128)(2,1)} %bitcast.118), calls=%async_computation.1 | async-start | bytes 9437184 | tf_op jit(solution)/shard_map/all_to_all | solution.py:199
  526.3 4.7 select_bitcast_fusion
  531.0 69.6 %all-to-all-done.1 = bf16[32,48,1536]{2,1,0:T(8,128)(2,1)} async-done(((bf16[32,48,1536]{2,1,0:T(8,128)(2,1)}), bf16[32,48,1536]{2,1,0:T(8,128)(2,1)}, u32[]{:S(2)}, u32[]{:S(2)}) %all-to-all-start.1) | async-done | bytes 4718624 | tf_op jit(solution)/shard_map/all_to_all | solution.py:199
  (98 shorter events, 78.7 us)
Async XLA Ops:
  7.2 17.6 %copy-start = (bf16[2,256,3072]{2,1,0:T(8,128)(2,1)S(1)}, bf16[2,256,3072]{2,1,0:T(8,128)(2,1)}, u32[]{:S(2)}) copy-start(bf16[2,256,3072]{2,1,0:T(8,128)(2,1)} %param.14) | copy-start | bytes 9437188
  7.2 298.7 %all-gather.2.cloned.1.call-start = ((), (), s32[]{:S(2)}) async-start(), calls=%async_computation.2 | async-start | bytes 14598144 | tf_op jit(solution)/shard_map/all_gather | solution.py:90
  16.1 8.6 %copy-start.16 = (s32[2,256]{1,0:T(2,128)S(1)}, s32[2,256]{1,0:T(2,128)}, u32[]{:S(2)}) copy-start(s32[2,256]{1,0:T(2,128)} %param.15) | copy-start | bytes 6148
  16.1 186.9 %all-to-all-start = ((bf16[32,96,1536]{2,1,0:T(8,128)(2,1)}), bf16[32,96,1536]{2,1,0:T(8,128)(2,1)}, u32[]{:S(2)}, u32[]{:S(2)}) async-start(bf16[32,96,1536]{2,1,0:T(8,128)(2,1)} %broadcast_in_dim.54), calls=%async_computation | async-start | bytes 18874368 | tf_op jit(solution)/shard_map/all_to_all | solution.py:96
  24.8 14.8 %copy-start.18 = (s32[2]{0:T(128)S(1)}, s32[2]{0:T(128)}, u32[]{:S(2)}) copy-start(s32[2]{0:T(128)} %param.17) | copy-start | bytes 28
  39.5 3.7 copy-start.17
  49.4 2.7 copy-start.2
  337.9 2.3 copy-start.9
  360.1 2.1 copy-start.4
  378.1 28.2 %collective-permute-start = (bf16[512,1536]{1,0:T(8,128)(2,1)S(1)}, bf16[512,1536]{1,0:T(8,128)(2,1)}, u32[]{:S(2)}, u32[]{:S(2)}) collective-permute-start(bf16[512,1536]{1,0:T(8,128)(2,1)S(1)} %convolution_convert_fusion.1), channel_id=1, source_target_pairs={{0,1},{1,0},{2,3},{3,2},{4,5},{5,4},{6,7},{7,6},{8,9},{9,8},{10,11... | collective-permute-start | bytes 4718600 | tf_op jit(solution)/shard_map/ppermute | solution.py:27
  408.2 4.9 copy-start.6
  414.8 27.2 %collective-permute-start.1 = (bf16[512,1536]{0,1:T(8,128)(2,1)S(1)}, bf16[512,1536]{0,1:T(8,128)(2,1)}, u32[]{:S(2)}, u32[]{:S(2)}) collective-permute-start(bf16[512,1536]{0,1:T(8,128)(2,1)S(1)} %copy.25), channel_id=1, source_target_pairs={{0,1},{1,0},{2,3},{3,2},{4,5},{5,4},{6,7},{7,6},{8,9},{9,8},{10,11... | collective-permute-start | bytes 4718600 | tf_op jit(solution)/shard_map/ppermute | solution.py:27
  445.4 17.8 %collective-permute-start.2 = (bf16[512,3072]{0,1:T(8,128)(2,1)S(1)}, bf16[512,3072]{0,1:T(8,128)(2,1)S(1)}, u32[]{:S(2)}, u32[]{:S(2)}) collective-permute-start(bf16[512,3072]{0,1:T(8,128)(2,1)S(1)} %maximum_select_fusion), channel_id=1, source_target_pairs={{0,2},{1,3},{4,6},{5,7},{8,10},{9,11},{12,14},{13,15},{16,18},{17,... | collective-permute-start | bytes 9437192 | tf_op jit(solution)/shard_map/ppermute | solution.py:17
  463.6 6.2 %copy-start.7 = (bf16[512,3072]{0,1:T(8,128)(2,1)}, bf16[512,3072]{0,1:T(8,128)(2,1)S(1)}, u32[]{:S(2)}) copy-start(bf16[512,3072]{0,1:T(8,128)(2,1)S(1)} %broadcast_select_fusion) | copy-start | bytes 9437188
  463.6 6.4 %copy-start.15 = (f32[2,2,3072]{2,1,0:T(2,128)S(1)}, f32[2,2,3072]{2,1,0:T(2,128)}, u32[]{:S(2)}) copy-start(f32[2,2,3072]{2,1,0:T(2,128)} %param.24) | copy-start | bytes 147460
  469.8 2.4 copy-start.10
  469.8 2.4 collective-permute-start.3
  477.4 19.8 %copy-start.3 = (f32[2,256,1536]{2,1,0:T(8,128)}, f32[2,256,1536]{2,1,0:T(8,128)S(1)}, u32[]{:S(2)}) copy-start(f32[2,256,1536]{2,1,0:T(8,128)S(1)} %get-tuple-element.8) | copy-start | bytes 9437188
  477.4 6.1 copy-start.12
  482.8 2.1 copy-start.13
  484.1 5.4 collective-permute-start.4
  501.2 8.7 %collective-permute-start.5 = (bf16[512,1536]{1,0:T(8,128)(2,1)}, bf16[512,1536]{1,0:T(8,128)(2,1)S(1)}, u32[]{:S(2)}, u32[]{:S(2)}) collective-permute-start(bf16[512,1536]{1,0:T(8,128)(2,1)} %bitcast.41), channel_id=1, source_target_pairs={{2,0},{3,1},{6,4},{7,5},{10,8},{11,9},{14,12},{15,13},{18,16},{19,... | collective-permute-start | bytes 4718600 | tf_op jit(solution)/shard_map/ppermute | solution.py:17
  515.5 85.0 %all-to-all-start.1 = ((bf16[32,48,1536]{2,1,0:T(8,128)(2,1)}), bf16[32,48,1536]{2,1,0:T(8,128)(2,1)}, u32[]{:S(2)}, u32[]{:S(2)}) async-start(bf16[32,48,1536]{2,1,0:T(8,128)(2,1)} %bitcast.118), calls=%async_computation.1 | async-start | bytes 9437184 | tf_op jit(solution)/shard_map/all_to_all | solution.py:199
  526.3 78.0 %copy-start.1 = (bf16[2,256,3072]{2,1,0:T(8,128)(2,1)S(1)}, bf16[2,256,3072]{2,1,0:T(8,128)(2,1)}, u32[]{:S(2)}) copy-start(bf16[2,256,3072]{2,1,0:T(8,128)(2,1)} %param.14) | copy-start | bytes 9437188
  (4 other events, 5.0 us)
Sparse Core Ops, SparseCore 0:
  9.7 296.0 all-gather.1

commit v3 on v1

--- a/solution.py
+++ b/solution.py
@@ -3,6 +3,7 @@
 import jax
 import jax.numpy as jnp
 from jax import lax
+from jax.experimental import pallas as pl
 from jax.sharding import PartitionSpec as P
 
 HEAD_DIM = 128
@@ -25,6 +26,30 @@
 
 def swap(value, axis):
     return lax.ppermute(value, axis, [(0, 1), (1, 0)])
+
+
+def block_matmul(rows, weight, first_block, block_count, width):
+    row_count, depth = rows.shape
+
+    def kernel(rows_ref, weight_ref, out_ref):
+        out_ref[...] = jnp.dot(rows_ref[...], weight_ref[...], preferred_element_type=jnp.float32)
+
+    return pl.pallas_call(
+        kernel,
+        grid=(block_count,),
+        in_specs=[
+            pl.BlockSpec((row_count, depth), lambda n: (0, 0)),
+            pl.BlockSpec((depth, width), lambda n: (0, first_block + n)),
+        ],
+        out_specs=pl.BlockSpec((row_count, width), lambda n: (0, n)),
+        out_shape=jax.ShapeDtypeStruct((row_count, block_count * width), jnp.float32),
+        cost_estimate=pl.CostEstimate(
+            flops=2 * row_count * depth * block_count * width,
+            transcendentals=0,
+            bytes_accessed=2 * depth * (row_count + block_count * width)
+            + 4 * row_count * block_count * width,
+        ),
+    )(rows, weight)
 
 
 def layer_norm(values):
@@ -97,12 +122,11 @@
     )
     gathered = lax.all_gather(packed, "ctl", axis=0, tiled=True)
     count_rows = gathered.shape[0]
-    query_weight = gathered[:, :local_heads]
-    pair_weight = gathered[:, local_heads : 3 * local_heads]
     out_cols = gathered[:, 3 * local_heads : 4 * local_heads]
-    zero_cols = gathered[:, 4 * local_heads :]
-    query_acc = jnp.dot(image_flat, query_weight, preferred_element_type=jnp.float32)
-    pair_acc = jnp.dot(text_flat, pair_weight, preferred_element_type=jnp.float32)
+    projected = block_matmul(text_flat, gathered, 0, 3, local_heads)
+    projected = projected.reshape(micro_count, seq_rows, 3 * local_heads)
+    query_acc = projected[:, text_rows:, :local_heads]
+    pair_acc = projected[:, :, local_heads:]
     gain_pair = qk_gain[0]
     queries = head_norm(
         query_acc.reshape(micro_count, img_rows, head_count, HEAD_DIM), gain_pair[0]
@@ -142,7 +166,7 @@
     )
     act_other = passed_along(act_narrow, "side", 1)
     control_rows = jnp.where(is_control, act_narrow, act_other)
-    own_part = jnp.dot(control_rows, zero_cols, preferred_element_type=jnp.float32)
+    own_part = block_matmul(control_rows, gathered, 4, 1, local_heads)
     own_narrow = own_part.astype(jnp.bfloat16)
     other_narrow = partner(own_narrow, "side", 0)
     residual_narrow = jnp.where(

time: 595 us -> 578 us (0.971)
  matrix products: 49.4 us -> 24.1 us
  Pallas kernels: 0 us -> 23.8 us
  local copies, waits for them, and re-layouts: 68.5 us -> 49.3 us
  other arithmetic: 44.2 us -> 58.6 us
  waiting for transfers between devices: 370 us -> 358 us
    dot_general x3 -> x0, local copies, waits for them, and re-layouts: 27.3 us -> none  [the longest x2 20.7 us: local(): jnp.dot(text_flat, pair_weight, preferred_element_type=jnp.float32)]
    pallas_call x0 -> x2, Pallas kernels: none -> 23.8 us  [block_matmul(): pl.pallas_call(kernel, grid=(block_count,), in_specs=[pl.BlockSpec((row_c...]
    dot_general x3 -> x0, matrix products: 23.6 us -> none  [the longest x1 11.5 us: local(): jnp.dot(text_flat, pair_weight, preferred_element_type=jnp.float32)]
    all_gather x1, waiting for transfers between devices: 228 us -> 217 us  [local(): gathered = lax.all_gather(packed, 'ctl', axis=0, tiled=True)]
    unnamed x43, local copies, waits for them, and re-layouts: 9.55 us -> 16.7 us
    slice x0 -> x2, local copies, waits for them, and re-layouts: none -> 6.32 us  [the longest x1 4.81 us: local(): pair_acc = projected[:, :, local_heads:]]
  transfers between devices with their start and end apart: 8 -> 8, of which waited for: 8 -> 7; matrix products, arithmetic and copies ran while one was open for 7% -> 9% of each run, Pallas kernels for 0% -> 0%
where the time goes in v3:
time: 578 us; the launch traced here: 566 us
  waiting for transfers between devices  358 us (62%)
  other arithmetic  58.6 us (10%)
  local copies, waits for them, and re-layouts  49.3 us (9%)
  starting transfers between devices  26.8 us (5%)
  matrix products  24.1 us (4%)
  Pallas kernels  23.8 us (4%)
  between operations  14.9 us (3%)
  blocking collectives  10.7 us (2%)
    all_gather x1, waiting for transfers between devices, local(): gathered = lax.all_gather(packed, 'ctl', axis=0, tiled=True)  217 us
    ppermute x3, waiting for transfers between devices, swap(): return lax.ppermute(value, axis, [(0, 1), (1, 0)])  66.4 us
    all_to_all x1, waiting for transfers between devices, local(): received = lax.all_to_all(group_parts, 'ctl', 0, 0, tiled=True)  64.8 us
    pallas_call x2, Pallas kernels, block_matmul(): pl.pallas_call(kernel, grid=(block_count,), in_specs=[pl.BlockSpec((row_c...  23.8 us
    unnamed x43, local copies, waits for them, and re-layouts  16.7 us
    gather x1, local copies, waits for them, and re-layouts, local(): jnp.take(latent, order_row, axis=0)  14.8 us
  transfers between devices with their start and end apart: 8, of which 7 were waited for; matrix products, arithmetic and copies ran while one was open for 9% of the time, Pallas kernels for 0%

profile of v3, /device:TPU:5, one launch (start us, length us, event | category | flops | bytes accessed | tf_op | source)
XLA Modules:
  0.0 566.4 jit_solution(3377415263524078255)
XLA Ops:
  12.6 14.8 %gather_fusion.1 = bf16[512,3072]{1,0:T(8,128)(2,1)} fusion(bf16[2,256,3072]{2,1,0:T(8,128)(2,1)S(1)} %copy-done, s32[512]{0:T(512)S(1)} %bitcast.101), kind=kCustom, calls=%fused_computation.1 | custom fusion | bytes 6295552 | tf_op jit(solution)/shard_map/vmap(jit(_take))/gather | solution.py:100
  39.8 6.1 %multiply_reduce_fusion = (f32[2,384]{1,0:T(2,128)S(1)}, f32[2,384,3072]{2,1,0:T(8,128)}) fusion(f32[2,384]{1,0:T(2,128)S(1)} %broadcast_multiply_fusion, f32[2,256,3072]{2,1,0:T(8,128)} %copy-done.2, f32[2,128,3072]{2,1,0:T(8,128)S(1)} %select_convert_fusion), kind=kLoop, calls=%fused_computation.10 | loop fusion | flops 9436416 | bytes 18880512 | tf_op jit(solution)/shard_map/reduce_sum | solution.py:57
  46.0 8.1 %fusion.1.rows_ref = bf16[768,3072]{1,0:T(8,128)(2,1)} fusion(f32[2,384,3072]{2,1,0:T(8,128)} %get-tuple-element.10, f32[2,3072]{1,0:T(2,128)S(1)} %get-tuple-element.12, f32[2,3072]{1,0:T(2,128)S(1)} %get-tuple-element.13, f32[768]{0:T(1024)S(1)} %rsqrt.31, f32[768]{0:T(1024)S(1)} %div.47), kind=kLoop, calls=%fused_computation.5 | loop fusion | flops 11796480 | bytes 14211072 | tf_op jit(solution)/shard_map/convert_element_type | solution.py:108
  54.1 217.4 %all-gather.2.cloned.1.call-done.weight_ref = bf16[3072,3840]{1,0:T(8,128)(2,1)} async-done(((bf16[96,3840]{1,0:T(8,128)(2,1)}), bf16[3072,3840]{1,0:T(8,128)(2,1)}) %all-gather.2.cloned.1.call-update) | async-done | bytes 23592976 | tf_op jit(solution)/shard_map/all_gather | solution.py:123
  271.5 16.7 %shard_map.140 = f32[768,2304]{1,0:T(8,128)} custom-call(bf16[768,3072]{1,0:T(8,128)(2,1)} %fusion.1.rows_ref, bf16[3072,3840]{1,0:T(8,128)(2,1)} %all-gather.2.cloned.1.call-done.weight_ref), custom_call_target="tpu_custom_call" | custom-call | flops 10871635968 | bytes 25952256 | tf_op jit(solution)/shard_map/pallas_call | solution.py:37
  288.2 4.8 slice.59
  294.5 6.2 %copy.31 = f32[2,384,1536]{1,2,0:T(8,128)} copy(f32[2,384,1536]{2,1,0:T(8,128)} %slice.59) | data formatting | bytes 9437184
  309.7 10.0 %fusion.14 = bf16[2,256,6,128]{1,3,2,0:T(8,128)(2,1)S(1)} fusion(f32[2,6,256]{2,1,0:T(8,128)S(1)} %fusion.41, f32[2,6,256,384]{3,2,1,0:T(8,128)} %copy-done.4, f32[2,384,2,6,128]{1,4,3,2,0:T(8,128)} %bitcast.106), kind=kOutput, calls=%fused_computation.47 | convolution fusion | flops 308284800 | bytes 11415552 | tf_op jit(solution)/shard_map/bhij,bjhd->bihd/dot_general | solution.py:141
  331.8 30.7 %collective-permute-done = bf16[512,1536]{1,0:T(8,128)(2,1)} collective-permute-done((bf16[512,1536]{1,0:T(8,128)(2,1)S(1)}, bf16[512,1536]{1,0:T(8,128)(2,1)}, u32[]{:S(2)}, u32[]{:S(2)}) %collective-permute-start) | collective-permute-done | bytes 1572896 | tf_op jit(solution)/shard_map/ppermute | solution.py:28
  364.4 4.9 fusion.20
  372.2 33.2 %collective-permute-done.1 = bf16[512,1536]{1,0:T(8,128)(2,1)} collective-permute-done((bf16[512,1536]{1,0:T(8,128)(2,1)}, bf16[512,1536]{1,0:T(8,128)(2,1)}, u32[]{:S(2)}, u32[]{:S(2)}) %collective-permute-start.1) | collective-permute-done | bytes 1572896 | tf_op jit(solution)/shard_map/ppermute | solution.py:28
  405.4 4.0 maximum_select_fusion
  410.7 7.7 %collective-permute-done.2 = bf16[512,3072]{1,0:T(8,128)(2,1)S(1)} collective-permute-done((bf16[512,3072]{1,0:T(8,128)(2,1)S(1)}, bf16[512,3072]{1,0:T(8,128)(2,1)S(1)}, u32[]{:S(2)}, u32[]{:S(2)}) %collective-permute-start.2) | collective-permute-done | bytes 3145760 | tf_op jit(solution)/shard_map/ppermute | solution.py:18
  420.5 7.1 %shard_map.141 = f32[512,768]{1,0:T(8,128)} custom-call(bf16[512,3072]{1,0:T(8,128)(2,1)} %broadcast_select_fusion.rows_ref, bf16[3072,3840]{1,0:T(8,128)(2,1)} %all-gather.2.cloned.1.call-done.weight_ref), custom_call_target="tpu_custom_call" | custom-call | flops 2415919104 | bytes 9437184 | tf_op jit(solution)/shard_map/pallas_call | solution.py:37
  432.3 4.3 fusion.39
  436.7 5.4 all-reduce.1
  451.2 5.3 all-reduce
  456.4 4.0 multiply_convert_fusion
  460.4 6.9 %collective-permute-start.5 = (bf16[512,1536]{1,0:T(8,128)(2,1)}, bf16[512,1536]{1,0:T(8,128)(2,1)}, u32[]{:S(2)}, u32[]{:S(2)}) collective-permute-start(bf16[512,1536]{1,0:T(8,128)(2,1)} %bitcast.36), channel_id=1, source_target_pairs={{2,0},{3,1},{6,4},{7,5},{10,8},{11,9},{14,12},{15,13},{18,16},{19,... | collective-permute-start | bytes 4718600 | tf_op jit(solution)/shard_map/ppermute | solution.py:18
  470.6 5.7 %convolution_convert_fusion = bf16[1536,1536]{1,0:T(8,128)(2,1)} fusion(bf16[512,1536]{0,1:T(8,128)(2,1)S(1)} %bitcast.122, bf16[512,1536]{1,0:T(8,128)(2,1)} %collective-permute-done.5, bf16[512,1536]{1,0:T(8,128)(2,1)} %bitcast.36, pred[]{:T(512)S(6)} %eq.6), kind=kOutput, calls=%fused_computation.11 | convolution fusion | flops 2419064832 | bytes 9437185 | tf_op jit(solution)/shard_map/dot_general | solution.py:222
  476.4 9.5 %all-to-all-start = ((bf16[32,48,1536]{2,1,0:T(8,128)(2,1)}), bf16[32,48,1536]{2,1,0:T(8,128)(2,1)}, u32[]{:S(2)}, u32[]{:S(2)}) async-start(bf16[32,48,1536]{2,1,0:T(8,128)(2,1)} %bitcast.116), calls=%async_computation | async-start | bytes 9437184 | tf_op jit(solution)/shard_map/all_to_all | solution.py:226
  485.8 4.7 select_bitcast_fusion
  490.5 64.8 %all-to-all-done = bf16[32,48,1536]{2,1,0:T(8,128)(2,1)} async-done(((bf16[32,48,1536]{2,1,0:T(8,128)(2,1)}), bf16[32,48,1536]{2,1,0:T(8,128)(2,1)}, u32[]{:S(2)}, u32[]{:S(2)}) %all-to-all-start) | async-done | bytes 4718624 | tf_op jit(solution)/shard_map/all_to_all | solution.py:226
  555.4 3.7 convert_reduce_fusion
  (96 shorter events, 65.5 us)
Async XLA Ops:
  7.2 5.5 copy-start
  7.2 5.4 copy-start.15
  7.2 264.3 %all-gather.2.cloned.1.call-start = ((), (), s32[]{:S(2)}) async-start(), calls=%async_computation.1 | async-start | bytes 24330240 | tf_op jit(solution)/shard_map/all_gather | solution.py:123
  12.6 14.8 %copy-start.17 = (s32[2]{0:T(128)S(1)}, s32[2]{0:T(128)}, u32[]{:S(2)}) copy-start(s32[2]{0:T(128)} %param.17) | copy-start | bytes 28
  31.1 2.4 copy-start.7
  37.1 2.7 copy-start.2
  39.8 6.1 %copy-start.13 = (f32[1,2,3,3072]{3,1,2,0:T(2,128)S(1)}, f32[1,2,3,3072]{3,1,2,0:T(2,128)}, u32[]{:S(2)}) copy-start(f32[1,2,3,3072]{3,1,2,0:T(2,128)} %param.18) | copy-start | bytes 221188
  46.0 8.1 %copy-start.16 = (f32[1,2,128]{2,1,0:T(2,128)S(1)}, f32[1,2,128]{2,1,0:T(2,128)}, u32[]{:S(2)}) copy-start(f32[1,2,128]{2,1,0:T(2,128)} %param.20) | copy-start | bytes 3076
  305.8 2.2 copy-start.4
  323.4 2.2 copy-start.9
  325.6 36.9 %collective-permute-start = (bf16[512,1536]{1,0:T(8,128)(2,1)S(1)}, bf16[512,1536]{1,0:T(8,128)(2,1)}, u32[]{:S(2)}, u32[]{:S(2)}) collective-permute-start(bf16[512,1536]{1,0:T(8,128)(2,1)S(1)} %convolution_convert_fusion.1), channel_id=1, source_target_pairs={{0,1},{1,0},{2,3},{3,2},{4,5},{5,4},{6,7},{7,6},{8,9},{9,8},{10,11... | collective-permute-start | bytes 4718600 | tf_op jit(solution)/shard_map/ppermute | solution.py:28
  364.4 4.9 copy-start.6
  369.3 36.1 %collective-permute-start.1 = (bf16[512,1536]{1,0:T(8,128)(2,1)}, bf16[512,1536]{1,0:T(8,128)(2,1)}, u32[]{:S(2)}, u32[]{:S(2)}) collective-permute-start(bf16[512,1536]{1,0:T(8,128)(2,1)} %bitcast.20), channel_id=1, source_target_pairs={{0,1},{1,0},{2,3},{3,2},{4,5},{5,4},{6,7},{7,6},{8,9},{9,8},{10,11... | collective-permute-start | bytes 4718600 | tf_op jit(solution)/shard_map/ppermute | solution.py:28
  409.4 9.0 %collective-permute-start.2 = (bf16[512,3072]{1,0:T(8,128)(2,1)S(1)}, bf16[512,3072]{1,0:T(8,128)(2,1)S(1)}, u32[]{:S(2)}, u32[]{:S(2)}) collective-permute-start(bf16[512,3072]{1,0:T(8,128)(2,1)S(1)} %maximum_select_fusion), channel_id=1, source_target_pairs={{0,2},{1,3},{4,6},{5,7},{8,10},{9,11},{12,14},{13,15},{16,18},{17,... | collective-permute-start | bytes 9437192 | tf_op jit(solution)/shard_map/ppermute | solution.py:18
  420.5 8.8 %copy-start.14 = (f32[2,2,3072]{2,1,0:T(2,128)S(1)}, f32[2,2,3072]{2,1,0:T(2,128)}, u32[]{:S(2)}) copy-start(f32[2,2,3072]{2,1,0:T(2,128)} %param.24) | copy-start | bytes 147460
  429.1 2.4 copy-start.8
  429.1 2.4 collective-permute-start.3
  436.7 19.8 %copy-start.3 = (f32[2,256,1536]{2,1,0:T(8,128)}, f32[2,256,1536]{2,1,0:T(8,128)S(1)}, u32[]{:S(2)}) copy-start(f32[2,256,1536]{2,1,0:T(8,128)S(1)} %get-tuple-element.8) | copy-start | bytes 9437188
  436.7 6.1 %copy-start.11 = (bf16[1536,64]{0,1:T(8,128)(2,1)S(1)}, bf16[1536,64]{0,1:T(8,128)(2,1)}, u32[]{:S(2)}) copy-start(bf16[1536,64]{0,1:T(8,128)(2,1)} %param.23) | copy-start | bytes 589828
  442.1 4.2 copy-start.12
  443.4 5.4 collective-permute-start.4
  460.4 10.2 %collective-permute-start.5 = (bf16[512,1536]{1,0:T(8,128)(2,1)}, bf16[512,1536]{1,0:T(8,128)(2,1)}, u32[]{:S(2)}, u32[]{:S(2)}) collective-permute-start(bf16[512,1536]{1,0:T(8,128)(2,1)} %bitcast.36), channel_id=1, source_target_pairs={{2,0},{3,1},{6,4},{7,5},{10,8},{11,9},{14,12},{15,13},{18,16},{19,... | collective-permute-start | bytes 4718600 | tf_op jit(solution)/shard_map/ppermute | solution.py:18
  476.4 79.0 %all-to-all-start = ((bf16[32,48,1536]{2,1,0:T(8,128)(2,1)}), bf16[32,48,1536]{2,1,0:T(8,128)(2,1)}, u32[]{:S(2)}, u32[]{:S(2)}) async-start(bf16[32,48,1536]{2,1,0:T(8,128)(2,1)} %bitcast.116), calls=%async_computation | async-start | bytes 9437184 | tf_op jit(solution)/shard_map/all_to_all | solution.py:226
  485.8 73.3 %copy-start.1 = (bf16[2,256,3072]{2,1,0:T(8,128)(2,1)S(1)}, bf16[2,256,3072]{2,1,0:T(8,128)(2,1)}, u32[]{:S(2)}) copy-start(bf16[2,256,3072]{2,1,0:T(8,128)(2,1)} %param.14) | copy-start | bytes 9437188
  (2 other events, 2.6 us)
Sparse Core Ops, SparseCore 0:
  12.7 258.7 all-gather.1

commit v4 on v3

--- a/solution.py
+++ b/solution.py
@@ -128,42 +128,49 @@
     query_acc = projected[:, text_rows:, :local_heads]
     pair_acc = projected[:, :, local_heads:]
     gain_pair = qk_gain[0]
-    queries = head_norm(
-        query_acc.reshape(micro_count, img_rows, head_count, HEAD_DIM), gain_pair[0]
-    )
-    pair_acc = pair_acc.reshape(micro_count, seq_rows, 2, head_count, HEAD_DIM)
-    keys_all = head_norm(pair_acc[:, :, 0], gain_pair[1])
-    values_all = pair_acc[:, :, 1].astype(jnp.bfloat16)
-    scores = jnp.einsum(
-        "bihd,bjhd->bhij", queries, keys_all, preferred_element_type=jnp.float32
-    ) / math.sqrt(HEAD_DIM)
-    attend = jax.nn.softmax(scores, axis=-1).astype(jnp.bfloat16)
-    mixed_heads = jnp.einsum(
-        "bhij,bjhd->bihd", attend, values_all, preferred_element_type=jnp.float32
-    )
-    mixed_heads = mixed_heads.astype(jnp.bfloat16).reshape(flat_rows, local_heads)
     contract_last = (((1,), (1,)), ((), ()))
     other_out = lax.dynamic_slice_in_dim(out_cols, (1 - tp_index) * half_width, half_width, 0)
     own_out = lax.dynamic_slice_in_dim(out_cols, tp_index * half_width, half_width, 0)
-    other_part = lax.dot_general(
-        mixed_heads, other_out, contract_last, preferred_element_type=jnp.float32
-    ).astype(jnp.bfloat16)
-    got_part = swap(other_part, "tp")
-    own_part_heads = rounded(
-        lax.dot_general(mixed_heads, own_out, contract_last, preferred_element_type=jnp.float32)
-    )
-    head_sum = own_part_heads + got_part.astype(jnp.float32)
     hid_half = lax.dynamic_slice_in_dim(hidden, tp_index * half_width, half_width, 2)
     gate_half = lax.dynamic_slice_in_dim(modulate[:, 2:3], tp_index * half_width, half_width, 2)
-    act_half = hid_half + gate_half * head_sum.reshape(micro_count, img_rows, half_width)
-    act_half = act_half.reshape(flat_rows, half_width)
-    act_own = act_half.astype(jnp.bfloat16)
-    act_got = swap(act_own, "tp")
-    act_narrow = jnp.where(
-        tp_index == 0,
-        jnp.concatenate([act_own, act_got], axis=1),
-        jnp.concatenate([act_got, act_own], axis=1),
-    )
+    act_halves = []
+    act_rows = []
+    for sample in range(micro_count):
+        queries = head_norm(
+            query_acc[sample].reshape(img_rows, head_count, HEAD_DIM), gain_pair[0]
+        )
+        pair_one = pair_acc[sample].reshape(seq_rows, 2, head_count, HEAD_DIM)
+        keys_all = head_norm(pair_one[:, 0], gain_pair[1])
+        values_all = pair_one[:, 1].astype(jnp.bfloat16)
+        scores = jnp.einsum(
+            "ihd,jhd->hij", queries, keys_all, preferred_element_type=jnp.float32
+        ) / math.sqrt(HEAD_DIM)
+        attend = jax.nn.softmax(scores, axis=-1).astype(jnp.bfloat16)
+        mixed_heads = jnp.einsum(
+            "hij,jhd->ihd", attend, values_all, preferred_element_type=jnp.float32
+        )
+        mixed_heads = mixed_heads.astype(jnp.bfloat16).reshape(img_rows, local_heads)
+        other_part = lax.dot_general(
+            mixed_heads, other_out, contract_last, preferred_element_type=jnp.float32
+        ).astype(jnp.bfloat16)
+        got_part = swap(other_part, "tp")
+        own_part_heads = rounded(
+            lax.dot_general(mixed_heads, own_out, contract_last, preferred_element_type=jnp.float32)
+        )
+        head_sum = own_part_heads + got_part.astype(jnp.float32)
+        act_one = hid_half[sample] + gate_half[sample] * head_sum
+        act_own = act_one.astype(jnp.bfloat16)
+        act_got = swap(act_own, "tp")
+        act_halves.append(act_one)
+        act_rows.append(
+            jnp.where(
+                tp_index == 0,
+                jnp.concatenate([act_own, act_got], axis=1),
+                jnp.concatenate([act_got, act_own], axis=1),
+            )
+        )
+    act_half = jnp.concatenate(act_halves, axis=0)
+    act_narrow = jnp.concatenate(act_rows, axis=0)
     act_other = passed_along(act_narrow, "side", 1)
     control_rows = jnp.where(is_control, act_narrow, act_other)
     own_part = block_matmul(control_rows, gathered, 4, 1, local_heads)

time: 578 us -> 567 us (0.981)
  waiting for transfers between devices: 358 us -> 347 us
  matrix products: 24.1 us -> 30.5 us
    ppermute x3 -> x5, waiting for transfers between devices: 66.4 us -> 47.8 us  [swap(): return lax.ppermute(value, axis, [(0, 1), (1, 0)])]
    all_to_all x1, waiting for transfers between devices: 64.8 us -> 71.7 us  [local(): received = lax.all_to_all(group_parts, 'ctl', 0, 0, tiled=True)]
    unnamed x43 -> x52, local copies, waits for them, and re-layouts: 16.7 us -> 10.8 us
    slice x2 -> x5, local copies, waits for them, and re-layouts: 6.32 us -> 11.8 us  [the longest x3 9.06 us: local(): pair_one = pair_acc[sample].reshape(seq_rows, 2, head_count, HEAD_DIM)]
    dot_general x2 -> x4, matrix products: 12.6 us -> 11.8 us  [the longest x2 10.7 us: local(): jnp.einsum('hij,jhd->ihd', attend, values_all, preferred_element_type=jnp...]
  transfers between devices with their start and end apart: 8 -> 10, of which waited for: 7 -> 8; matrix products, arithmetic and copies ran while one was open for 9% -> 12% of each run, Pallas kernels for 0% -> 0%
where the time goes in v4:
time: 567 us; the launch traced here: 557 us
  waiting for transfers between devices  347 us (61%)
  other arithmetic  55.6 us (10%)
  local copies, waits for them, and re-layouts  48.2 us (9%)
  matrix products  30.5 us (5%)
  starting transfers between devices  26.2 us (5%)
  Pallas kernels  23.8 us (4%)
  between operations  15 us (3%)
  blocking collectives  10.8 us (2%)
    all_gather x1, waiting for transfers between devices, local(): gathered = lax.all_gather(packed, 'ctl', axis=0, tiled=True)  217 us
    all_to_all x1, waiting for transfers between devices, local(): received = lax.all_to_all(group_parts, 'ctl', 0, 0, tiled=True)  71.7 us
    ppermute x5, waiting for transfers between devices, swap(): return lax.ppermute(value, axis, [(0, 1), (1, 0)])  47.8 us
    pallas_call x2, Pallas kernels, block_matmul(): pl.pallas_call(kernel, grid=(block_count,), in_specs=[pl.BlockSpec((row_c...  23.8 us
    gather x1, local copies, waits for them, and re-layouts, local(): jnp.take(latent, order_row, axis=0)  14.8 us
  transfers between devices with their start and end apart: 10, of which 8 were waited for; matrix products, arithmetic and copies ran while one was open for 12% of the time, Pallas kernels for 0%

profile of v4, /device:TPU:5, one launch (start us, length us, event | category | flops | bytes accessed | tf_op | source)
XLA Modules:
  0.0 557.0 jit_solution(16773006445229831885)
XLA Ops:
  12.6 14.8 %gather_fusion.1 = bf16[512,3072]{1,0:T(8,128)(2,1)} fusion(bf16[2,256,3072]{2,1,0:T(8,128)(2,1)S(1)} %copy-done, s32[512]{0:T(512)S(1)} %bitcast.124), kind=kCustom, calls=%fused_computation.1 | custom fusion | bytes 6295552 | tf_op jit(solution)/shard_map/vmap(jit(_take))/gather | solution.py:100
  39.8 6.1 %multiply_reduce_fusion = (f32[2,384]{1,0:T(2,128)S(1)}, f32[2,384,3072]{2,1,0:T(8,128)}) fusion(f32[2,384]{1,0:T(2,128)S(1)} %broadcast_multiply_fusion, f32[2,256,3072]{2,1,0:T(8,128)} %copy-done.2, f32[2,128,3072]{2,1,0:T(8,128)S(1)} %select_convert_fusion), kind=kLoop, calls=%fused_computation.11 | loop fusion | flops 9436416 | bytes 18880512 | tf_op jit(solution)/shard_map/reduce_sum | solution.py:57
  45.9 8.1 %fusion.2.rows_ref = bf16[768,3072]{1,0:T(8,128)(2,1)} fusion(f32[2,384,3072]{2,1,0:T(8,128)} %get-tuple-element.18, f32[2,3072]{1,0:T(2,128)S(1)} %get-tuple-element.27, f32[2,3072]{1,0:T(2,128)S(1)} %get-tuple-element.28, f32[768]{0:T(1024)S(1)} %rsqrt.47, f32[768]{0:T(1024)S(1)} %div.55), kind=kLoop, calls=%fused_computation.6 | loop fusion | flops 11796480 | bytes 14211072 | tf_op jit(solution)/shard_map/convert_element_type | solution.py:108
  54.1 217.3 %all-gather.2.cloned.1.call-done.weight_ref = bf16[3072,3840]{1,0:T(8,128)(2,1)} async-done(((bf16[96,3840]{1,0:T(8,128)(2,1)}), bf16[3072,3840]{1,0:T(8,128)(2,1)}) %all-gather.2.cloned.1.call-update) | async-done | bytes 23592976 | tf_op jit(solution)/shard_map/all_gather | solution.py:123
  271.4 16.7 %shard_map.140 = f32[768,2304]{1,0:T(8,128)} custom-call(bf16[768,3072]{1,0:T(8,128)(2,1)} %fusion.2.rows_ref, bf16[3072,3840]{1,0:T(8,128)(2,1)} %all-gather.2.cloned.1.call-done.weight_ref), custom_call_target="tpu_custom_call" | custom-call | flops 10871635968 | bytes 25952256 | tf_op jit(solution)/shard_map/pallas_call | solution.py:37
  288.1 4.8 fusion.69
  302.3 5.3 convolution_convert_fusion.5
  322.2 5.4 convolution_convert_fusion.6
  335.8 14.2 %collective-permute-done = bf16[256,1536]{1,0:T(8,128)(2,1)S(1)} collective-permute-done((bf16[256,1536]{1,0:T(8,128)(2,1)S(1)}, bf16[256,1536]{1,0:T(8,128)(2,1)S(1)}, u32[]{:S(2)}, u32[]{:S(2)}) %collective-permute-start) | collective-permute-done | bytes 786464 | tf_op jit(solution)/shard_map/ppermute | solution.py:28
  350.0 4.5 fusion.64
  357.5 15.8 %collective-permute-done.1 = bf16[256,1536]{1,0:T(8,128)(2,1)} collective-permute-done((bf16[256,1536]{1,0:T(8,128)(2,1)S(1)}, bf16[256,1536]{1,0:T(8,128)(2,1)}, u32[]{:S(2)}, u32[]{:S(2)}) %collective-permute-start.1) | collective-permute-done | bytes 786464 | tf_op jit(solution)/shard_map/ppermute | solution.py:28
  375.1 15.0 %collective-permute-done.3 = bf16[256,1536]{1,0:T(8,128)(2,1)} collective-permute-done((bf16[256,1536]{1,0:T(8,128)(2,1)S(1)}, bf16[256,1536]{1,0:T(8,128)(2,1)}, u32[]{:S(2)}, u32[]{:S(2)}) %collective-permute-start.3) | collective-permute-done | bytes 786464 | tf_op jit(solution)/shard_map/ppermute | solution.py:28
  394.0 8.0 %collective-permute-done.4 = bf16[512,3072]{1,0:T(8,128)(2,1)S(1)} collective-permute-done((bf16[512,3072]{1,0:T(8,128)(2,1)S(1)}, bf16[512,3072]{1,0:T(8,128)(2,1)S(1)}, u32[]{:S(2)}, u32[]{:S(2)}) %collective-permute-start.4) | collective-permute-done | bytes 3145760 | tf_op jit(solution)/shard_map/ppermute | solution.py:18
  404.8 7.1 %shard_map.141 = f32[512,768]{1,0:T(8,128)} custom-call(bf16[512,3072]{1,0:T(8,128)(2,1)} %broadcast_select_fusion.rows_ref, bf16[3072,3840]{1,0:T(8,128)(2,1)} %all-gather.2.cloned.1.call-done.weight_ref), custom_call_target="tpu_custom_call" | custom-call | flops 2415919104 | bytes 9437184 | tf_op jit(solution)/shard_map/pallas_call | solution.py:37
  416.0 4.4 fusion.63
  420.4 5.3 all-reduce.1
  435.2 5.5 all-reduce
  440.8 3.9 multiply_convert_fusion
  444.7 6.7 %collective-permute-start.7 = (bf16[512,1536]{1,0:T(8,128)(2,1)}, bf16[512,1536]{1,0:T(8,128)(2,1)}, u32[]{:S(2)}, u32[]{:S(2)}) collective-permute-start(bf16[512,1536]{1,0:T(8,128)(2,1)} %multiply_convert_fusion), channel_id=1, source_target_pairs={{2,0},{3,1},{6,4},{7,5},{10,8},{11,9},{14,12},{15,13},{18,16},{19,... | collective-permute-start | bytes 4718600 | tf_op jit(solution)/shard_map/ppermute | solution.py:18
  454.6 5.7 %convolution_convert_fusion = bf16[1536,1536]{1,0:T(8,128)(2,1)} fusion(bf16[512,1536]{0,1:T(8,128)(2,1)S(1)} %bitcast.145, bf16[512,1536]{1,0:T(8,128)(2,1)} %collective-permute-done.7, bf16[512,1536]{1,0:T(8,128)(2,1)} %multiply_convert_fusion, pred[]{:T(512)S(6)} %eq.7), kind=kOutput, calls=%fused_computation.12 | convolution fusion | flops 2419064832 | bytes 9437185 | tf_op jit(solution)/shard_map/dot_general | solution.py:229
  460.4 9.2 %all-to-all-start = ((bf16[32,48,1536]{2,1,0:T(8,128)(2,1)}), bf16[32,48,1536]{2,1,0:T(8,128)(2,1)}, u32[]{:S(2)}, u32[]{:S(2)}) async-start(bf16[32,48,1536]{2,1,0:T(8,128)(2,1)} %bitcast.141), calls=%async_computation | async-start | bytes 9437184 | tf_op jit(solution)/shard_map/all_to_all | solution.py:233
  469.5 4.7 fusion.6
  474.3 71.7 %all-to-all-done = bf16[32,48,1536]{2,1,0:T(8,128)(2,1)} async-done(((bf16[32,48,1536]{2,1,0:T(8,128)(2,1)}), bf16[32,48,1536]{2,1,0:T(8,128)(2,1)}, u32[]{:S(2)}, u32[]{:S(2)}) %all-to-all-start) | async-done | bytes 4718624 | tf_op jit(solution)/shard_map/all_to_all | solution.py:233
  546.0 3.7 convert_reduce_fusion
  (122 shorter events, 78.1 us)
Async XLA Ops:
  7.2 5.4 copy-start
  7.2 3.4 copy-start.12
  7.2 5.3 copy-start.16
  7.2 264.2 %all-gather.2.cloned.1.call-start = ((), (), s32[]{:S(2)}) async-start(), calls=%async_computation.1 | async-start | bytes 24330240 | tf_op jit(solution)/shard_map/all_gather | solution.py:123
  12.6 14.8 %copy-start.18 = (s32[2]{0:T(128)S(1)}, s32[2]{0:T(128)}, u32[]{:S(2)}) copy-start(s32[2]{0:T(128)} %param.17) | copy-start | bytes 28
  39.8 6.1 %copy-start.14 = (f32[1,2,3,3072]{3,1,2,0:T(2,128)S(1)}, f32[1,2,3,3072]{3,1,2,0:T(2,128)}, u32[]{:S(2)}) copy-start(f32[1,2,3,3072]{3,1,2,0:T(2,128)} %param.18) | copy-start | bytes 221188
  45.9 8.1 %copy-start.17 = (f32[1,2,128]{2,1,0:T(2,128)S(1)}, f32[1,2,128]{2,1,0:T(2,128)}, u32[]{:S(2)}) copy-start(f32[1,2,128]{2,1,0:T(2,128)} %param.20) | copy-start | bytes 3076
  310.4 5.2 copy-start.6
  312.7 23.1 %collective-permute-start.2 = (bf16[256,1536]{1,0:T(8,128)(2,1)}, bf16[256,1536]{1,0:T(8,128)(2,1)}, u32[]{:S(2)}, u32[]{:S(2)}) collective-permute-start(bf16[256,1536]{1,0:T(8,128)(2,1)} %convolution_convert_fusion.1), channel_id=1, source_target_pairs={{0,1},{1,0},{2,3},{3,2},{4,5},{5,4},{6,7},{7,6},{8,9},{9,8},{10,11... | collective-permute-start | bytes 2359304 | tf_op jit(solution)/shard_map/ppermute | solution.py:28
  327.7 3.1 copy-start.20
  330.2 19.8 %collective-permute-start = (bf16[256,1536]{1,0:T(8,128)(2,1)S(1)}, bf16[256,1536]{1,0:T(8,128)(2,1)S(1)}, u32[]{:S(2)}, u32[]{:S(2)}) collective-permute-start(bf16[256,1536]{1,0:T(8,128)(2,1)S(1)} %convolution_convert_fusion.3), channel_id=1, source_target_pairs={{0,1},{1,0},{2,3},{3,2},{4,5},{5,4},{6,7},{7,6},{8,9},{9,8},{10,11... | collective-permute-start | bytes 2359304 | tf_op jit(solution)/shard_map/ppermute | solution.py:28
  354.5 20.6 %copy-start.8 = (bf16[256,1536]{1,0:T(8,128)(2,1)}, bf16[256,1536]{1,0:T(8,128)(2,1)S(1)}, u32[]{:S(2)}) copy-start(bf16[256,1536]{1,0:T(8,128)(2,1)S(1)} %get-tuple-element.23) | copy-start | bytes 2359300
  354.5 18.7 %collective-permute-start.1 = (bf16[256,1536]{1,0:T(8,128)(2,1)S(1)}, bf16[256,1536]{1,0:T(8,128)(2,1)}, u32[]{:S(2)}, u32[]{:S(2)}) collective-permute-start(bf16[256,1536]{1,0:T(8,128)(2,1)S(1)} %get-tuple-element.13), channel_id=1, source_target_pairs={{0,1},{1,0},{2,3},{3,2},{4,5},{5,4},{6,7},{7,6},{8,9},{9,8},{10,11... | collective-permute-start | bytes 2359304 | tf_op jit(solution)/shard_map/ppermute | solution.py:28
  356.9 33.2 %collective-permute-start.3 = (bf16[256,1536]{1,0:T(8,128)(2,1)S(1)}, bf16[256,1536]{1,0:T(8,128)(2,1)}, u32[]{:S(2)}, u32[]{:S(2)}) collective-permute-start(bf16[256,1536]{1,0:T(8,128)(2,1)S(1)} %get-tuple-element.23), channel_id=1, source_target_pairs={{0,1},{1,0},{2,3},{3,2},{4,5},{5,4},{6,7},{7,6},{8,9},{9,8},{10,11... | collective-permute-start | bytes 2359304 | tf_op jit(solution)/shard_map/ppermute | solution.py:28
  392.7 9.3 %collective-permute-start.4 = (bf16[512,3072]{1,0:T(8,128)(2,1)S(1)}, bf16[512,3072]{1,0:T(8,128)(2,1)S(1)}, u32[]{:S(2)}, u32[]{:S(2)}) collective-permute-start(bf16[512,3072]{1,0:T(8,128)(2,1)S(1)} %pad_maximum_fusion.1), channel_id=1, source_target_pairs={{0,2},{1,3},{4,6},{5,7},{8,10},{9,11},{12,14},{13,15},{16,18},{17,... | collective-permute-start | bytes 9437192 | tf_op jit(solution)/shard_map/ppermute | solution.py:18
  412.0 4.0 copy-start.5
  413.6 6.8 %copy-start.4 = (bf16[512,768]{1,0:T(8,128)(2,1)}, bf16[512,768]{1,0:T(8,128)(2,1)S(1)}, u32[]{:S(2)}) copy-start(bf16[512,768]{1,0:T(8,128)(2,1)S(1)} %convert_element_type.157) | copy-start | bytes 2359300
  413.6 2.4 collective-permute-start.5
  416.0 4.5 copy-start.7
  425.8 4.0 copy-start.13
  427.3 5.4 collective-permute-start.6
  444.7 10.0 %collective-permute-start.7 = (bf16[512,1536]{1,0:T(8,128)(2,1)}, bf16[512,1536]{1,0:T(8,128)(2,1)}, u32[]{:S(2)}, u32[]{:S(2)}) collective-permute-start(bf16[512,1536]{1,0:T(8,128)(2,1)} %multiply_convert_fusion), channel_id=1, source_target_pairs={{2,0},{3,1},{6,4},{7,5},{10,8},{11,9},{14,12},{15,13},{18,16},{19,... | collective-permute-start | bytes 4718600 | tf_op jit(solution)/shard_map/ppermute | solution.py:18
  460.4 85.6 %all-to-all-start = ((bf16[32,48,1536]{2,1,0:T(8,128)(2,1)}), bf16[32,48,1536]{2,1,0:T(8,128)(2,1)}, u32[]{:S(2)}, u32[]{:S(2)}) async-start(bf16[32,48,1536]{2,1,0:T(8,128)(2,1)} %bitcast.141), calls=%async_computation | async-start | bytes 9437184 | tf_op jit(solution)/shard_map/all_to_all | solution.py:233
  469.5 80.2 %copy-start.1 = (bf16[2,256,3072]{2,1,0:T(8,128)(2,1)S(1)}, bf16[2,256,3072]{2,1,0:T(8,128)(2,1)}, u32[]{:S(2)}) copy-start(bf16[2,256,3072]{2,1,0:T(8,128)(2,1)} %param.14) | copy-start | bytes 9437188
  (7 other events, 13.7 us)
Sparse Core Ops, SparseCore 0:
  12.6 258.7 all-gather.1

commit v5 on v4

--- a/solution.py
+++ b/solution.py
@@ -160,7 +160,7 @@
         head_sum = own_part_heads + got_part.astype(jnp.float32)
         act_one = hid_half[sample] + gate_half[sample] * head_sum
         act_own = act_one.astype(jnp.bfloat16)
-        act_got = swap(act_own, "tp")
+        act_got = lax.ppermute(act_own, ("side", "tp"), [(0, 1), (1, 0)])
         act_halves.append(act_one)
         act_rows.append(
             jnp.where(

time: 567 us -> 549 us (0.968)
  the two profiles are of different devices: /device:TPU:5 before, /device:TPU:49 now
where the time goes in v5:
time: 549 us; the launch traced here: 540 us
  waiting for transfers between devices  331 us (60%)
  other arithmetic  55.6 us (10%)
  local copies, waits for them, and re-layouts  48.2 us (9%)
  matrix products  30.5 us (6%)
  starting transfers between devices  25.4 us (5%)
  Pallas kernels  23.8 us (4%)
  between operations  15 us (3%)
  blocking collectives  10.5 us (2%)
    all_gather x1, waiting for transfers between devices, local(): gathered = lax.all_gather(packed, 'ctl', axis=0, tiled=True)  218 us
    all_to_all x1, waiting for transfers between devices, local(): received = lax.all_to_all(group_parts, 'ctl', 0, 0, tiled=True)  67.9 us
    ppermute x2, waiting for transfers between devices, passed_along(): return lax.ppermute(shard, axis, pairs)  26 us
    pallas_call x2, Pallas kernels, block_matmul(): pl.pallas_call(kernel, grid=(block_count,), in_specs=[pl.BlockSpec((row_c...  23.8 us
    ppermute x3, waiting for transfers between devices, swap(): return lax.ppermute(value, axis, [(0, 1), (1, 0)])  16.8 us
    gather x1, local copies, waits for them, and re-layouts, local(): jnp.take(latent, order_row, axis=0)  14.8 us
  transfers between devices with their start and end apart: 10, of which 6 were waited for; matrix products, arithmetic and copies ran while one was open for 12% of the time, Pallas kernels for 0%

profile of v5, /device:TPU:49, one launch (start us, length us, event | category | flops | bytes accessed | tf_op | source)
XLA Modules:
  0.0 540.1 jit_solution(10147647707800917474)
XLA Ops:
  12.6 14.8 %gather_fusion.1 = bf16[512,3072]{1,0:T(8,128)(2,1)} fusion(bf16[2,256,3072]{2,1,0:T(8,128)(2,1)S(1)} %copy-done, s32[512]{0:T(512)S(1)} %bitcast.124), kind=kCustom, calls=%fused_computation.1 | custom fusion | bytes 6295552 | tf_op jit(solution)/shard_map/vmap(jit(_take))/gather | solution.py:100
  27.3 3.7 gather_fusion
  33.4 3.6 multiply_add_fusion
  39.7 6.1 %multiply_reduce_fusion = (f32[2,384]{1,0:T(2,128)S(1)}, f32[2,384,3072]{2,1,0:T(8,128)}) fusion(f32[2,384]{1,0:T(2,128)S(1)} %broadcast_multiply_fusion, f32[2,256,3072]{2,1,0:T(8,128)} %copy-done.2, f32[2,128,3072]{2,1,0:T(8,128)S(1)} %select_convert_fusion), kind=kLoop, calls=%fused_computation.11 | loop fusion | flops 9436416 | bytes 18880512 | tf_op jit(solution)/shard_map/reduce_sum | solution.py:57
  45.9 8.1 %fusion.2.rows_ref = bf16[768,3072]{1,0:T(8,128)(2,1)} fusion(f32[2,384,3072]{2,1,0:T(8,128)} %get-tuple-element.18, f32[2,3072]{1,0:T(2,128)S(1)} %get-tuple-element.27, f32[2,3072]{1,0:T(2,128)S(1)} %get-tuple-element.28, f32[768]{0:T(1024)S(1)} %rsqrt.47, f32[768]{0:T(1024)S(1)} %div.55), kind=kLoop, calls=%fused_computation.6 | loop fusion | flops 11796480 | bytes 14211072 | tf_op jit(solution)/shard_map/convert_element_type | solution.py:108
  54.0 218.3 %all-gather.2.cloned.1.call-done.weight_ref = bf16[3072,3840]{1,0:T(8,128)(2,1)} async-done(((bf16[96,3840]{1,0:T(8,128)(2,1)}), bf16[3072,3840]{1,0:T(8,128)(2,1)}) %all-gather.2.cloned.1.call-update) | async-done | bytes 23592976 | tf_op jit(solution)/shard_map/all_gather | solution.py:123
  272.4 16.7 %shard_map.140 = f32[768,2304]{1,0:T(8,128)} custom-call(bf16[768,3072]{1,0:T(8,128)(2,1)} %fusion.2.rows_ref, bf16[3072,3840]{1,0:T(8,128)(2,1)} %all-gather.2.cloned.1.call-done.weight_ref), custom_call_target="tpu_custom_call" | custom-call | flops 10871635968 | bytes 25952256 | tf_op jit(solution)/shard_map/pallas_call | solution.py:37
  289.0 4.8 fusion.69
  303.3 5.3 convolution_convert_fusion.5
  322.6 5.4 %convolution_convert_fusion.6 = bf16[6,128,256]{2,1,0:T(8,128)(2,1)S(1)} fusion(f32[6,256]{1,0:T(8,128)S(1)} %fusion.71, f32[384,2,6,128]{0,3,2,1:T(8,128)S(1)} %bitcast.129, f32[6,256,384]{2,1,0:T(8,128)} %copy-done.9), kind=kOutput, calls=%fused_computation.56 | convolution fusion | flops 154142592 | bytes 5709824 | tf_op jit(solution)/shard_map/hij,jhd->ihd/dot_general | solution.py:149
  336.7 13.6 %collective-permute-done = bf16[256,1536]{1,0:T(8,128)(2,1)S(1)} collective-permute-done((bf16[256,1536]{1,0:T(8,128)(2,1)S(1)}, bf16[256,1536]{1,0:T(8,128)(2,1)S(1)}, u32[]{:S(2)}, u32[]{:S(2)}) %collective-permute-start) | collective-permute-done | bytes 786464 | tf_op jit(solution)/shard_map/ppermute | solution.py:28
  350.4 4.5 fusion.64
  363.7 26.0 %collective-permute-done.4 = bf16[512,3072]{1,0:T(8,128)(2,1)S(1)} collective-permute-done((bf16[512,3072]{1,0:T(8,128)(2,1)S(1)}, bf16[512,3072]{1,0:T(8,128)(2,1)S(1)}, u32[]{:S(2)}, u32[]{:S(2)}) %collective-permute-start.4) | collective-permute-done | bytes 3145760 | tf_op jit(solution)/shard_map/ppermute | solution.py:18
  392.7 7.1 %shard_map.141 = f32[512,768]{1,0:T(8,128)} custom-call(bf16[512,3072]{1,0:T(8,128)(2,1)} %broadcast_select_fusion.rows_ref, bf16[3072,3840]{1,0:T(8,128)(2,1)} %all-gather.2.cloned.1.call-done.weight_ref), custom_call_target="tpu_custom_call" | custom-call | flops 2415919104 | bytes 9437184 | tf_op jit(solution)/shard_map/pallas_call | solution.py:37
  403.8 4.4 fusion.63
  408.3 5.3 all-reduce.1
  423.1 5.3 all-reduce
  428.4 3.9 multiply_convert_fusion
  432.2 6.9 %collective-permute-start.7 = (bf16[512,1536]{1,0:T(8,128)(2,1)}, bf16[512,1536]{1,0:T(8,128)(2,1)}, u32[]{:S(2)}, u32[]{:S(2)}) collective-permute-start(bf16[512,1536]{1,0:T(8,128)(2,1)} %multiply_convert_fusion), channel_id=1, source_target_pairs={{2,0},{3,1},{6,4},{7,5},{10,8},{11,9},{14,12},{15,13},{18,16},{19,... | collective-permute-start | bytes 4718600 | tf_op jit(solution)/shard_map/ppermute | solution.py:18
  442.5 5.7 %convolution_convert_fusion = bf16[1536,1536]{1,0:T(8,128)(2,1)} fusion(bf16[512,1536]{0,1:T(8,128)(2,1)S(1)} %bitcast.145, bf16[512,1536]{1,0:T(8,128)(2,1)} %collective-permute-done.7, bf16[512,1536]{1,0:T(8,128)(2,1)} %multiply_convert_fusion, pred[]{:T(512)S(6)} %eq.7), kind=kOutput, calls=%fused_computation.12 | convolution fusion | flops 2419064832 | bytes 9437185 | tf_op jit(solution)/shard_map/dot_general | solution.py:229
  448.2 8.3 %all-to-all-start = ((bf16[32,48,1536]{2,1,0:T(8,128)(2,1)}), bf16[32,48,1536]{2,1,0:T(8,128)(2,1)}, u32[]{:S(2)}, u32[]{:S(2)}) async-start(bf16[32,48,1536]{2,1,0:T(8,128)(2,1)} %bitcast.141), calls=%async_computation | async-start | bytes 9437184 | tf_op jit(solution)/shard_map/all_to_all | solution.py:233
  456.5 4.7 fusion.6
  461.2 67.9 %all-to-all-done = bf16[32,48,1536]{2,1,0:T(8,128)(2,1)} async-done(((bf16[32,48,1536]{2,1,0:T(8,128)(2,1)}), bf16[32,48,1536]{2,1,0:T(8,128)(2,1)}, u32[]{:S(2)}, u32[]{:S(2)}) %all-to-all-start) | async-done | bytes 4718624 | tf_op jit(solution)/shard_map/all_to_all | solution.py:233
  529.1 3.7 convert_reduce_fusion
  (122 shorter events, 70.9 us)
Async XLA Ops:
  7.2 5.4 copy-start
  7.2 3.4 copy-start.12
  7.2 5.3 copy-start.16
  7.2 265.2 %all-gather.2.cloned.1.call-start = ((), (), s32[]{:S(2)}) async-start(), calls=%async_computation.1 | async-start | bytes 24330240 | tf_op jit(solution)/shard_map/all_gather | solution.py:123
  12.6 14.8 %copy-start.18 = (s32[2]{0:T(128)S(1)}, s32[2]{0:T(128)}, u32[]{:S(2)}) copy-start(s32[2]{0:T(128)} %param.17) | copy-start | bytes 28
  39.7 6.1 %copy-start.14 = (f32[1,2,3,3072]{3,1,2,0:T(2,128)S(1)}, f32[1,2,3,3072]{3,1,2,0:T(2,128)}, u32[]{:S(2)}) copy-start(f32[1,2,3,3072]{3,1,2,0:T(2,128)} %param.18) | copy-start | bytes 221188
  45.9 8.2 %copy-start.17 = (f32[1,2,128]{2,1,0:T(2,128)S(1)}, f32[1,2,128]{2,1,0:T(2,128)}, u32[]{:S(2)}) copy-start(f32[1,2,128]{2,1,0:T(2,128)} %param.20) | copy-start | bytes 3076
  311.4 4.6 copy-start.6
  313.7 23.0 %collective-permute-start.2 = (bf16[256,1536]{1,0:T(8,128)(2,1)}, bf16[256,1536]{1,0:T(8,128)(2,1)}, u32[]{:S(2)}, u32[]{:S(2)}) collective-permute-start(bf16[256,1536]{1,0:T(8,128)(2,1)} %convolution_convert_fusion.1), channel_id=1, source_target_pairs={{0,1},{1,0},{2,3},{3,2},{4,5},{5,4},{6,7},{7,6},{8,9},{9,8},{10,11... | collective-permute-start | bytes 2359304 | tf_op jit(solution)/shard_map/ppermute | solution.py:28
  328.0 3.7 copy-start.20
  330.6 19.8 %collective-permute-start = (bf16[256,1536]{1,0:T(8,128)(2,1)S(1)}, bf16[256,1536]{1,0:T(8,128)(2,1)S(1)}, u32[]{:S(2)}, u32[]{:S(2)}) collective-permute-start(bf16[256,1536]{1,0:T(8,128)(2,1)S(1)} %convolution_convert_fusion.3), channel_id=1, source_target_pairs={{0,1},{1,0},{2,3},{3,2},{4,5},{5,4},{6,7},{7,6},{8,9},{9,8},{10,11... | collective-permute-start | bytes 2359304 | tf_op jit(solution)/shard_map/ppermute | solution.py:28
  354.9 5.0 copy-start.8
  354.9 3.1 collective-permute-start.1
  356.5 3.4 collective-permute-start.3
  362.4 27.3 %collective-permute-start.4 = (bf16[512,3072]{1,0:T(8,128)(2,1)S(1)}, bf16[512,3072]{1,0:T(8,128)(2,1)S(1)}, u32[]{:S(2)}, u32[]{:S(2)}) collective-permute-start(bf16[512,3072]{1,0:T(8,128)(2,1)S(1)} %pad_maximum_fusion.1), channel_id=1, source_target_pairs={{0,2},{1,3},{4,6},{5,7},{8,10},{9,11},{12,14},{13,15},{16,18},{17,... | collective-permute-start | bytes 9437192 | tf_op jit(solution)/shard_map/ppermute | solution.py:18
  399.8 4.0 copy-start.5
  401.4 6.8 %copy-start.4 = (bf16[512,768]{1,0:T(8,128)(2,1)}, bf16[512,768]{1,0:T(8,128)(2,1)S(1)}, u32[]{:S(2)}) copy-start(bf16[512,768]{1,0:T(8,128)(2,1)S(1)} %convert_element_type.157) | copy-start | bytes 2359300
  401.4 2.4 collective-permute-start.5
  403.8 4.5 copy-start.7
  413.6 3.7 copy-start.13
  415.1 5.4 %collective-permute-start.6 = (f32[512,64]{0,1:T(8,128)S(1)}, f32[512,64]{0,1:T(8,128)S(1)}, u32[]{:S(2)}, u32[]{:S(2)}) collective-permute-start(f32[512,64]{0,1:T(8,128)S(1)} %fusion.73), channel_id=1, source_target_pairs={{0,1},{1,0},{2,3},{3,2},{4,5},{5,4},{6,7},{7,6},{8,9},{9,8},{10,11... | collective-permute-start | bytes 393224 | tf_op jit(solution)/shard_map/ppermute | solution.py:28
  432.2 10.2 %collective-permute-start.7 = (bf16[512,1536]{1,0:T(8,128)(2,1)}, bf16[512,1536]{1,0:T(8,128)(2,1)}, u32[]{:S(2)}, u32[]{:S(2)}) collective-permute-start(bf16[512,1536]{1,0:T(8,128)(2,1)} %multiply_convert_fusion), channel_id=1, source_target_pairs={{2,0},{3,1},{6,4},{7,5},{10,8},{11,9},{14,12},{15,13},{18,16},{19,... | collective-permute-start | bytes 4718600 | tf_op jit(solution)/shard_map/ppermute | solution.py:18
  448.2 80.9 %all-to-all-start = ((bf16[32,48,1536]{2,1,0:T(8,128)(2,1)}), bf16[32,48,1536]{2,1,0:T(8,128)(2,1)}, u32[]{:S(2)}, u32[]{:S(2)}) async-start(bf16[32,48,1536]{2,1,0:T(8,128)(2,1)} %bitcast.141), calls=%async_computation | async-start | bytes 9437184 | tf_op jit(solution)/shard_map/all_to_all | solution.py:233
  456.5 76.4 %copy-start.1 = (bf16[2,256,3072]{2,1,0:T(8,128)(2,1)S(1)}, bf16[2,256,3072]{2,1,0:T(8,128)(2,1)}, u32[]{:S(2)}) copy-start(bf16[2,256,3072]{2,1,0:T(8,128)(2,1)} %param.14) | copy-start | bytes 9437188
  (7 other events, 13.6 us)
Sparse Core Ops, SparseCore 0:
  12.6 259.6 all-gather.1

commit v6 on v5

--- a/solution.py
+++ b/solution.py
@@ -22,6 +22,52 @@
     mask = 2**bit
     pairs = [(source, source ^ mask) for source in range(lax.axis_size(axis))]
     return lax.ppermute(value, axis, pairs)
+
+
+CTL_SHAPE = (4, 2, 4)
+
+
+def ctl_coords(index):
+    _, count_z, count_x = CTL_SHAPE
+    return index // (count_z * count_x), (index // count_x) % count_z, index % count_x
+
+
+def ctl_shift(value, step_y, flip_z, step_x):
+    count_y, count_z, count_x = CTL_SHAPE
+    pairs = []
+    for source in range(count_y * count_z * count_x):
+        at_y, at_z, at_x = ctl_coords(source)
+        target = ((at_y + step_y) % count_y * count_z + (at_z ^ flip_z)) * count_x + (at_x + step_x) % count_x
+        pairs.append((source, target))
+    return lax.ppermute(value, "ctl", pairs)
+
+
+def ring_stage(block, along_y, position):
+    step = (1, 0) if along_y else (0, 1)
+    forward = lambda value: ctl_shift(value, step[0], 0, step[1])
+    backward = lambda value: ctl_shift(value, -step[0], 0, -step[1])
+    from_before = forward(block)
+    from_after = backward(block)
+    half = block.shape[0] // 2
+    far = jnp.concatenate([backward(from_after[:half]), forward(from_before[half:])], axis=0)
+    relative = jnp.stack([block, from_after, far, from_before])
+    return jnp.roll(relative, position, axis=0)
+
+
+def ctl_gather(piece):
+    at_y, at_z, at_x = ctl_coords(lax.axis_index("ctl"))
+    rows, width = piece.shape
+    paired = ctl_shift(piece, 0, 1, 0)
+    pair = jnp.where(at_z == 0, jnp.stack([piece, paired]), jnp.stack([paired, piece]))
+    split = width // 2
+    first = ring_stage(pair[..., :split], False, at_x)
+    first = ring_stage(jnp.swapaxes(first, 0, 1), True, at_y)
+    second = ring_stage(pair[..., split:], True, at_y)
+    second = ring_stage(second, False, at_x)
+    second = jnp.moveaxis(second, 0, 2)
+    return jnp.concatenate(
+        [first.reshape(-1, split), second.reshape(-1, width - split)], axis=1
+    )
 
 
 def swap(value, axis):
@@ -120,7 +166,7 @@
         ],
         axis=1,
     )
-    gathered = lax.all_gather(packed, "ctl", axis=0, tiled=True)
+    gathered = ctl_gather(packed)
     count_rows = gathered.shape[0]
     out_cols = gathered[:, 3 * local_heads : 4 * local_heads]
     projected = block_matmul(text_flat, gathered, 0, 3, local_heads)

time: 549 us -> 523 us (0.953)
  the two profiles are of different devices: /device:TPU:49 before, /device:TPU:5 now
where the time goes in v6:
time: 523 us; the launch traced here: 514 us
  waiting for transfers between devices  193 us (37%)
  local copies, waits for them, and re-layouts  109 us (21%)
  other arithmetic  97.6 us (19%)
  starting transfers between devices  46.3 us (9%)
  matrix products  31.8 us (6%)
  Pallas kernels  23.8 us (5%)
  blocking collectives  10.7 us (2%)
    ppermute x17, waiting for transfers between devices, ctl_shift(): return lax.ppermute(value, 'ctl', pairs)  76.1 us
    all_to_all x1, waiting for transfers between devices, local(): received = lax.all_to_all(group_parts, 'ctl', 0, 0, tiled=True)  71.9 us
    unnamed x90, local copies, waits for them, and re-layouts  32.4 us
    ppermute x2, waiting for transfers between devices, passed_along(): return lax.ppermute(shard, axis, pairs)  29 us
    pallas_call x2, Pallas kernels, block_matmul(): pl.pallas_call(kernel, grid=(block_count,), in_specs=[pl.BlockSpec((row_c...  23.8 us
    ppermute x17, starting transfers between devices, ctl_shift(): return lax.ppermute(value, 'ctl', pairs)  22.7 us
    unnamed x11, other arithmetic  22.1 us
    concatenate x1, other arithmetic, ctl_gather(): jnp.concatenate([first.reshape(-1, split), second.reshape(-1, width - spl...  20 us
  transfers between devices with their start and end apart: 26, of which 10 were waited for; matrix products, arithmetic and copies ran while one was open for 24% of the time, Pallas kernels for 0%

profile of v6, /device:TPU:5, one launch (start us, length us, event | category | flops | bytes accessed | tf_op | source)
XLA Modules:
  0.0 514.0 jit_solution(1112932608498236780)
XLA Ops:
  11.6 12.7 %collective-permute-done = bf16[96,3840]{1,0:T(8,128)(2,1)} collective-permute-done((bf16[96,3840]{1,0:T(8,128)(2,1)}, bf16[96,3840]{1,0:T(8,128)(2,1)}, u32[]{:S(2)}, u32[]{:S(2)}) %collective-permute-start) | collective-permute-done | bytes 737312 | tf_op jit(solution)/shard_map/ppermute | solution.py:42
  34.4 10.8 %collective-permute-done.1 = bf16[2,96,1920]{2,1,0:T(8,128)(2,1)} collective-permute-done((bf16[2,96,1920]{2,1,0:T(8,128)(2,1)}, bf16[2,96,1920]{2,1,0:T(8,128)(2,1)}, u32[]{:S(2)}, u32[]{:S(2)}) %collective-permute-start.1) | collective-permute-done | bytes 737312 | tf_op jit(solution)/shard_map/ppermute | solution.py:42
  51.0 14.7 %gather_fusion.1 = bf16[512,3072]{1,0:T(8,128)(2,1)} fusion(bf16[2,256,3072]{2,1,0:T(8,128)(2,1)S(1)} %copy-done, s32[512]{0:T(512)S(1)} %bitcast.178), kind=kCustom, calls=%fused_computation.1 | custom fusion | bytes 6295552 | tf_op jit(solution)/shard_map/vmap(jit(_take))/gather | solution.py:146
  71.8 6.6 %bitcast_dynamic-update-slice_fusion = (bf16[8,2,4,96,1920]{4,3,1,2,0:T(8,128)(2,1)}, bf16[4,2,96,1920]{3,2,1,0:T(8,128)(2,1)S(1)}) fusion(s32[]{:T(128)S(6)} %select_n.186, bf16[1,2,96,1920]{3,2,1,0:T(8,128)(2,1)} %bitcast.16, bf16[1,2,96,1920]{3,2,1,0:T(8,128)(2,1)S(1)} %maximum_bitcast_fusion.2, bf16[1,2,96,1920]{3,2,1,0:T(8,128)(2,1)} %bitcast.14, ...), kind=kLoop, calls=%fused_computation.61 | loop fusion | flops 23592960 | bytes 8847364
  81.6 7.3 %bitcast_dynamic-update-slice_fusion.6 = (bf16[8,4,2,96,1920]{4,3,2,1,0:T(8,128)(2,1)}, bf16[4,2,96,1920]{3,2,1,0:T(8,128)(2,1)}) fusion(s32[]{:T(128)S(6)} %select_n.170, bf16[1,2,96,1920]{3,2,1,0:T(8,128)(2,1)} %bitcast.26, bf16[1,2,96,1920]{3,2,1,0:T(8,128)(2,1)S(1)} %maximum_bitcast_fusion.3, bf16[1,2,96,1920]{3,2,1,0:T(8,128)(2,1)} %bitcast.24, ...), kind=kLoop, calls=%fused_computation.67 | loop fusion | flops 23592960 | bytes 8847364
  100.5 40.7 %collective-permute-done.5 = bf16[2,4,96,1920]{3,2,0,1:T(8,128)(2,1)S(1)} collective-permute-done((bf16[2,4,96,1920]{3,2,0,1:T(8,128)(2,1)S(1)}, bf16[2,4,96,1920]{3,2,0,1:T(8,128)(2,1)S(1)}, u32[]{:S(2)}, u32[]{:S(2)}) %collective-permute-start.5) | collective-permute-done | bytes 2949152 | tf_op jit(solution)/shard_map/ppermute | solution.py:42
  148.9 8.0 %fusion.2.rows_ref = bf16[768,3072]{1,0:T(8,128)(2,1)} fusion(f32[2,384,3072]{2,1,0:T(8,128)} %get-tuple-element.23, f32[2,3072]{1,0:T(2,128)S(1)} %get-tuple-element.38, f32[2,3072]{1,0:T(2,128)S(1)} %get-tuple-element.39, f32[768]{0:T(1024)S(1)} %rsqrt.47, f32[768]{0:T(1024)S(1)} %div.70), kind=kLoop, calls=%fused_computation.8 | loop fusion | flops 11796480 | bytes 14211072 | tf_op jit(solution)/shard_map/convert_element_type | solution.py:154
  168.2 5.9 %collective-permute-done.6 = bf16[1,4,96,1920]{3,2,0,1:T(8,128)(2,1)} collective-permute-done((bf16[1,4,96,1920]{3,2,0,1:T(8,128)(2,1)}, bf16[1,4,96,1920]{3,2,0,1:T(8,128)(2,1)}, u32[]{:S(2)}, u32[]{:S(2)}) %collective-permute-start.6) | collective-permute-done | bytes 1474592 | tf_op jit(solution)/shard_map/ppermute | solution.py:42
  174.1 6.0 %collective-permute-done.8 = bf16[1,4,96,1920]{3,2,0,1:T(8,128)(2,1)} collective-permute-done((bf16[1,4,96,1920]{3,2,0,1:T(8,128)(2,1)}, bf16[1,4,96,1920]{3,2,0,1:T(8,128)(2,1)}, u32[]{:S(2)}, u32[]{:S(2)}) %collective-permute-start.8) | collective-permute-done | bytes 1474592 | tf_op jit(solution)/shard_map/ppermute | solution.py:42
  195.8 7.9 %constant_dynamic-slice_fusion.3 = bf16[4,2,4,96,1920]{4,3,1,2,0:T(8,128)(2,1)S(1)} fusion(bf16[8,2,4,96,1920]{4,3,1,2,0:T(8,128)(2,1)} %bitcast_dynamic-update-slice_fusion.9, s32[]{:T(128)S(6)} %select_n.170), kind=kLoop, calls=%fused_computation.157 | loop fusion | bytes 23592964 | tf_op jit(solution)/shard_map/jit(_roll_dynamic)/dynamic_slice | solution.py:54
  203.7 6.0 %copy.26 = bf16[4,2,4,96,1920]{4,3,2,1,0:T(8,128)(2,1)} copy(bf16[4,2,4,96,1920]{4,3,1,2,0:T(8,128)(2,1)S(1)} %constant_dynamic-slice_fusion.3) | data formatting | bytes 23592960 | tf_op jit(solution)/shard_map/jit(_roll_dynamic)/dynamic_slice | solution.py:54
  227.7 20.0 %pad_maximum_fusion.weight_ref = bf16[3072,3840]{1,0:T(8,128)(2,1)} fusion(bf16[3072,1920]{1,0:T(8,128)(2,1)} %bitcast.175, bf16[3072,1920]{1,0:T(8,128)(2,1)} %bitcast.177), kind=kLoop, calls=%fused_computation.4 | loop fusion | flops 47185920 | bytes 47185920 | tf_op jit(solution)/shard_map/concatenate | solution.py:68
  247.7 16.7 %shard_map.140 = f32[768,2304]{1,0:T(8,128)} custom-call(bf16[768,3072]{1,0:T(8,128)(2,1)} %fusion.2.rows_ref, bf16[3072,3840]{1,0:T(8,128)(2,1)} %pad_maximum_fusion.weight_ref), custom_call_target="tpu_custom_call" | custom-call | flops 10871635968 | bytes 25952256 | tf_op jit(solution)/shard_map/pallas_call | solution.py:83
  283.1 5.3 %convolution_convert_fusion.5 = bf16[6,128,256]{2,1,0:T(8,128)(2,1)S(1)} fusion(f32[6,256]{1,0:T(8,128)S(1)} %fusion.95, f32[384,2,6,128]{0,3,2,1:T(8,128)S(1)} %bitcast.188, f32[6,256,384]{2,1,0:T(8,128)} %copy-done.20), kind=kOutput, calls=%fused_computation.106 | convolution fusion | flops 154142592 | bytes 5709824 | tf_op jit(solution)/shard_map/hij,jhd->ihd/dot_general | solution.py:195
  301.4 5.3 %convolution_convert_fusion.6 = bf16[6,128,256]{2,1,0:T(8,128)(2,1)S(1)} fusion(f32[6,256]{1,0:T(8,128)S(1)} %fusion.94, f32[384,2,6,128]{0,3,2,1:T(8,128)S(1)} %bitcast.185, f32[6,256,384]{2,1,0:T(8,128)} %copy-done.19), kind=kOutput, calls=%fused_computation.107 | convolution fusion | flops 154142592 | bytes 5709824 | tf_op jit(solution)/shard_map/hij,jhd->ihd/dot_general | solution.py:195
  314.7 10.9 %collective-permute-done.17 = bf16[256,1536]{1,0:T(8,128)(2,1)S(1)} collective-permute-done((bf16[256,1536]{1,0:T(8,128)(2,1)S(1)}, bf16[256,1536]{1,0:T(8,128)(2,1)S(1)}, u32[]{:S(2)}, u32[]{:S(2)}) %collective-permute-start.17) | collective-permute-done | bytes 786464 | tf_op jit(solution)/shard_map/ppermute | solution.py:74
  339.2 29.0 %collective-permute-done.21 = bf16[512,3072]{1,0:T(8,128)(2,1)S(1)} collective-permute-done((bf16[512,3072]{1,0:T(8,128)(2,1)S(1)}, bf16[512,3072]{1,0:T(8,128)(2,1)S(1)}, u32[]{:S(2)}, u32[]{:S(2)}) %collective-permute-start.21) | collective-permute-done | bytes 3145760 | tf_op jit(solution)/shard_map/ppermute | solution.py:18
  371.1 7.1 %shard_map.141 = f32[512,768]{1,0:T(8,128)} custom-call(bf16[512,3072]{1,0:T(8,128)(2,1)} %broadcast_select_fusion.rows_ref, bf16[3072,3840]{1,0:T(8,128)(2,1)} %pad_maximum_fusion.weight_ref), custom_call_target="tpu_custom_call" | custom-call | flops 2415919104 | bytes 9437184 | tf_op jit(solution)/shard_map/pallas_call | solution.py:83
  386.7 5.4 %all-reduce.1 = (f32[2,256,1]{1,0,2:T(2,128)S(1)}, f32[2,256,1]{1,0,2:T(2,128)S(1)}) all-reduce(f32[2,256,1]{1,0,2:T(2,128)S(1)} %broadcast_in_dim.53, f32[2,256,1]{1,0,2:T(2,128)S(1)} %broadcast_in_dim.52), channel_id=1, replica_groups=mesh['ctl'=32,'side'=2,'tp'=2] {'tp'}, use_global_device_ids=true, to_apply=%region_13.15 | all-reduce | flops 1024 | bytes 8192 | tf_op jit(solution)/shard_map/psum | solution.py:234
  401.8 5.3 %all-reduce = (f32[2,256,1]{1,0,2:T(2,128)S(1)}, f32[2,256,1]{1,0,2:T(2,128)S(1)}) all-reduce(f32[2,256,1]{1,0,2:T(2,128)S(1)} %broadcast_in_dim.55, f32[2,256,1]{1,0,2:T(2,128)S(1)} %broadcast_in_dim.54), channel_id=1, replica_groups=mesh['ctl'=32,'side'=2,'tp'=2] {'tp'}, use_global_device_ids=true, to_apply=%region_17.19 | all-reduce | flops 1024 | bytes 8192 | tf_op jit(solution)/shard_map/psum | solution.py:258
  410.9 6.7 %collective-permute-start.24 = (bf16[512,1536]{1,0:T(8,128)(2,1)}, bf16[512,1536]{1,0:T(8,128)(2,1)}, u32[]{:S(2)}, u32[]{:S(2)}) collective-permute-start(bf16[512,1536]{1,0:T(8,128)(2,1)} %multiply_convert_fusion), channel_id=1, source_target_pairs={{2,0},{3,1},{6,4},{7,5},{10,8},{11,9},{14,12},{15,13},{18,16},{19,... | collective-permute-start | bytes 4718600 | tf_op jit(solution)/shard_map/ppermute | solution.py:18
  420.9 5.8 %convolution_convert_fusion = bf16[1536,1536]{1,0:T(8,128)(2,1)} fusion(bf16[512,1536]{0,1:T(8,128)(2,1)S(1)} %bitcast.203, bf16[512,1536]{1,0:T(8,128)(2,1)} %collective-permute-done.24, bf16[512,1536]{1,0:T(8,128)(2,1)} %multiply_convert_fusion, pred[]{:T(512)S(6)} %eq.19), kind=kOutput, calls=%fused_computation.14 | convolution fusion | flops 2419064832 | bytes 9437185 | tf_op jit(solution)/shard_map/dot_general | solution.py:275
  426.7 6.5 %all-to-all-start = ((bf16[32,48,1536]{2,1,0:T(8,128)(2,1)}), bf16[32,48,1536]{2,1,0:T(8,128)(2,1)}, u32[]{:S(2)}, u32[]{:S(2)}) async-start(bf16[32,48,1536]{2,1,0:T(8,128)(2,1)} %bitcast.199), calls=%async_computation | async-start | bytes 9437184 | tf_op jit(solution)/shard_map/all_to_all | solution.py:279
  437.9 71.9 %all-to-all-done = bf16[32,48,1536]{2,1,0:T(8,128)(2,1)} async-done(((bf16[32,48,1536]{2,1,0:T(8,128)(2,1)}), bf16[32,48,1536]{2,1,0:T(8,128)(2,1)}, u32[]{:S(2)}, u32[]{:S(2)}) %all-to-all-start) | async-done | bytes 4718624 | tf_op jit(solution)/shard_map/all_to_all | solution.py:279
  (217 shorter events, 189.7 us)
Async XLA Ops:
  6.3 18.0 %collective-permute-start = (bf16[96,3840]{1,0:T(8,128)(2,1)}, bf16[96,3840]{1,0:T(8,128)(2,1)}, u32[]{:S(2)}, u32[]{:S(2)}) collective-permute-start(bf16[96,3840]{1,0:T(8,128)(2,1)} %get-tuple-element.36), channel_id=1, source_target_pairs={{0,16},{4,20},{8,24},{12,28},{16,0},{20,4},{24,8},{28,12},{32,48},... | collective-permute-start | bytes 2211848 | tf_op jit(solution)/shard_map/ppermute | solution.py:42
  28.3 17.0 %collective-permute-start.1 = (bf16[2,96,1920]{2,1,0:T(8,128)(2,1)}, bf16[2,96,1920]{2,1,0:T(8,128)(2,1)}, u32[]{:S(2)}, u32[]{:S(2)}) collective-permute-start(bf16[2,96,1920]{2,1,0:T(8,128)(2,1)} %get-tuple-element.34), channel_id=1, source_target_pairs={{0,12},{4,0},{8,4},{12,8},{16,28},{20,16},{24,20},{28,24},{32,44},... | collective-permute-start | bytes 2211848 | tf_op jit(solution)/shard_map/ppermute | solution.py:42
  28.5 18.8 %collective-permute-start.3 = (bf16[2,96,1920]{2,1,0:T(8,128)(2,1)}, bf16[2,96,1920]{2,1,0:T(8,128)(2,1)}, u32[]{:S(2)}, u32[]{:S(2)}) collective-permute-start(bf16[2,96,1920]{2,1,0:T(8,128)(2,1)} %get-tuple-element.34), channel_id=1, source_target_pairs={{0,4},{4,8},{8,12},{12,0},{16,20},{20,24},{24,28},{28,16},{32,36},... | collective-permute-start | bytes 2211848 | tf_op jit(solution)/shard_map/ppermute | solution.py:42
  29.7 36.0 %collective-permute-start.9 = (bf16[2,96,1920]{2,1,0:T(8,128)(2,1)}, bf16[2,96,1920]{2,1,0:T(8,128)(2,1)}, u32[]{:S(2)}, u32[]{:S(2)}) collective-permute-start(bf16[2,96,1920]{2,1,0:T(8,128)(2,1)} %get-tuple-element.33), channel_id=1, source_target_pairs={{0,96},{4,100},{8,104},{12,108},{16,112},{20,116},{24,120},{28,124... | collective-permute-start | bytes 2211848 | tf_op jit(solution)/shard_map/ppermute | solution.py:42
  32.5 37.2 %collective-permute-start.11 = (bf16[2,96,1920]{2,1,0:T(8,128)(2,1)}, bf16[2,96,1920]{2,1,0:T(8,128)(2,1)}, u32[]{:S(2)}, u32[]{:S(2)}) collective-permute-start(bf16[2,96,1920]{2,1,0:T(8,128)(2,1)} %get-tuple-element.33), channel_id=1, source_target_pairs={{0,32},{4,36},{8,40},{12,44},{16,48},{20,52},{24,56},{28,60},{32,6... | collective-permute-start | bytes 2211848 | tf_op jit(solution)/shard_map/ppermute | solution.py:42
  47.0 23.7 %collective-permute-start.2 = (bf16[1,96,1920]{2,1,0:T(8,128)(2,1)}, bf16[1,96,1920]{2,1,0:T(8,128)(2,1)S(1)}, u32[]{:S(2)}, u32[]{:S(2)}) collective-permute-start(bf16[1,96,1920]{2,1,0:T(8,128)(2,1)} %slice.141), channel_id=1, source_target_pairs={{0,12},{4,0},{8,4},{12,8},{16,28},{20,16},{24,20},{28,24},{32,44},... | collective-permute-start | bytes 1105928 | tf_op jit(solution)/shard_map/ppermute | solution.py:42
  49.0 21.7 %collective-permute-start.4 = (bf16[1,96,1920]{2,1,0:T(8,128)(2,1)}, bf16[1,96,1920]{2,1,0:T(8,128)(2,1)}, u32[]{:S(2)}, u32[]{:S(2)}) collective-permute-start(bf16[1,96,1920]{2,1,0:T(8,128)(2,1)} %slice.142), channel_id=1, source_target_pairs={{0,4},{4,8},{8,12},{12,0},{16,20},{20,24},{24,28},{28,16},{32,36},... | collective-permute-start | bytes 1105928 | tf_op jit(solution)/shard_map/ppermute | solution.py:42
  66.8 14.7 %collective-permute-start.10 = (bf16[1,96,1920]{2,1,0:T(8,128)(2,1)S(1)}, bf16[1,96,1920]{2,1,0:T(8,128)(2,1)S(1)}, u32[]{:S(2)}, u32[]{:S(2)}) collective-permute-start(bf16[1,96,1920]{2,1,0:T(8,128)(2,1)S(1)} %slice.146), channel_id=1, source_target_pairs={{0,96},{4,100},{8,104},{12,108},{16,112},{20,116},{24,120},{28,124... | collective-permute-start | bytes 1105928 | tf_op jit(solution)/shard_map/ppermute | solution.py:42
  70.6 10.9 %collective-permute-start.12 = (bf16[1,96,1920]{2,1,0:T(8,128)(2,1)S(1)}, bf16[1,96,1920]{2,1,0:T(8,128)(2,1)S(1)}, u32[]{:S(2)}, u32[]{:S(2)}) collective-permute-start(bf16[1,96,1920]{2,1,0:T(8,128)(2,1)S(1)} %slice.147), channel_id=1, source_target_pairs={{0,32},{4,36},{8,40},{12,44},{16,48},{20,52},{24,56},{28,60},{32,6... | collective-permute-start | bytes 1105928 | tf_op jit(solution)/shard_map/ppermute | solution.py:42
  78.4 62.8 %collective-permute-start.5 = (bf16[2,4,96,1920]{3,2,0,1:T(8,128)(2,1)S(1)}, bf16[2,4,96,1920]{3,2,0,1:T(8,128)(2,1)S(1)}, u32[]{:S(2)}, u32[]{:S(2)}) collective-permute-start(bf16[2,4,96,1920]{3,2,0,1:T(8,128)(2,1)S(1)} %bitcast.181), channel_id=1, source_target_pairs={{0,96},{4,100},{8,104},{12,108},{16,112},{20,116},{24,120},{28,124... | collective-permute-start | bytes 8847368 | tf_op jit(solution)/shard_map/ppermute | solution.py:42
  81.0 65.0 %collective-permute-start.7 = (bf16[2,4,96,1920]{3,2,0,1:T(8,128)(2,1)S(1)}, bf16[2,4,96,1920]{3,2,0,1:T(8,128)(2,1)S(1)}, u32[]{:S(2)}, u32[]{:S(2)}) collective-permute-start(bf16[2,4,96,1920]{3,2,0,1:T(8,128)(2,1)S(1)} %bitcast.182), channel_id=1, source_target_pairs={{0,32},{4,36},{8,40},{12,44},{16,48},{20,52},{24,56},{28,60},{32,6... | collective-permute-start | bytes 8847368 | tf_op jit(solution)/shard_map/ppermute | solution.py:42
  89.0 68.0 %collective-permute-start.13 = (bf16[4,2,96,1920]{3,2,1,0:T(8,128)(2,1)}, bf16[4,2,96,1920]{3,2,1,0:T(8,128)(2,1)}, u32[]{:S(2)}, u32[]{:S(2)}) collective-permute-start(bf16[4,2,96,1920]{3,2,1,0:T(8,128)(2,1)} %get-tuple-element.21), channel_id=1, source_target_pairs={{0,12},{4,0},{8,4},{12,8},{16,28},{20,16},{24,20},{28,24},{32,44},... | collective-permute-start | bytes 8847368 | tf_op jit(solution)/shard_map/ppermute | solution.py:42
  89.0 69.7 %collective-permute-start.15 = (bf16[4,2,96,1920]{3,2,1,0:T(8,128)(2,1)}, bf16[4,2,96,1920]{3,2,1,0:T(8,128)(2,1)}, u32[]{:S(2)}, u32[]{:S(2)}) collective-permute-start(bf16[4,2,96,1920]{3,2,1,0:T(8,128)(2,1)} %get-tuple-element.21), channel_id=1, source_target_pairs={{0,4},{4,8},{8,12},{12,0},{16,20},{20,24},{24,28},{28,16},{32,36},... | collective-permute-start | bytes 8847368 | tf_op jit(solution)/shard_map/ppermute | solution.py:42
  142.6 31.5 %collective-permute-start.6 = (bf16[1,4,96,1920]{3,2,0,1:T(8,128)(2,1)}, bf16[1,4,96,1920]{3,2,0,1:T(8,128)(2,1)}, u32[]{:S(2)}, u32[]{:S(2)}) collective-permute-start(bf16[1,4,96,1920]{3,2,0,1:T(8,128)(2,1)} %slice.143), channel_id=1, source_target_pairs={{0,96},{4,100},{8,104},{12,108},{16,112},{20,116},{24,120},{28,124... | collective-permute-start | bytes 4423688 | tf_op jit(solution)/shard_map/ppermute | solution.py:42
  148.9 31.2 %collective-permute-start.8 = (bf16[1,4,96,1920]{3,2,0,1:T(8,128)(2,1)}, bf16[1,4,96,1920]{3,2,0,1:T(8,128)(2,1)}, u32[]{:S(2)}, u32[]{:S(2)}) collective-permute-start(bf16[1,4,96,1920]{3,2,0,1:T(8,128)(2,1)} %slice.144), channel_id=1, source_target_pairs={{0,32},{4,36},{8,40},{12,44},{16,48},{20,52},{24,56},{28,60},{32,6... | collective-permute-start | bytes 4423688 | tf_op jit(solution)/shard_map/ppermute | solution.py:42
  158.6 51.2 %collective-permute-start.14 = (bf16[2,2,96,1920]{3,2,1,0:T(8,128)(2,1)S(1)}, bf16[2,2,96,1920]{3,2,1,0:T(8,128)(2,1)S(1)}, u32[]{:S(2)}, u32[]{:S(2)}) collective-permute-start(bf16[2,2,96,1920]{3,2,1,0:T(8,128)(2,1)S(1)} %slice.148), channel_id=1, source_target_pairs={{0,12},{4,0},{8,4},{12,8},{16,28},{20,16},{24,20},{28,24},{32,44},... | collective-permute-start | bytes 4423688 | tf_op jit(solution)/shard_map/ppermute | solution.py:42
  160.2 49.6 %collective-permute-start.16 = (bf16[2,2,96,1920]{3,2,1,0:T(8,128)(2,1)S(1)}, bf16[2,2,96,1920]{3,2,1,0:T(8,128)(2,1)S(1)}, u32[]{:S(2)}, u32[]{:S(2)}) collective-permute-start(bf16[2,2,96,1920]{3,2,1,0:T(8,128)(2,1)S(1)} %slice.149), channel_id=1, source_target_pairs={{0,4},{4,8},{8,12},{12,0},{16,20},{20,24},{24,28},{28,16},{32,36},... | collective-permute-start | bytes 4423688 | tf_op jit(solution)/shard_map/ppermute | solution.py:42
  291.9 22.7 %collective-permute-start.19 = (bf16[256,1536]{1,0:T(8,128)(2,1)}, bf16[256,1536]{1,0:T(8,128)(2,1)}, u32[]{:S(2)}, u32[]{:S(2)}) collective-permute-start(bf16[256,1536]{1,0:T(8,128)(2,1)} %convolution_convert_fusion.1), channel_id=1, source_target_pairs={{0,1},{1,0},{2,3},{3,2},{4,5},{5,4},{6,7},{7,6},{8,9},{9,8},{10,11... | collective-permute-start | bytes 2359304 | tf_op jit(solution)/shard_map/ppermute | solution.py:74
  309.2 16.3 %collective-permute-start.17 = (bf16[256,1536]{1,0:T(8,128)(2,1)S(1)}, bf16[256,1536]{1,0:T(8,128)(2,1)S(1)}, u32[]{:S(2)}, u32[]{:S(2)}) collective-permute-start(bf16[256,1536]{1,0:T(8,128)(2,1)S(1)} %convolution_convert_fusion.3), channel_id=1, source_target_pairs={{0,1},{1,0},{2,3},{3,2},{4,5},{5,4},{6,7},{7,6},{8,9},{9,8},{10,11... | collective-permute-start | bytes 2359304 | tf_op jit(solution)/shard_map/ppermute | solution.py:74
  331.6 3.4 collective-permute-start.20
  337.7 30.6 %collective-permute-start.21 = (bf16[512,3072]{1,0:T(8,128)(2,1)S(1)}, bf16[512,3072]{1,0:T(8,128)(2,1)S(1)}, u32[]{:S(2)}, u32[]{:S(2)}) collective-permute-start(bf16[512,3072]{1,0:T(8,128)(2,1)S(1)} %pad_maximum_fusion.2), channel_id=1, source_target_pairs={{0,2},{1,3},{4,6},{5,7},{8,10},{9,11},{12,14},{13,15},{16,18},{17,... | collective-permute-start | bytes 9437192 | tf_op jit(solution)/shard_map/ppermute | solution.py:18
  393.7 5.4 %collective-permute-start.23 = (f32[512,64]{0,1:T(8,128)S(1)}, f32[512,64]{0,1:T(8,128)S(1)}, u32[]{:S(2)}, u32[]{:S(2)}) collective-permute-start(f32[512,64]{0,1:T(8,128)S(1)} %fusion.96), channel_id=1, source_target_pairs={{0,1},{1,0},{2,3},{3,2},{4,5},{5,4},{6,7},{7,6},{8,9},{9,8},{10,11... | collective-permute-start | bytes 393224 | tf_op jit(solution)/shard_map/ppermute | solution.py:74
  410.9 10.0 %collective-permute-start.24 = (bf16[512,1536]{1,0:T(8,128)(2,1)}, bf16[512,1536]{1,0:T(8,128)(2,1)}, u32[]{:S(2)}, u32[]{:S(2)}) collective-permute-start(bf16[512,1536]{1,0:T(8,128)(2,1)} %multiply_convert_fusion), channel_id=1, source_target_pairs={{2,0},{3,1},{6,4},{7,5},{10,8},{11,9},{14,12},{15,13},{18,16},{19,... | collective-permute-start | bytes 4718600 | tf_op jit(solution)/shard_map/ppermute | solution.py:18
  426.7 83.1 %all-to-all-start = ((bf16[32,48,1536]{2,1,0:T(8,128)(2,1)}), bf16[32,48,1536]{2,1,0:T(8,128)(2,1)}, u32[]{:S(2)}, u32[]{:S(2)}) async-start(bf16[32,48,1536]{2,1,0:T(8,128)(2,1)} %bitcast.199), calls=%async_computation | async-start | bytes 9437184 | tf_op jit(solution)/shard_map/all_to_all | solution.py:279
  (38 other events, 395.1 us)

commit v7 on v6

--- a/solution.py
+++ b/solution.py
@@ -65,9 +65,7 @@
     second = ring_stage(pair[..., split:], True, at_y)
     second = ring_stage(second, False, at_x)
     second = jnp.moveaxis(second, 0, 2)
-    return jnp.concatenate(
-        [first.reshape(-1, split), second.reshape(-1, width - split)], axis=1
-    )
+    return first.reshape(-1, split), second.reshape(-1, width - split)
 
 
 def swap(value, axis):
@@ -166,13 +164,23 @@
         ],
         axis=1,
     )
-    gathered = ctl_gather(packed)
-    count_rows = gathered.shape[0]
-    out_cols = gathered[:, 3 * local_heads : 4 * local_heads]
-    projected = block_matmul(text_flat, gathered, 0, 3, local_heads)
-    projected = projected.reshape(micro_count, seq_rows, 3 * local_heads)
+    front, back = ctl_gather(packed)
+    count_rows = front.shape[0]
+    narrow = local_heads // 2
+    front_blocks = front.shape[1] // narrow
+    out_cols = back[:, narrow : narrow + local_heads]
+    projected = block_matmul(text_flat, front, 0, front_blocks, narrow)
+    value_rest = block_matmul(text_flat, back, 0, 1, narrow)
+    projected = projected.reshape(micro_count, seq_rows, front_blocks * narrow)
     query_acc = projected[:, text_rows:, :local_heads]
-    pair_acc = projected[:, :, local_heads:]
+    key_acc = projected[:, :, local_heads : 2 * local_heads]
+    value_acc = jnp.concatenate(
+        [
+            projected[:, :, 2 * local_heads :],
+            value_rest.reshape(micro_count, seq_rows, narrow),
+        ],
+        axis=2,
+    )
     gain_pair = qk_gain[0]
     contract_last = (((1,), (1,)), ((), ()))
     other_out = lax.dynamic_slice_in_dim(out_cols, (1 - tp_index) * half_width, half_width, 0)
@@ -185,9 +193,10 @@
         queries = head_norm(
             query_acc[sample].reshape(img_rows, head_count, HEAD_DIM), gain_pair[0]
         )
-        pair_one = pair_acc[sample].reshape(seq_rows, 2, head_count, HEAD_DIM)
-        keys_all = head_norm(pair_one[:, 0], gain_pair[1])
-        values_all = pair_one[:, 1].astype(jnp.bfloat16)
+        keys_all = head_norm(
+            key_acc[sample].reshape(seq_rows, head_count, HEAD_DIM), gain_pair[1]
+        )
+        values_all = value_acc[sample].reshape(seq_rows, head_count, HEAD_DIM).astype(jnp.bfloat16)
         scores = jnp.einsum(
             "ihd,jhd->hij", queries, keys_all, preferred_element_type=jnp.float32
         ) / math.sqrt(HEAD_DIM)
@@ -219,7 +228,7 @@
     act_narrow = jnp.concatenate(act_rows, axis=0)
     act_other = passed_along(act_narrow, "side", 1)
     control_rows = jnp.where(is_control, act_narrow, act_other)
-    own_part = block_matmul(control_rows, gathered, 4, 1, local_heads)
+    own_part = block_matmul(control_rows, back, 3, 2, narrow)
     own_narrow = own_part.astype(jnp.bfloat16)
     other_narrow = partner(own_narrow, "side", 0)
     residual_narrow = jnp.where(

time: 523 us -> 519 us (level)
  other arithmetic: 97.6 us -> 83.8 us
  Pallas kernels: 23.8 us -> 31 us
    concatenate x1 -> x0, other arithmetic: 20 us -> none  [ctl_gather(): jnp.concatenate([first.reshape(-1, split), second.reshape(-1, width - spl...]
    pallas_call x2 -> x3, Pallas kernels: 23.8 us -> 31 us  [block_matmul(): pl.pallas_call(kernel, grid=(block_count,), in_specs=[pl.BlockSpec((row_c...]
    unnamed x11 -> x10, other arithmetic: 22.1 us -> 28.3 us
    slice x4 -> x6, local copies, waits for them, and re-layouts: 13.8 us -> 11.3 us  [the longest x1 4.77 us: local(): out_cols = back[:, narrow:narrow + local_heads]]
    unnamed x90 -> x94, local copies, waits for them, and re-layouts: 32.4 us -> 32.8 us
  transfers between devices with their start and end apart: 26 -> 26, of which waited for: 10 -> 10; matrix products, arithmetic and copies ran while one was open for 24% -> 25% of each run, Pallas kernels for 0% -> 3%
where the time goes in v7:
time: 519 us; the launch traced here: 510 us
  waiting for transfers between devices  192 us (37%)
  local copies, waits for them, and re-layouts  113 us (22%)
  other arithmetic  83.8 us (16%)
  starting transfers between devices  46.7 us (9%)
  matrix products  31.6 us (6%)
  Pallas kernels  31 us (6%)
  blocking collectives  10.7 us (2%)
    ppermute x17, waiting for transfers between devices, ctl_shift(): return lax.ppermute(value, 'ctl', pairs)  74.4 us
    all_to_all x1, waiting for transfers between devices, local(): received = lax.all_to_all(group_parts, 'ctl', 0, 0, tiled=True)  70.9 us
    unnamed x94, local copies, waits for them, and re-layouts  32.8 us
    pallas_call x3, Pallas kernels, block_matmul(): pl.pallas_call(kernel, grid=(block_count,), in_specs=[pl.BlockSpec((row_c...  31 us
    ppermute x2, waiting for transfers between devices, passed_along(): return lax.ppermute(shard, axis, pairs)  28.7 us
    unnamed x10, other arithmetic  28.3 us
    ppermute x17, starting transfers between devices, ctl_shift(): return lax.ppermute(value, 'ctl', pairs)  22.6 us
    ppermute x3, waiting for transfers between devices, swap(): return lax.ppermute(value, axis, [(0, 1), (1, 0)])  15.6 us
  transfers between devices with their start and end apart: 26, of which 10 were waited for; matrix products, arithmetic and copies ran while one was open for 25% of the time, Pallas kernels for 3%

profile of v7, /device:TPU:5, one launch (start us, length us, event | category | flops | bytes accessed | tf_op | source)
XLA Modules:
  0.0 510.1 jit_solution(10768099219338420693)
XLA Ops:
  11.6 12.7 %collective-permute-done = bf16[96,3840]{1,0:T(8,128)(2,1)} collective-permute-done((bf16[96,3840]{1,0:T(8,128)(2,1)}, bf16[96,3840]{1,0:T(8,128)(2,1)}, u32[]{:S(2)}, u32[]{:S(2)}) %collective-permute-start) | collective-permute-done | bytes 737312 | tf_op jit(solution)/shard_map/ppermute | solution.py:42
  34.3 10.9 %collective-permute-done.1 = bf16[2,96,1920]{2,1,0:T(8,128)(2,1)} collective-permute-done((bf16[2,96,1920]{2,1,0:T(8,128)(2,1)}, bf16[2,96,1920]{2,1,0:T(8,128)(2,1)}, u32[]{:S(2)}, u32[]{:S(2)}) %collective-permute-start.1) | collective-permute-done | bytes 737312 | tf_op jit(solution)/shard_map/ppermute | solution.py:42
  50.9 14.7 %gather_fusion.1 = bf16[512,3072]{1,0:T(8,128)(2,1)} fusion(bf16[2,256,3072]{2,1,0:T(8,128)(2,1)S(1)} %copy-done, s32[512]{0:T(512)S(1)} %bitcast.163), kind=kCustom, calls=%fused_computation.1 | custom fusion | bytes 6295552 | tf_op jit(solution)/shard_map/vmap(jit(_take))/gather | solution.py:144
  71.7 6.5 %bitcast_dynamic-update-slice_fusion = (bf16[8,2,4,96,1920]{4,3,1,2,0:T(8,128)(2,1)}, bf16[4,2,96,1920]{3,2,1,0:T(8,128)(2,1)S(1)}) fusion(s32[]{:T(128)S(6)} %select_n.186, bf16[1,2,96,1920]{3,2,1,0:T(8,128)(2,1)} %bitcast.16, bf16[1,2,96,1920]{3,2,1,0:T(8,128)(2,1)S(1)} %maximum_bitcast_fusion.2, bf16[1,2,96,1920]{3,2,1,0:T(8,128)(2,1)} %bitcast.14, ...), kind=kLoop, calls=%fused_computation.60 | loop fusion | flops 23592960 | bytes 8847364
  81.5 7.2 %bitcast_dynamic-update-slice_fusion.6 = (bf16[8,4,2,96,1920]{4,3,2,1,0:T(8,128)(2,1)}, bf16[4,2,96,1920]{3,2,1,0:T(8,128)(2,1)}) fusion(s32[]{:T(128)S(6)} %select_n.170, bf16[1,2,96,1920]{3,2,1,0:T(8,128)(2,1)} %bitcast.27, bf16[1,2,96,1920]{3,2,1,0:T(8,128)(2,1)S(1)} %maximum_bitcast_fusion.3, bf16[1,2,96,1920]{3,2,1,0:T(8,128)(2,1)} %bitcast.25, ...), kind=kLoop, calls=%fused_computation.66 | loop fusion | flops 23592960 | bytes 8847364
  100.1 41.0 %collective-permute-done.5 = bf16[2,4,96,1920]{3,2,0,1:T(8,128)(2,1)S(1)} collective-permute-done((bf16[2,4,96,1920]{3,2,0,1:T(8,128)(2,1)S(1)}, bf16[2,4,96,1920]{3,2,0,1:T(8,128)(2,1)S(1)}, u32[]{:S(2)}, u32[]{:S(2)}) %collective-permute-start.5) | collective-permute-done | bytes 2949152 | tf_op jit(solution)/shard_map/ppermute | solution.py:42
  148.8 8.0 %fusion.2.rows_ref = bf16[768,3072]{1,0:T(8,128)(2,1)} fusion(f32[2,384,3072]{2,1,0:T(8,128)} %get-tuple-element.23, f32[2,3072]{1,0:T(2,128)S(1)} %get-tuple-element.40, f32[2,3072]{1,0:T(2,128)S(1)} %get-tuple-element.41, f32[768]{0:T(1024)S(1)} %rsqrt.47, f32[768]{0:T(1024)S(1)} %div.70), kind=kLoop, calls=%fused_computation.7 | loop fusion | flops 11796480 | bytes 14211072 | tf_op jit(solution)/shard_map/convert_element_type | solution.py:152
  173.9 6.1 %collective-permute-done.8 = bf16[1,4,96,1920]{3,2,0,1:T(8,128)(2,1)} collective-permute-done((bf16[1,4,96,1920]{3,2,0,1:T(8,128)(2,1)}, bf16[1,4,96,1920]{3,2,0,1:T(8,128)(2,1)}, u32[]{:S(2)}, u32[]{:S(2)}) %collective-permute-start.8) | collective-permute-done | bytes 1474592 | tf_op jit(solution)/shard_map/ppermute | solution.py:42
  195.7 6.3 %constant_dynamic-slice_fusion.3 = bf16[4,2,4,96,1920]{4,3,1,2,0:T(8,128)(2,1)S(1)} fusion(bf16[8,2,4,96,1920]{4,3,1,2,0:T(8,128)(2,1)} %bitcast_dynamic-update-slice_fusion.9, s32[]{:T(128)S(6)} %select_n.170), kind=kLoop, calls=%fused_computation.151 | loop fusion | bytes 23592964 | tf_op jit(solution)/shard_map/jit(_roll_dynamic)/dynamic_slice | solution.py:54
  202.0 5.2 %copy.24 = bf16[4,2,4,96,1920]{4,3,2,1,0:T(8,128)(2,1)} copy(bf16[4,2,4,96,1920]{4,3,1,2,0:T(8,128)(2,1)S(1)} %constant_dynamic-slice_fusion.3) | data formatting | bytes 23592960 | tf_op jit(solution)/shard_map/jit(_roll_dynamic)/dynamic_slice | solution.py:54
  207.2 17.1 %shard_map.140 = f32[768,1920]{1,0:T(8,128)} custom-call(bf16[768,3072]{1,0:T(8,128)(2,1)} %fusion.2.rows_ref, bf16[3072,1920]{1,0:T(8,128)(2,1)} %bitcast.166), custom_call_target="tpu_custom_call" | custom-call | flops 9059696640 | bytes 22413312 | tf_op jit(solution)/shard_map/pallas_call | solution.py:81
  253.5 6.1 %dynamic-slice_bitcast_fusion = bf16[4,2,4,96,1920]{4,3,1,0,2:T(8,128)(2,1)S(1)} fusion(bf16[8,4,2,96,1920]{4,3,2,1,0:T(8,128)(2,1)} %bitcast_dynamic-update-slice_fusion.3, s32[]{:T(128)S(6)} %select_n.186), kind=kLoop, calls=%fused_computation.4 | loop fusion | bytes 23592964 | tf_op jit(solution)/shard_map/transpose | solution.py:67
  264.9 6.7 %shard_map.141 = f32[768,384]{1,0:T(8,128)} custom-call(bf16[768,3072]{1,0:T(8,128)(2,1)} %fusion.2.rows_ref, bf16[3072,1920]{1,0:T(8,128)(2,1)} %bitcast.160), custom_call_target="tpu_custom_call" | custom-call | flops 1811939328 | bytes 8257536 | tf_op jit(solution)/shard_map/pallas_call | solution.py:81
  280.0 5.3 %convolution_convert_fusion.5 = bf16[6,128,256]{2,1,0:T(8,128)(2,1)S(1)} fusion(bf16[384,6,128]{0,2,1:T(8,128)(2,1)S(1)} %bitcast.188, f32[6,256]{1,0:T(8,128)S(1)} %fusion.92, f32[6,256,384]{2,1,0:T(8,128)} %copy-done.22), kind=kOutput, calls=%fused_computation.106 | convolution fusion | flops 154142592 | bytes 3348480 | tf_op jit(solution)/shard_map/hij,jhd->ihd/dot_general | solution.py:204
  295.9 5.3 %convolution_convert_fusion.6 = bf16[6,128,256]{2,1,0:T(8,128)(2,1)S(1)} fusion(bf16[384,6,128]{0,2,1:T(8,128)(2,1)S(1)} %bitcast.189, f32[6,256]{1,0:T(8,128)S(1)} %fusion.91, f32[6,256,384]{2,1,0:T(8,128)} %copy-done.23), kind=kOutput, calls=%fused_computation.107 | convolution fusion | flops 154142592 | bytes 3348480 | tf_op jit(solution)/shard_map/hij,jhd->ihd/dot_general | solution.py:204
  309.8 13.0 %collective-permute-done.17 = bf16[256,1536]{1,0:T(8,128)(2,1)S(1)} collective-permute-done((bf16[256,1536]{1,0:T(8,128)(2,1)S(1)}, bf16[256,1536]{1,0:T(8,128)(2,1)S(1)}, u32[]{:S(2)}, u32[]{:S(2)}) %collective-permute-start.17) | collective-permute-done | bytes 786464 | tf_op jit(solution)/shard_map/ppermute | solution.py:72
  336.5 28.7 %collective-permute-done.21 = bf16[512,3072]{1,0:T(8,128)(2,1)S(1)} collective-permute-done((bf16[512,3072]{1,0:T(8,128)(2,1)S(1)}, bf16[512,3072]{1,0:T(8,128)(2,1)S(1)}, u32[]{:S(2)}, u32[]{:S(2)}) %collective-permute-start.21) | collective-permute-done | bytes 3145760 | tf_op jit(solution)/shard_map/ppermute | solution.py:18
  368.1 7.1 %shard_map.142 = f32[512,768]{1,0:T(8,128)} custom-call(bf16[512,3072]{1,0:T(8,128)(2,1)} %broadcast_select_fusion.rows_ref, bf16[3072,1920]{1,0:T(8,128)(2,1)} %bitcast.162), custom_call_target="tpu_custom_call" | custom-call | flops 2415919104 | bytes 9437184 | tf_op jit(solution)/shard_map/pallas_call | solution.py:81
  384.0 5.4 %all-reduce.1 = (f32[2,256,1]{1,0,2:T(2,128)S(1)}, f32[2,256,1]{1,0,2:T(2,128)S(1)}) all-reduce(f32[2,256,1]{1,0,2:T(2,128)S(1)} %broadcast_in_dim.53, f32[2,256,1]{1,0,2:T(2,128)S(1)} %broadcast_in_dim.52), channel_id=1, replica_groups=mesh['ctl'=32,'side'=2,'tp'=2] {'tp'}, use_global_device_ids=true, to_apply=%region_13.15 | all-reduce | flops 1024 | bytes 8192 | tf_op jit(solution)/shard_map/psum | solution.py:243
  398.9 5.3 %all-reduce = (f32[2,256,1]{1,0,2:T(2,128)S(1)}, f32[2,256,1]{1,0,2:T(2,128)S(1)}) all-reduce(f32[2,256,1]{1,0,2:T(2,128)S(1)} %broadcast_in_dim.55, f32[2,256,1]{1,0,2:T(2,128)S(1)} %broadcast_in_dim.54), channel_id=1, replica_groups=mesh['ctl'=32,'side'=2,'tp'=2] {'tp'}, use_global_device_ids=true, to_apply=%region_17.19 | all-reduce | flops 1024 | bytes 8192 | tf_op jit(solution)/shard_map/psum | solution.py:267
  408.0 6.7 %collective-permute-start.24 = (bf16[512,1536]{1,0:T(8,128)(2,1)}, bf16[512,1536]{1,0:T(8,128)(2,1)}, u32[]{:S(2)}, u32[]{:S(2)}) collective-permute-start(bf16[512,1536]{1,0:T(8,128)(2,1)} %multiply_convert_fusion), channel_id=1, source_target_pairs={{2,0},{3,1},{6,4},{7,5},{10,8},{11,9},{14,12},{15,13},{18,16},{19,... | collective-permute-start | bytes 4718600 | tf_op jit(solution)/shard_map/ppermute | solution.py:18
  418.0 5.7 %convolution_convert_fusion = bf16[1536,1536]{1,0:T(8,128)(2,1)} fusion(bf16[512,1536]{0,1:T(8,128)(2,1)S(1)} %bitcast.187, bf16[512,1536]{1,0:T(8,128)(2,1)} %collective-permute-done.24, bf16[512,1536]{1,0:T(8,128)(2,1)} %multiply_convert_fusion, pred[]{:T(512)S(6)} %eq.19), kind=kOutput, calls=%fused_computation.13 | convolution fusion | flops 2419064832 | bytes 9437185 | tf_op jit(solution)/shard_map/dot_general | solution.py:284
  423.8 6.5 %all-to-all-start = ((bf16[32,48,1536]{2,1,0:T(8,128)(2,1)}), bf16[32,48,1536]{2,1,0:T(8,128)(2,1)}, u32[]{:S(2)}, u32[]{:S(2)}) async-start(bf16[32,48,1536]{2,1,0:T(8,128)(2,1)} %bitcast.180), calls=%async_computation | async-start | bytes 9437184 | tf_op jit(solution)/shard_map/all_to_all | solution.py:288
  435.0 70.9 %all-to-all-done = bf16[32,48,1536]{2,1,0:T(8,128)(2,1)} async-done(((bf16[32,48,1536]{2,1,0:T(8,128)(2,1)}), bf16[32,48,1536]{2,1,0:T(8,128)(2,1)}, u32[]{:S(2)}, u32[]{:S(2)}) %all-to-all-start) | async-done | bytes 4718624 | tf_op jit(solution)/shard_map/all_to_all | solution.py:288
  (223 shorter events, 199.8 us)
Async XLA Ops:
  6.3 18.0 %collective-permute-start = (bf16[96,3840]{1,0:T(8,128)(2,1)}, bf16[96,3840]{1,0:T(8,128)(2,1)}, u32[]{:S(2)}, u32[]{:S(2)}) collective-permute-start(bf16[96,3840]{1,0:T(8,128)(2,1)} %get-tuple-element.38), channel_id=1, source_target_pairs={{0,16},{4,20},{8,24},{12,28},{16,0},{20,4},{24,8},{28,12},{32,48},... | collective-permute-start | bytes 2211848 | tf_op jit(solution)/shard_map/ppermute | solution.py:42
  28.2 17.0 %collective-permute-start.1 = (bf16[2,96,1920]{2,1,0:T(8,128)(2,1)}, bf16[2,96,1920]{2,1,0:T(8,128)(2,1)}, u32[]{:S(2)}, u32[]{:S(2)}) collective-permute-start(bf16[2,96,1920]{2,1,0:T(8,128)(2,1)} %get-tuple-element.34), channel_id=1, source_target_pairs={{0,12},{4,0},{8,4},{12,8},{16,28},{20,16},{24,20},{28,24},{32,44},... | collective-permute-start | bytes 2211848 | tf_op jit(solution)/shard_map/ppermute | solution.py:42
  28.4 18.8 %collective-permute-start.3 = (bf16[2,96,1920]{2,1,0:T(8,128)(2,1)}, bf16[2,96,1920]{2,1,0:T(8,128)(2,1)}, u32[]{:S(2)}, u32[]{:S(2)}) collective-permute-start(bf16[2,96,1920]{2,1,0:T(8,128)(2,1)} %get-tuple-element.34), channel_id=1, source_target_pairs={{0,4},{4,8},{8,12},{12,0},{16,20},{20,24},{24,28},{28,16},{32,36},... | collective-permute-start | bytes 2211848 | tf_op jit(solution)/shard_map/ppermute | solution.py:42
  29.6 36.0 %collective-permute-start.9 = (bf16[2,96,1920]{2,1,0:T(8,128)(2,1)}, bf16[2,96,1920]{2,1,0:T(8,128)(2,1)}, u32[]{:S(2)}, u32[]{:S(2)}) collective-permute-start(bf16[2,96,1920]{2,1,0:T(8,128)(2,1)} %get-tuple-element.33), channel_id=1, source_target_pairs={{0,96},{4,100},{8,104},{12,108},{16,112},{20,116},{24,120},{28,124... | collective-permute-start | bytes 2211848 | tf_op jit(solution)/shard_map/ppermute | solution.py:42
  32.4 37.1 %collective-permute-start.11 = (bf16[2,96,1920]{2,1,0:T(8,128)(2,1)}, bf16[2,96,1920]{2,1,0:T(8,128)(2,1)}, u32[]{:S(2)}, u32[]{:S(2)}) collective-permute-start(bf16[2,96,1920]{2,1,0:T(8,128)(2,1)} %get-tuple-element.33), channel_id=1, source_target_pairs={{0,32},{4,36},{8,40},{12,44},{16,48},{20,52},{24,56},{28,60},{32,6... | collective-permute-start | bytes 2211848 | tf_op jit(solution)/shard_map/ppermute | solution.py:42
  46.9 23.7 %collective-permute-start.2 = (bf16[1,96,1920]{2,1,0:T(8,128)(2,1)}, bf16[1,96,1920]{2,1,0:T(8,128)(2,1)S(1)}, u32[]{:S(2)}, u32[]{:S(2)}) collective-permute-start(bf16[1,96,1920]{2,1,0:T(8,128)(2,1)} %slice.137), channel_id=1, source_target_pairs={{0,12},{4,0},{8,4},{12,8},{16,28},{20,16},{24,20},{28,24},{32,44},... | collective-permute-start | bytes 1105928 | tf_op jit(solution)/shard_map/ppermute | solution.py:42
  48.9 21.7 %collective-permute-start.4 = (bf16[1,96,1920]{2,1,0:T(8,128)(2,1)}, bf16[1,96,1920]{2,1,0:T(8,128)(2,1)}, u32[]{:S(2)}, u32[]{:S(2)}) collective-permute-start(bf16[1,96,1920]{2,1,0:T(8,128)(2,1)} %slice.138), channel_id=1, source_target_pairs={{0,4},{4,8},{8,12},{12,0},{16,20},{20,24},{24,28},{28,16},{32,36},... | collective-permute-start | bytes 1105928 | tf_op jit(solution)/shard_map/ppermute | solution.py:42
  66.7 14.7 %collective-permute-start.10 = (bf16[1,96,1920]{2,1,0:T(8,128)(2,1)S(1)}, bf16[1,96,1920]{2,1,0:T(8,128)(2,1)S(1)}, u32[]{:S(2)}, u32[]{:S(2)}) collective-permute-start(bf16[1,96,1920]{2,1,0:T(8,128)(2,1)S(1)} %slice.143), channel_id=1, source_target_pairs={{0,96},{4,100},{8,104},{12,108},{16,112},{20,116},{24,120},{28,124... | collective-permute-start | bytes 1105928 | tf_op jit(solution)/shard_map/ppermute | solution.py:42
  70.5 10.8 %collective-permute-start.12 = (bf16[1,96,1920]{2,1,0:T(8,128)(2,1)S(1)}, bf16[1,96,1920]{2,1,0:T(8,128)(2,1)S(1)}, u32[]{:S(2)}, u32[]{:S(2)}) collective-permute-start(bf16[1,96,1920]{2,1,0:T(8,128)(2,1)S(1)} %slice.144), channel_id=1, source_target_pairs={{0,32},{4,36},{8,40},{12,44},{16,48},{20,52},{24,56},{28,60},{32,6... | collective-permute-start | bytes 1105928 | tf_op jit(solution)/shard_map/ppermute | solution.py:42
  78.3 62.8 %collective-permute-start.5 = (bf16[2,4,96,1920]{3,2,0,1:T(8,128)(2,1)S(1)}, bf16[2,4,96,1920]{3,2,0,1:T(8,128)(2,1)S(1)}, u32[]{:S(2)}, u32[]{:S(2)}) collective-permute-start(bf16[2,4,96,1920]{3,2,0,1:T(8,128)(2,1)S(1)} %bitcast.167), channel_id=1, source_target_pairs={{0,96},{4,100},{8,104},{12,108},{16,112},{20,116},{24,120},{28,124... | collective-permute-start | bytes 8847368 | tf_op jit(solution)/shard_map/ppermute | solution.py:42
  80.9 64.9 %collective-permute-start.7 = (bf16[2,4,96,1920]{3,2,0,1:T(8,128)(2,1)S(1)}, bf16[2,4,96,1920]{3,2,0,1:T(8,128)(2,1)S(1)}, u32[]{:S(2)}, u32[]{:S(2)}) collective-permute-start(bf16[2,4,96,1920]{3,2,0,1:T(8,128)(2,1)S(1)} %bitcast.168), channel_id=1, source_target_pairs={{0,32},{4,36},{8,40},{12,44},{16,48},{20,52},{24,56},{28,60},{32,6... | collective-permute-start | bytes 8847368 | tf_op jit(solution)/shard_map/ppermute | solution.py:42
  88.7 68.2 %collective-permute-start.13 = (bf16[4,2,96,1920]{3,2,1,0:T(8,128)(2,1)}, bf16[4,2,96,1920]{3,2,1,0:T(8,128)(2,1)}, u32[]{:S(2)}, u32[]{:S(2)}) collective-permute-start(bf16[4,2,96,1920]{3,2,1,0:T(8,128)(2,1)} %get-tuple-element.21), channel_id=1, source_target_pairs={{0,12},{4,0},{8,4},{12,8},{16,28},{20,16},{24,20},{28,24},{32,44},... | collective-permute-start | bytes 8847368 | tf_op jit(solution)/shard_map/ppermute | solution.py:42
  88.7 70.9 %collective-permute-start.15 = (bf16[4,2,96,1920]{3,2,1,0:T(8,128)(2,1)}, bf16[4,2,96,1920]{3,2,1,0:T(8,128)(2,1)}, u32[]{:S(2)}, u32[]{:S(2)}) collective-permute-start(bf16[4,2,96,1920]{3,2,1,0:T(8,128)(2,1)} %get-tuple-element.21), channel_id=1, source_target_pairs={{0,4},{4,8},{8,12},{12,0},{16,20},{20,24},{24,28},{28,16},{32,36},... | collective-permute-start | bytes 8847368 | tf_op jit(solution)/shard_map/ppermute | solution.py:42
  142.4 31.5 %collective-permute-start.6 = (bf16[1,4,96,1920]{3,2,0,1:T(8,128)(2,1)}, bf16[1,4,96,1920]{3,2,0,1:T(8,128)(2,1)}, u32[]{:S(2)}, u32[]{:S(2)}) collective-permute-start(bf16[1,4,96,1920]{3,2,0,1:T(8,128)(2,1)} %slice.139), channel_id=1, source_target_pairs={{0,96},{4,100},{8,104},{12,108},{16,112},{20,116},{24,120},{28,124... | collective-permute-start | bytes 4423688 | tf_op jit(solution)/shard_map/ppermute | solution.py:42
  148.8 31.2 %collective-permute-start.8 = (bf16[1,4,96,1920]{3,2,0,1:T(8,128)(2,1)}, bf16[1,4,96,1920]{3,2,0,1:T(8,128)(2,1)}, u32[]{:S(2)}, u32[]{:S(2)}) collective-permute-start(bf16[1,4,96,1920]{3,2,0,1:T(8,128)(2,1)} %slice.140), channel_id=1, source_target_pairs={{0,32},{4,36},{8,40},{12,44},{16,48},{20,52},{24,56},{28,60},{32,6... | collective-permute-start | bytes 4423688 | tf_op jit(solution)/shard_map/ppermute | solution.py:42
  159.6 72.0 %collective-permute-start.14 = (bf16[2,2,96,1920]{3,2,1,0:T(8,128)(2,1)}, bf16[2,2,96,1920]{3,2,1,0:T(8,128)(2,1)}, u32[]{:S(2)}, u32[]{:S(2)}) collective-permute-start(bf16[2,2,96,1920]{3,2,1,0:T(8,128)(2,1)} %slice.145), channel_id=1, source_target_pairs={{0,12},{4,0},{8,4},{12,8},{16,28},{20,16},{24,20},{28,24},{32,44},... | collective-permute-start | bytes 4423688 | tf_op jit(solution)/shard_map/ppermute | solution.py:42
  162.2 69.4 %collective-permute-start.16 = (bf16[2,2,96,1920]{3,2,1,0:T(8,128)(2,1)}, bf16[2,2,96,1920]{3,2,1,0:T(8,128)(2,1)}, u32[]{:S(2)}, u32[]{:S(2)}) collective-permute-start(bf16[2,2,96,1920]{3,2,1,0:T(8,128)(2,1)} %slice.146), channel_id=1, source_target_pairs={{0,4},{4,8},{8,12},{12,0},{16,20},{20,24},{24,28},{28,16},{32,36},... | collective-permute-start | bytes 4423688 | tf_op jit(solution)/shard_map/ppermute | solution.py:42
  288.9 21.0 %collective-permute-start.19 = (bf16[256,1536]{1,0:T(8,128)(2,1)}, bf16[256,1536]{1,0:T(8,128)(2,1)}, u32[]{:S(2)}, u32[]{:S(2)}) collective-permute-start(bf16[256,1536]{1,0:T(8,128)(2,1)} %convolution_convert_fusion.1), channel_id=1, source_target_pairs={{0,1},{1,0},{2,3},{3,2},{4,5},{5,4},{6,7},{7,6},{8,9},{9,8},{10,11... | collective-permute-start | bytes 2359304 | tf_op jit(solution)/shard_map/ppermute | solution.py:72
  304.4 18.5 %collective-permute-start.17 = (bf16[256,1536]{1,0:T(8,128)(2,1)S(1)}, bf16[256,1536]{1,0:T(8,128)(2,1)S(1)}, u32[]{:S(2)}, u32[]{:S(2)}) collective-permute-start(bf16[256,1536]{1,0:T(8,128)(2,1)S(1)} %convolution_convert_fusion.3), channel_id=1, source_target_pairs={{0,1},{1,0},{2,3},{3,2},{4,5},{5,4},{6,7},{7,6},{8,9},{9,8},{10,11... | collective-permute-start | bytes 2359304 | tf_op jit(solution)/shard_map/ppermute | solution.py:72
  329.0 3.5 collective-permute-start.20
  335.2 30.0 %collective-permute-start.21 = (bf16[512,3072]{1,0:T(8,128)(2,1)S(1)}, bf16[512,3072]{1,0:T(8,128)(2,1)S(1)}, u32[]{:S(2)}, u32[]{:S(2)}) collective-permute-start(bf16[512,3072]{1,0:T(8,128)(2,1)S(1)} %pad_maximum_fusion.1), channel_id=1, source_target_pairs={{0,2},{1,3},{4,6},{5,7},{8,10},{9,11},{12,14},{13,15},{16,18},{17,... | collective-permute-start | bytes 9437192 | tf_op jit(solution)/shard_map/ppermute | solution.py:18
  390.9 5.4 %collective-permute-start.23 = (f32[512,64]{0,1:T(8,128)S(1)}, f32[512,64]{0,1:T(8,128)S(1)}, u32[]{:S(2)}, u32[]{:S(2)}) collective-permute-start(f32[512,64]{0,1:T(8,128)S(1)} %fusion.93), channel_id=1, source_target_pairs={{0,1},{1,0},{2,3},{3,2},{4,5},{5,4},{6,7},{7,6},{8,9},{9,8},{10,11... | collective-permute-start | bytes 393224 | tf_op jit(solution)/shard_map/ppermute | solution.py:72
  408.0 10.0 %collective-permute-start.24 = (bf16[512,1536]{1,0:T(8,128)(2,1)}, bf16[512,1536]{1,0:T(8,128)(2,1)}, u32[]{:S(2)}, u32[]{:S(2)}) collective-permute-start(bf16[512,1536]{1,0:T(8,128)(2,1)} %multiply_convert_fusion), channel_id=1, source_target_pairs={{2,0},{3,1},{6,4},{7,5},{10,8},{11,9},{14,12},{15,13},{18,16},{19,... | collective-permute-start | bytes 4718600 | tf_op jit(solution)/shard_map/ppermute | solution.py:18
  423.8 82.1 %all-to-all-start = ((bf16[32,48,1536]{2,1,0:T(8,128)(2,1)}), bf16[32,48,1536]{2,1,0:T(8,128)(2,1)}, u32[]{:S(2)}, u32[]{:S(2)}) async-start(bf16[32,48,1536]{2,1,0:T(8,128)(2,1)} %bitcast.180), calls=%async_computation | async-start | bytes 9437184 | tf_op jit(solution)/shard_map/all_to_all | solution.py:288
  (39 other events, 347.0 us)

commit v8 on v7

--- a/solution.py
+++ b/solution.py
@@ -54,12 +54,11 @@
     return jnp.roll(relative, position, axis=0)
 
 
-def ctl_gather(piece):
+def ctl_gather(piece, split):
     at_y, at_z, at_x = ctl_coords(lax.axis_index("ctl"))
     rows, width = piece.shape
     paired = ctl_shift(piece, 0, 1, 0)
     pair = jnp.where(at_z == 0, jnp.stack([piece, paired]), jnp.stack([paired, piece]))
-    split = width // 2
     first = ring_stage(pair[..., :split], False, at_x)
     first = ring_stage(jnp.swapaxes(first, 0, 1), True, at_y)
     second = ring_stage(pair[..., split:], True, at_y)
@@ -164,23 +163,14 @@
         ],
         axis=1,
     )
-    front, back = ctl_gather(packed)
+    front, back = ctl_gather(packed, 3 * local_heads)
     count_rows = front.shape[0]
-    narrow = local_heads // 2
-    front_blocks = front.shape[1] // narrow
-    out_cols = back[:, narrow : narrow + local_heads]
-    projected = block_matmul(text_flat, front, 0, front_blocks, narrow)
-    value_rest = block_matmul(text_flat, back, 0, 1, narrow)
-    projected = projected.reshape(micro_count, seq_rows, front_blocks * narrow)
+    out_cols = back[:, :local_heads]
+    projected = block_matmul(text_flat, front, 0, 3, local_heads)
+    projected = projected.reshape(micro_count, seq_rows, 3 * local_heads)
     query_acc = projected[:, text_rows:, :local_heads]
     key_acc = projected[:, :, local_heads : 2 * local_heads]
-    value_acc = jnp.concatenate(
-        [
-            projected[:, :, 2 * local_heads :],
-            value_rest.reshape(micro_count, seq_rows, narrow),
-        ],
-        axis=2,
-    )
+    value_acc = projected[:, :, 2 * local_heads :]
     gain_pair = qk_gain[0]
     contract_last = (((1,), (1,)), ((), ()))
     other_out = lax.dynamic_slice_in_dim(out_cols, (1 - tp_index) * half_width, half_width, 0)
@@ -228,7 +218,7 @@
     act_narrow = jnp.concatenate(act_rows, axis=0)
     act_other = passed_along(act_narrow, "side", 1)
     control_rows = jnp.where(is_control, act_narrow, act_other)
-    own_part = block_matmul(control_rows, back, 3, 2, narrow)
+    own_part = block_matmul(control_rows, back, 1, 1, local_heads)
     own_narrow = own_part.astype(jnp.bfloat16)
     other_narrow = partner(own_narrow, "side", 0)
     residual_narrow = jnp.where(

time: 519 us -> 562 us (1.083)
  waiting for transfers between devices: 192 us -> 240 us
  local copies, waits for them, and re-layouts: 113 us -> 125 us
  other arithmetic: 83.8 us -> 73.4 us
  Pallas kernels: 31 us -> 23.8 us
    ppermute x17, waiting for transfers between devices: 74.4 us -> 123 us  [ctl_shift(): return lax.ppermute(value, 'ctl', pairs)]
    unnamed x10 -> x13, other arithmetic: 28.3 us -> 14.7 us
    unnamed x94, local copies, waits for them, and re-layouts: 32.8 us -> 43.9 us
    pallas_call x3 -> x2, Pallas kernels: 31 us -> 23.8 us  [block_matmul(): pl.pallas_call(kernel, grid=(block_count,), in_specs=[pl.BlockSpec((row_c...]
  transfers between devices with their start and end apart: 26 -> 26, of which waited for: 10 -> 14; matrix products, arithmetic and copies ran while one was open for 25% -> 22% of each run, Pallas kernels for 3% -> 0%
where the time goes in v8:
time: 562 us; the launch traced here: 552 us
  waiting for transfers between devices  240 us (43%)
  local copies, waits for them, and re-layouts  125 us (22%)
  other arithmetic  73.4 us (13%)
  starting transfers between devices  45.6 us (8%)
  matrix products  31.6 us (6%)
  Pallas kernels  23.8 us (4%)
  blocking collectives  10.7 us (2%)
    ppermute x17, waiting for transfers between devices, ctl_shift(): return lax.ppermute(value, 'ctl', pairs)  123 us
    all_to_all x1, waiting for transfers between devices, local(): received = lax.all_to_all(group_parts, 'ctl', 0, 0, tiled=True)  71.8 us
    unnamed x94, local copies, waits for them, and re-layouts  43.9 us
    ppermute x2, waiting for transfers between devices, passed_along(): return lax.ppermute(shard, axis, pairs)  28.2 us
    pallas_call x2, Pallas kernels, block_matmul(): pl.pallas_call(kernel, grid=(block_count,), in_specs=[pl.BlockSpec((row_c...  23.8 us
    ppermute x17, starting transfers between devices, ctl_shift(): return lax.ppermute(value, 'ctl', pairs)  19.3 us
    transpose x2, local copies, waits for them, and re-layouts, ctl_gather(): second = jnp.moveaxis(second, 0, 2)  16.5 us
    gather x1, local copies, waits for them, and re-layouts, local(): jnp.take(latent, order_row, axis=0)  14.8 us
  transfers between devices with their start and end apart: 26, of which 14 were waited for; matrix products, arithmetic and copies ran while one was open for 22% of the time, Pallas kernels for 0%

profile of v8, /device:TPU:5, one launch (start us, length us, event | category | flops | bytes accessed | tf_op | source)
XLA Modules:
  0.0 552.4 jit_solution(235453150524588578)
XLA Ops:
  8.0 14.8 %gather_fusion.1 = bf16[512,3072]{1,0:T(8,128)(2,1)} fusion(bf16[2,256,3072]{2,1,0:T(8,128)(2,1)S(1)} %copy-done, s32[512]{0:T(512)S(1)} %bitcast.180), kind=kCustom, calls=%fused_computation.1 | custom fusion | bytes 6295552 | tf_op jit(solution)/shard_map/vmap(jit(_take))/gather | solution.py:143
  46.1 10.0 %collective-permute-done.9 = bf16[2,96,1536]{2,1,0:T(8,128)(2,1)S(1)} collective-permute-done((bf16[2,96,1536]{2,1,0:T(8,128)(2,1)S(1)}, bf16[2,96,1536]{2,1,0:T(8,128)(2,1)S(1)}, u32[]{:S(2)}, u32[]{:S(2)}) %collective-permute-start.9) | collective-permute-done | bytes 589856 | tf_op jit(solution)/shard_map/ppermute | solution.py:42
  73.8 55.0 %collective-permute-done.2 = bf16[1,96,2304]{2,1,0:T(8,128)(2,1)S(1)} collective-permute-done((bf16[1,96,2304]{2,1,0:T(8,128)(2,1)S(1)}, bf16[1,96,2304]{2,1,0:T(8,128)(2,1)S(1)}, u32[]{:S(2)}, u32[]{:S(2)}) %collective-permute-start.2) | collective-permute-done | bytes 442400 | tf_op jit(solution)/shard_map/ppermute | solution.py:42
  140.6 8.0 %fusion.2.rows_ref = bf16[768,3072]{1,0:T(8,128)(2,1)} fusion(f32[2,384,3072]{2,1,0:T(8,128)} %get-tuple-element.20, f32[2,3072]{1,0:T(2,128)S(1)} %get-tuple-element.33, f32[2,3072]{1,0:T(2,128)S(1)} %get-tuple-element.34, f32[768]{0:T(1024)S(1)} %rsqrt.47, f32[768]{0:T(1024)S(1)} %div.70), kind=kLoop, calls=%fused_computation.6 | loop fusion | flops 11796480 | bytes 14211072 | tf_op jit(solution)/shard_map/convert_element_type | solution.py:151
  154.3 6.0 %collective-permute-done.14 = bf16[2,2,96,1536]{3,2,1,0:T(8,128)(2,1)} collective-permute-done((bf16[2,2,96,1536]{3,2,1,0:T(8,128)(2,1)}, bf16[2,2,96,1536]{3,2,1,0:T(8,128)(2,1)}, u32[]{:S(2)}, u32[]{:S(2)}) %collective-permute-start.14) | collective-permute-done | bytes 1179680 | tf_op jit(solution)/shard_map/ppermute | solution.py:42
  176.1 31.4 %collective-permute-done.5 = bf16[2,4,96,2304]{3,2,0,1:T(8,128)(2,1)} collective-permute-done((bf16[2,4,96,2304]{3,2,0,1:T(8,128)(2,1)}, bf16[2,4,96,2304]{3,2,0,1:T(8,128)(2,1)}, u32[]{:S(2)}, u32[]{:S(2)}) %collective-permute-start.5) | collective-permute-done | bytes 3538976 | tf_op jit(solution)/shard_map/ppermute | solution.py:42
  216.8 8.2 %dynamic-slice_bitcast_fusion = bf16[4,2,4,96,1536]{4,3,1,0,2:T(8,128)(2,1)} fusion(bf16[8,4,2,96,1536]{4,3,2,1,0:T(8,128)(2,1)} %bitcast_dynamic-update-slice_fusion.7, s32[]{:T(128)S(6)} %select_n.174), kind=kLoop, calls=%fused_computation.11 | loop fusion | bytes 18874372 | tf_op jit(solution)/shard_map/transpose | solution.py:66
  225.0 8.3 %copy.30 = bf16[4,2,4,96,1536]{4,3,2,1,0:T(8,128)(2,1)} copy(bf16[4,2,4,96,1536]{4,3,1,0,2:T(8,128)(2,1)} %dynamic-slice_bitcast_fusion) | data formatting | bytes 18874368 | tf_op jit(solution)/shard_map/transpose | solution.py:66
  233.4 4.8 slice.148
  246.0 6.0 %collective-permute-done.8 = bf16[1,4,96,2304]{3,2,0,1:T(8,128)(2,1)} collective-permute-done((bf16[1,4,96,2304]{3,2,0,1:T(8,128)(2,1)}, bf16[1,4,96,2304]{3,2,0,1:T(8,128)(2,1)}, u32[]{:S(2)}, u32[]{:S(2)}) %collective-permute-start.8) | collective-permute-done | bytes 1769504 | tf_op jit(solution)/shard_map/ppermute | solution.py:42
  274.2 7.0 %constant_dynamic-slice_fusion.3 = bf16[4,2,4,96,2304]{4,3,1,2,0:T(8,128)(2,1)S(1)} fusion(bf16[8,2,4,96,2304]{4,3,1,2,0:T(8,128)(2,1)} %bitcast_dynamic-update-slice_fusion.3, s32[]{:T(128)S(6)} %select_n.177), kind=kLoop, calls=%fused_computation.141 | loop fusion | bytes 28311556 | tf_op jit(solution)/shard_map/jit(_roll_dynamic)/dynamic_slice | solution.py:54
  281.2 5.6 %copy.24 = bf16[4,2,4,96,2304]{4,3,2,1,0:T(8,128)(2,1)} copy(bf16[4,2,4,96,2304]{4,3,1,2,0:T(8,128)(2,1)S(1)} %constant_dynamic-slice_fusion.3) | data formatting | bytes 28311552 | tf_op jit(solution)/shard_map/jit(_roll_dynamic)/dynamic_slice | solution.py:54
  286.9 16.7 %shard_map.140 = f32[768,2304]{1,0:T(8,128)} custom-call(bf16[768,3072]{1,0:T(8,128)(2,1)} %fusion.2.rows_ref, bf16[3072,2304]{1,0:T(8,128)(2,1)} %bitcast.186), custom_call_target="tpu_custom_call" | custom-call | flops 10871635968 | bytes 25952256 | tf_op jit(solution)/shard_map/pallas_call | solution.py:80
  320.1 5.3 convolution_convert_fusion.5
  337.6 5.3 convolution_convert_fusion.6
  351.4 12.2 %collective-permute-done.17 = bf16[256,1536]{1,0:T(8,128)(2,1)S(1)} collective-permute-done((bf16[256,1536]{1,0:T(8,128)(2,1)S(1)}, bf16[256,1536]{1,0:T(8,128)(2,1)S(1)}, u32[]{:S(2)}, u32[]{:S(2)}) %collective-permute-start.17) | collective-permute-done | bytes 786464 | tf_op jit(solution)/shard_map/ppermute | solution.py:71
  377.3 28.2 %collective-permute-done.21 = bf16[512,3072]{1,0:T(8,128)(2,1)S(1)} collective-permute-done((bf16[512,3072]{1,0:T(8,128)(2,1)S(1)}, bf16[512,3072]{1,0:T(8,128)(2,1)S(1)}, u32[]{:S(2)}, u32[]{:S(2)}) %collective-permute-start.21) | collective-permute-done | bytes 3145760 | tf_op jit(solution)/shard_map/ppermute | solution.py:18
  408.3 7.1 %shard_map.141 = f32[512,768]{1,0:T(8,128)} custom-call(bf16[512,3072]{1,0:T(8,128)(2,1)} %broadcast_select_fusion.rows_ref, bf16[3072,1536]{1,0:T(8,128)(2,1)} %bitcast.179), custom_call_target="tpu_custom_call" | custom-call | flops 2415919104 | bytes 9437184 | tf_op jit(solution)/shard_map/pallas_call | solution.py:80
  423.9 5.4 all-reduce.1
  438.8 5.3 all-reduce
  448.0 6.7 %collective-permute-start.24 = (bf16[512,1536]{1,0:T(8,128)(2,1)}, bf16[512,1536]{1,0:T(8,128)(2,1)}, u32[]{:S(2)}, u32[]{:S(2)}) collective-permute-start(bf16[512,1536]{1,0:T(8,128)(2,1)} %multiply_convert_fusion), channel_id=1, source_target_pairs={{2,0},{3,1},{6,4},{7,5},{10,8},{11,9},{14,12},{15,13},{18,16},{19,... | collective-permute-start | bytes 4718600 | tf_op jit(solution)/shard_map/ppermute | solution.py:18
  458.0 5.7 %convolution_convert_fusion = bf16[1536,1536]{1,0:T(8,128)(2,1)} fusion(bf16[512,1536]{0,1:T(8,128)(2,1)S(1)} %bitcast.203, bf16[512,1536]{1,0:T(8,128)(2,1)} %collective-permute-done.24, bf16[512,1536]{1,0:T(8,128)(2,1)} %multiply_convert_fusion, pred[]{:T(512)S(6)} %eq.22), kind=kOutput, calls=%fused_computation.13 | convolution fusion | flops 2419064832 | bytes 9437185 | tf_op jit(solution)/shard_map/dot_general | solution.py:274
  463.7 8.0 %all-to-all-start = ((bf16[32,48,1536]{2,1,0:T(8,128)(2,1)}), bf16[32,48,1536]{2,1,0:T(8,128)(2,1)}, u32[]{:S(2)}, u32[]{:S(2)}) async-start(bf16[32,48,1536]{2,1,0:T(8,128)(2,1)} %bitcast.199), calls=%async_computation | async-start | bytes 9437184 | tf_op jit(solution)/shard_map/all_to_all | solution.py:278
  476.5 71.8 %all-to-all-done = bf16[32,48,1536]{2,1,0:T(8,128)(2,1)} async-done(((bf16[32,48,1536]{2,1,0:T(8,128)(2,1)}), bf16[32,48,1536]{2,1,0:T(8,128)(2,1)}, u32[]{:S(2)}, u32[]{:S(2)}) %all-to-all-start) | async-done | bytes 4718624 | tf_op jit(solution)/shard_map/all_to_all | solution.py:278
  (226 shorter events, 207.7 us)
Async XLA Ops:
  6.3 33.2 %collective-permute-start = (bf16[96,3840]{1,0:T(8,128)(2,1)}, bf16[96,3840]{1,0:T(8,128)(2,1)}, u32[]{:S(2)}, u32[]{:S(2)}) collective-permute-start(bf16[96,3840]{1,0:T(8,128)(2,1)} %get-tuple-element.31), channel_id=1, source_target_pairs={{0,16},{4,20},{8,24},{12,28},{16,0},{20,4},{24,8},{28,12},{32,48},... | collective-permute-start | bytes 2211848 | tf_op jit(solution)/shard_map/ppermute | solution.py:42
  41.5 14.5 %collective-permute-start.9 = (bf16[2,96,1536]{2,1,0:T(8,128)(2,1)S(1)}, bf16[2,96,1536]{2,1,0:T(8,128)(2,1)S(1)}, u32[]{:S(2)}, u32[]{:S(2)}) collective-permute-start(bf16[2,96,1536]{2,1,0:T(8,128)(2,1)S(1)} %slice.143), channel_id=1, source_target_pairs={{0,96},{4,100},{8,104},{12,108},{16,112},{20,116},{24,120},{28,124... | collective-permute-start | bytes 1769480 | tf_op jit(solution)/shard_map/ppermute | solution.py:42
  44.3 15.2 %collective-permute-start.11 = (bf16[2,96,1536]{2,1,0:T(8,128)(2,1)S(1)}, bf16[2,96,1536]{2,1,0:T(8,128)(2,1)S(1)}, u32[]{:S(2)}, u32[]{:S(2)}) collective-permute-start(bf16[2,96,1536]{2,1,0:T(8,128)(2,1)S(1)} %slice.143), channel_id=1, source_target_pairs={{0,32},{4,36},{8,40},{12,44},{16,48},{20,52},{24,56},{28,60},{32,6... | collective-permute-start | bytes 1769480 | tf_op jit(solution)/shard_map/ppermute | solution.py:42
  44.5 26.5 %collective-permute-start.1 = (bf16[2,96,2304]{2,1,0:T(8,128)(2,1)S(1)}, bf16[2,96,2304]{2,1,0:T(8,128)(2,1)S(1)}, u32[]{:S(2)}, u32[]{:S(2)}) collective-permute-start(bf16[2,96,2304]{2,1,0:T(8,128)(2,1)S(1)} %slice.135), channel_id=1, source_target_pairs={{0,12},{4,0},{8,4},{12,8},{16,28},{20,16},{24,20},{28,24},{32,44},... | collective-permute-start | bytes 2654216 | tf_op jit(solution)/shard_map/ppermute | solution.py:42
  44.8 26.5 %collective-permute-start.3 = (bf16[2,96,2304]{2,1,0:T(8,128)(2,1)S(1)}, bf16[2,96,2304]{2,1,0:T(8,128)(2,1)S(1)}, u32[]{:S(2)}, u32[]{:S(2)}) collective-permute-start(bf16[2,96,2304]{2,1,0:T(8,128)(2,1)S(1)} %slice.135), channel_id=1, source_target_pairs={{0,4},{4,8},{8,12},{12,0},{16,20},{20,24},{24,28},{28,16},{32,36},... | collective-permute-start | bytes 2654216 | tf_op jit(solution)/shard_map/ppermute | solution.py:42
  56.1 8.0 %collective-permute-start.10 = (bf16[1,96,1536]{2,1,0:T(8,128)(2,1)S(1)}, bf16[1,96,1536]{2,1,0:T(8,128)(2,1)S(1)}, u32[]{:S(2)}, u32[]{:S(2)}) collective-permute-start(bf16[1,96,1536]{2,1,0:T(8,128)(2,1)S(1)} %slice.144), channel_id=1, source_target_pairs={{0,96},{4,100},{8,104},{12,108},{16,112},{20,116},{24,120},{28,124... | collective-permute-start | bytes 884744 | tf_op jit(solution)/shard_map/ppermute | solution.py:42
  59.6 7.8 %collective-permute-start.12 = (bf16[1,96,1536]{2,1,0:T(8,128)(2,1)S(1)}, bf16[1,96,1536]{2,1,0:T(8,128)(2,1)S(1)}, u32[]{:S(2)}, u32[]{:S(2)}) collective-permute-start(bf16[1,96,1536]{2,1,0:T(8,128)(2,1)S(1)} %slice.145), channel_id=1, source_target_pairs={{0,32},{4,36},{8,40},{12,44},{16,48},{20,52},{24,56},{28,60},{32,6... | collective-permute-start | bytes 884744 | tf_op jit(solution)/shard_map/ppermute | solution.py:42
  69.5 65.2 %collective-permute-start.13 = (bf16[4,2,96,1536]{3,2,1,0:T(8,128)(2,1)S(1)}, bf16[4,2,96,1536]{3,2,1,0:T(8,128)(2,1)S(1)}, u32[]{:S(2)}, u32[]{:S(2)}) collective-permute-start(bf16[4,2,96,1536]{3,2,1,0:T(8,128)(2,1)S(1)} %get-tuple-element.18), channel_id=1, source_target_pairs={{0,12},{4,0},{8,4},{12,8},{16,28},{20,16},{24,20},{28,24},{32,44},... | collective-permute-start | bytes 7077896 | tf_op jit(solution)/shard_map/ppermute | solution.py:42
  69.7 67.7 %collective-permute-start.15 = (bf16[4,2,96,1536]{3,2,1,0:T(8,128)(2,1)S(1)}, bf16[4,2,96,1536]{3,2,1,0:T(8,128)(2,1)S(1)}, u32[]{:S(2)}, u32[]{:S(2)}) collective-permute-start(bf16[4,2,96,1536]{3,2,1,0:T(8,128)(2,1)S(1)} %get-tuple-element.18), channel_id=1, source_target_pairs={{0,4},{4,8},{8,12},{12,0},{16,20},{20,24},{24,28},{28,16},{32,36},... | collective-permute-start | bytes 7077896 | tf_op jit(solution)/shard_map/ppermute | solution.py:42
  71.0 57.8 %collective-permute-start.2 = (bf16[1,96,2304]{2,1,0:T(8,128)(2,1)S(1)}, bf16[1,96,2304]{2,1,0:T(8,128)(2,1)S(1)}, u32[]{:S(2)}, u32[]{:S(2)}) collective-permute-start(bf16[1,96,2304]{2,1,0:T(8,128)(2,1)S(1)} %slice.136), channel_id=1, source_target_pairs={{0,12},{4,0},{8,4},{12,8},{16,28},{20,16},{24,20},{28,24},{32,44},... | collective-permute-start | bytes 1327112 | tf_op jit(solution)/shard_map/ppermute | solution.py:42
  71.3 57.5 %collective-permute-start.4 = (bf16[1,96,2304]{2,1,0:T(8,128)(2,1)S(1)}, bf16[1,96,2304]{2,1,0:T(8,128)(2,1)S(1)}, u32[]{:S(2)}, u32[]{:S(2)}) collective-permute-start(bf16[1,96,2304]{2,1,0:T(8,128)(2,1)S(1)} %slice.137), channel_id=1, source_target_pairs={{0,4},{4,8},{8,12},{12,0},{16,20},{20,24},{24,28},{28,16},{32,36},... | collective-permute-start | bytes 1327112 | tf_op jit(solution)/shard_map/ppermute | solution.py:42
  133.2 74.3 %collective-permute-start.5 = (bf16[2,4,96,2304]{3,2,0,1:T(8,128)(2,1)}, bf16[2,4,96,2304]{3,2,0,1:T(8,128)(2,1)}, u32[]{:S(2)}, u32[]{:S(2)}) collective-permute-start(bf16[2,4,96,2304]{3,2,0,1:T(8,128)(2,1)} %dynamic-slice_bitcast_fusion.1), channel_id=1, source_target_pairs={{0,96},{4,100},{8,104},{12,108},{16,112},{20,116},{24,120},{28,124... | collective-permute-start | bytes 10616840 | tf_op jit(solution)/shard_map/ppermute | solution.py:42
  133.7 78.7 %collective-permute-start.7 = (bf16[2,4,96,2304]{3,2,0,1:T(8,128)(2,1)}, bf16[2,4,96,2304]{3,2,0,1:T(8,128)(2,1)}, u32[]{:S(2)}, u32[]{:S(2)}) collective-permute-start(bf16[2,4,96,2304]{3,2,0,1:T(8,128)(2,1)} %dynamic-slice_bitcast_fusion.1), channel_id=1, source_target_pairs={{0,32},{4,36},{8,40},{12,44},{16,48},{20,52},{24,56},{28,60},{32,6... | collective-permute-start | bytes 10616840 | tf_op jit(solution)/shard_map/ppermute | solution.py:42
  135.9 24.4 %collective-permute-start.14 = (bf16[2,2,96,1536]{3,2,1,0:T(8,128)(2,1)}, bf16[2,2,96,1536]{3,2,1,0:T(8,128)(2,1)}, u32[]{:S(2)}, u32[]{:S(2)}) collective-permute-start(bf16[2,2,96,1536]{3,2,1,0:T(8,128)(2,1)} %slice.146), channel_id=1, source_target_pairs={{0,12},{4,0},{8,4},{12,8},{16,28},{20,16},{24,20},{28,24},{32,44},... | collective-permute-start | bytes 3538952 | tf_op jit(solution)/shard_map/ppermute | solution.py:42
  140.0 24.1 %collective-permute-start.16 = (bf16[2,2,96,1536]{3,2,1,0:T(8,128)(2,1)}, bf16[2,2,96,1536]{3,2,1,0:T(8,128)(2,1)}, u32[]{:S(2)}, u32[]{:S(2)}) collective-permute-start(bf16[2,2,96,1536]{3,2,1,0:T(8,128)(2,1)} %slice.147), channel_id=1, source_target_pairs={{0,4},{4,8},{8,12},{12,0},{16,20},{20,24},{24,28},{28,16},{32,36},... | collective-permute-start | bytes 3538952 | tf_op jit(solution)/shard_map/ppermute | solution.py:42
  210.4 35.6 %collective-permute-start.6 = (bf16[1,4,96,2304]{3,2,0,1:T(8,128)(2,1)}, bf16[1,4,96,2304]{3,2,0,1:T(8,128)(2,1)}, u32[]{:S(2)}, u32[]{:S(2)}) collective-permute-start(bf16[1,4,96,2304]{3,2,0,1:T(8,128)(2,1)} %slice.138), channel_id=1, source_target_pairs={{0,96},{4,100},{8,104},{12,108},{16,112},{20,116},{24,120},{28,124... | collective-permute-start | bytes 5308424 | tf_op jit(solution)/shard_map/ppermute | solution.py:42
  215.2 36.8 %collective-permute-start.8 = (bf16[1,4,96,2304]{3,2,0,1:T(8,128)(2,1)}, bf16[1,4,96,2304]{3,2,0,1:T(8,128)(2,1)}, u32[]{:S(2)}, u32[]{:S(2)}) collective-permute-start(bf16[1,4,96,2304]{3,2,0,1:T(8,128)(2,1)} %slice.139), channel_id=1, source_target_pairs={{0,32},{4,36},{8,40},{12,44},{16,48},{20,52},{24,56},{28,60},{32,6... | collective-permute-start | bytes 5308424 | tf_op jit(solution)/shard_map/ppermute | solution.py:42
  328.9 22.5 %collective-permute-start.19 = (bf16[256,1536]{1,0:T(8,128)(2,1)}, bf16[256,1536]{1,0:T(8,128)(2,1)}, u32[]{:S(2)}, u32[]{:S(2)}) collective-permute-start(bf16[256,1536]{1,0:T(8,128)(2,1)} %convolution_convert_fusion.1), channel_id=1, source_target_pairs={{0,1},{1,0},{2,3},{3,2},{4,5},{5,4},{6,7},{7,6},{8,9},{9,8},{10,11... | collective-permute-start | bytes 2359304 | tf_op jit(solution)/shard_map/ppermute | solution.py:71
  346.1 17.5 %collective-permute-start.17 = (bf16[256,1536]{1,0:T(8,128)(2,1)S(1)}, bf16[256,1536]{1,0:T(8,128)(2,1)S(1)}, u32[]{:S(2)}, u32[]{:S(2)}) collective-permute-start(bf16[256,1536]{1,0:T(8,128)(2,1)S(1)} %convolution_convert_fusion.3), channel_id=1, source_target_pairs={{0,1},{1,0},{2,3},{3,2},{4,5},{5,4},{6,7},{7,6},{8,9},{9,8},{10,11... | collective-permute-start | bytes 2359304 | tf_op jit(solution)/shard_map/ppermute | solution.py:71
  369.7 3.4 collective-permute-start.20
  375.8 29.7 %collective-permute-start.21 = (bf16[512,3072]{1,0:T(8,128)(2,1)S(1)}, bf16[512,3072]{1,0:T(8,128)(2,1)S(1)}, u32[]{:S(2)}, u32[]{:S(2)}) collective-permute-start(bf16[512,3072]{1,0:T(8,128)(2,1)S(1)} %pad_maximum_fusion.1), channel_id=1, source_target_pairs={{0,2},{1,3},{4,6},{5,7},{8,10},{9,11},{12,14},{13,15},{16,18},{17,... | collective-permute-start | bytes 9437192 | tf_op jit(solution)/shard_map/ppermute | solution.py:18
  430.8 5.4 collective-permute-start.23
  448.0 10.0 %collective-permute-start.24 = (bf16[512,1536]{1,0:T(8,128)(2,1)}, bf16[512,1536]{1,0:T(8,128)(2,1)}, u32[]{:S(2)}, u32[]{:S(2)}) collective-permute-start(bf16[512,1536]{1,0:T(8,128)(2,1)} %multiply_convert_fusion), channel_id=1, source_target_pairs={{2,0},{3,1},{6,4},{7,5},{10,8},{11,9},{14,12},{15,13},{18,16},{19,... | collective-permute-start | bytes 4718600 | tf_op jit(solution)/shard_map/ppermute | solution.py:18
  463.7 84.5 %all-to-all-start = ((bf16[32,48,1536]{2,1,0:T(8,128)(2,1)}), bf16[32,48,1536]{2,1,0:T(8,128)(2,1)}, u32[]{:S(2)}, u32[]{:S(2)}) async-start(bf16[32,48,1536]{2,1,0:T(8,128)(2,1)} %bitcast.199), calls=%async_computation | async-start | bytes 9437184 | tf_op jit(solution)/shard_map/all_to_all | solution.py:278
  (33 other events, 317.1 us)

commit v9 on v7

--- a/solution.py
+++ b/solution.py
@@ -56,16 +56,24 @@
 
 def ctl_gather(piece):
     at_y, at_z, at_x = ctl_coords(lax.axis_index("ctl"))
-    rows, width = piece.shape
-    paired = ctl_shift(piece, 0, 1, 0)
-    pair = jnp.where(at_z == 0, jnp.stack([piece, paired]), jnp.stack([paired, piece]))
-    split = width // 2
-    first = ring_stage(pair[..., :split], False, at_x)
-    first = ring_stage(jnp.swapaxes(first, 0, 1), True, at_y)
-    second = ring_stage(pair[..., split:], True, at_y)
-    second = ring_stage(second, False, at_x)
-    second = jnp.moveaxis(second, 0, 2)
-    return first.reshape(-1, split), second.reshape(-1, width - split)
+    split = piece.shape[1] // 2
+
+    def both_rings(block):
+        first = ring_stage(block[:, :split], False, at_x)
+        first = ring_stage(first, True, at_y)
+        second = ring_stage(block[:, split:], True, at_y)
+        second = jnp.swapaxes(ring_stage(second, False, at_x), 0, 1)
+        return first, second
+
+    own_first, own_second = both_rings(piece)
+    paired_first, paired_second = both_rings(ctl_shift(piece, 0, 1, 0))
+
+    def join(own, paired):
+        low = jnp.where(at_z == 0, own, paired)
+        high = jnp.where(at_z == 0, paired, own)
+        return jnp.stack([low, high], axis=1).reshape(-1, own.shape[-1])
+
+    return join(own_first, paired_first), join(own_second, paired_second)
 
 
 def swap(value, axis):

time: 519 us -> 549 us (1.058)
  the two profiles are of different devices: /device:TPU:5 before, /device:TPU:19 now
where the time goes in v9:
time: 549 us; the launch traced here: 538 us
  waiting for transfers between devices  177 us (32%)
  other arithmetic  142 us (26%)
  local copies, waits for them, and re-layouts  73.2 us (13%)
  starting transfers between devices  71.1 us (13%)
  matrix products  31.6 us (6%)
  Pallas kernels  31 us (6%)
  blocking collectives  10.8 us (2%)
    all_to_all x1, waiting for transfers between devices, local(): received = lax.all_to_all(group_parts, 'ctl', 0, 0, tiled=True)  71.2 us
    ppermute x33, waiting for transfers between devices, ctl_shift(): return lax.ppermute(value, 'ctl', pairs)  58.6 us
    another operation x6, other arithmetic, join(): return jnp.stack([low, high], axis=1).reshape(-1, own.shape[-1])  55.9 us
    ppermute x33, starting transfers between devices, ctl_shift(): return lax.ppermute(value, 'ctl', pairs)  42.8 us
    pallas_call x3, Pallas kernels, block_matmul(): pl.pallas_call(kernel, grid=(block_count,), in_specs=[pl.BlockSpec((row_c...  31 us
    ppermute x2, waiting for transfers between devices, passed_along(): return lax.ppermute(shard, axis, pairs)  30.3 us
    another operation x12, other arithmetic, ring_stage(): relative = jnp.stack([block, from_after, far, from_before])  16.9 us
    gather x1, local copies, waits for them, and re-layouts, local(): jnp.take(latent, order_row, axis=0)  14.7 us
  transfers between devices with their start and end apart: 42, of which 13 were waited for; matrix products, arithmetic and copies ran while one was open for 28% of the time, Pallas kernels for 3%

profile of v9, /device:TPU:19, one launch (start us, length us, event | category | flops | bytes accessed | tf_op | source)
XLA Modules:
  0.0 538.4 jit_solution(6227762656354656584)
XLA Ops:
  14.8 14.7 %gather_fusion.1 = bf16[512,3072]{1,0:T(8,128)(2,1)} fusion(bf16[2,256,3072]{2,1,0:T(8,128)(2,1)S(1)} %copy-done, s32[512]{0:T(512)S(1)} %bitcast.174), kind=kCustom, calls=%fused_computation.1 | custom fusion | bytes 6295552 | tf_op jit(solution)/shard_map/vmap(jit(_take))/gather | solution.py:152
  77.1 22.0 %collective-permute-done.25 = bf16[96,1920]{1,0:T(8,128)(2,1)} collective-permute-done((bf16[96,1920]{1,0:T(8,128)(2,1)S(1)}, bf16[96,1920]{1,0:T(8,128)(2,1)}, u32[]{:S(2)}, u32[]{:S(2)}) %collective-permute-start.25) | collective-permute-done | bytes 368672 | tf_op jit(solution)/shard_map/ppermute | solution.py:42
  101.9 8.1 %fusion.2.rows_ref = bf16[768,3072]{1,0:T(8,128)(2,1)} fusion(f32[2,384,3072]{2,1,0:T(8,128)} %get-tuple-element.26, f32[2,3072]{1,0:T(2,128)S(1)} %get-tuple-element.45, f32[2,3072]{1,0:T(2,128)} %get-tuple-element.46, f32[768]{0:T(1024)S(1)} %rsqrt.47, f32[768]{0:T(1024)S(1)} %div.70), kind=kLoop, calls=%fused_computation.40 | loop fusion | flops 11796480 | bytes 14211072 | tf_op jit(solution)/shard_map/convert_element_type | solution.py:160
  132.5 10.7 %collective-permute-done.23 = bf16[4,96,1920]{2,1,0:T(8,128)(2,1)S(1)} collective-permute-done((bf16[4,96,1920]{2,1,0:T(8,128)(2,1)}, bf16[4,96,1920]{2,1,0:T(8,128)(2,1)S(1)}, u32[]{:S(2)}, u32[]{:S(2)}) %collective-permute-start.23) | collective-permute-done | bytes 1474592 | tf_op jit(solution)/shard_map/ppermute | solution.py:42
  155.6 10.7 %collective-permute-done.5 = bf16[2,96,1920]{2,1,0:T(8,128)(2,1)S(1)} collective-permute-done((bf16[2,96,1920]{2,1,0:T(8,128)(2,1)S(1)}, bf16[2,96,1920]{2,1,0:T(8,128)(2,1)S(1)}, u32[]{:S(2)}, u32[]{:S(2)}) %collective-permute-start.5) | collective-permute-done | bytes 737312 | tf_op jit(solution)/shard_map/ppermute | solution.py:42
  192.0 16.6 %select_bitcast_fusion.3 = (bf16[4,1,4,96,1920]{4,3,2,0,1:T(8,128)(2,1)}, bf16[4,4,96,1920]{3,2,1,0:T(8,128)(2,1)S(1)}, bf16[4,4,96,1920]{3,2,1,0:T(8,128)(2,1)}) fusion(pred[]{:T(512)S(6)} %eq.21, s32[]{:T(128)S(6)} %select_n.204, bf16[1,4,96,1920]{3,2,1,0:T(8,128)(2,1)} %bitcast.16, bf16[1,4,96,1920]{3,2,1,0:T(8,128)(2,1)S(1)} %maximum_bitcast_fusion, ...), kind=kLoop, calls=%fused_computation.79 | loop fusion | flops 44236800 | bytes 29491204 | tf_op jit(solution)/shard_map/stack | solution.py:74
  208.6 5.8 %select_bitcast_fusion.2 = bf16[4,1,4,96,1920]{4,3,2,0,1:T(8,128)(2,1)} fusion(bf16[4,4,96,1920]{3,2,1,0:T(8,128)(2,1)} %get-tuple-element.21, bf16[4,4,96,1920]{3,2,1,0:T(8,128)(2,1)S(1)} %get-tuple-element.20, pred[]{:T(512)S(6)} %eq.21), kind=kLoop, calls=%fused_computation.78 | loop fusion | flops 2949120 | bytes 17694720 | tf_op jit(solution)/shard_map/stack | solution.py:74
  214.3 6.0 %pad_maximum_fusion = bf16[4,2,4,96,1920]{4,3,2,0,1:T(8,128)(2,1)S(1)} fusion(bf16[4,1,4,96,1920]{4,3,2,0,1:T(8,128)(2,1)} %select_bitcast_fusion.2, bf16[4,1,4,96,1920]{4,3,2,0,1:T(8,128)(2,1)} %get-tuple-element.19), kind=kLoop, calls=%fused_computation.20 | loop fusion | flops 5898240 | bytes 23592960 | tf_op jit(solution)/shard_map/stack | solution.py:74
  225.5 17.2 %shard_map.140 = f32[768,1920]{1,0:T(8,128)} custom-call(bf16[768,3072]{1,0:T(8,128)(2,1)} %fusion.2.rows_ref, bf16[3072,1920]{1,0:T(8,128)(2,1)} %bitcast.177), custom_call_target="tpu_custom_call" | custom-call | flops 9059696640 | bytes 22413312 | tf_op jit(solution)/shard_map/pallas_call | solution.py:89
  253.2 15.8 %select_bitcast_fusion.1 = (bf16[4,1,4,96,1920]{4,3,0,2,1:T(8,128)(2,1)}, bf16[4,4,96,1920]{3,2,1,0:T(8,128)(2,1)S(1)}, bf16[4,4,96,1920]{3,2,1,0:T(8,128)(2,1)}) fusion(pred[]{:T(512)S(6)} %eq.21, s32[]{:T(128)S(6)} %select_n.202, bf16[1,4,96,1920]{3,2,1,0:T(8,128)(2,1)S(1)} %bitcast.197, bf16[1,4,96,1920]{3,2,1,0:T(8,128)(2,1)S(1)} %copy-done.6, ...), kind=kLoop, calls=%fused_computation.77 | loop fusion | flops 44236800 | bytes 29491204 | tf_op jit(solution)/shard_map/stack | solution.py:74
  269.0 5.7 %select_bitcast_fusion = bf16[4,1,4,96,1920]{4,3,0,2,1:T(8,128)(2,1)} fusion(bf16[4,4,96,1920]{3,2,1,0:T(8,128)(2,1)} %get-tuple-element.24, bf16[4,4,96,1920]{3,2,1,0:T(8,128)(2,1)S(1)} %get-tuple-element.23, pred[]{:T(512)S(6)} %eq.21), kind=kLoop, calls=%fused_computation.76 | loop fusion | flops 2949120 | bytes 17694720 | tf_op jit(solution)/shard_map/stack | solution.py:74
  274.8 6.0 %pad_maximum_fusion.1 = bf16[4,2,4,96,1920]{4,3,0,2,1:T(8,128)(2,1)S(1)} fusion(bf16[4,1,4,96,1920]{4,3,0,2,1:T(8,128)(2,1)} %select_bitcast_fusion, bf16[4,1,4,96,1920]{4,3,0,2,1:T(8,128)(2,1)} %get-tuple-element.22), kind=kLoop, calls=%fused_computation.37 | loop fusion | flops 5898240 | bytes 23592960 | tf_op jit(solution)/shard_map/stack | solution.py:74
  280.8 5.4 %copy.27 = bf16[4,2,4,96,1920]{4,3,2,1,0:T(8,128)(2,1)} copy(bf16[4,2,4,96,1920]{4,3,0,2,1:T(8,128)(2,1)S(1)} %pad_maximum_fusion.1) | data formatting | bytes 23592960 | tf_op jit(solution)/shard_map/stack | solution.py:74
  286.2 6.7 %shard_map.141 = f32[768,384]{1,0:T(8,128)} custom-call(bf16[768,3072]{1,0:T(8,128)(2,1)} %fusion.2.rows_ref, bf16[3072,1920]{1,0:T(8,128)(2,1)} %bitcast.171), custom_call_target="tpu_custom_call" | custom-call | flops 1811939328 | bytes 8257536 | tf_op jit(solution)/shard_map/pallas_call | solution.py:89
  303.5 5.3 convolution_convert_fusion.5
  333.6 12.2 %collective-permute-done.33 = bf16[256,1536]{1,0:T(8,128)(2,1)S(1)} collective-permute-done((bf16[256,1536]{1,0:T(8,128)(2,1)S(1)}, bf16[256,1536]{1,0:T(8,128)(2,1)S(1)}, u32[]{:S(2)}, u32[]{:S(2)}) %collective-permute-start.33) | collective-permute-done | bytes 786464 | tf_op jit(solution)/shard_map/ppermute | solution.py:80
  359.2 30.3 %collective-permute-done.37 = bf16[512,3072]{1,0:T(8,128)(2,1)S(1)} collective-permute-done((bf16[512,3072]{1,0:T(8,128)(2,1)S(1)}, bf16[512,3072]{1,0:T(8,128)(2,1)S(1)}, u32[]{:S(2)}, u32[]{:S(2)}) %collective-permute-start.37) | collective-permute-done | bytes 3145760 | tf_op jit(solution)/shard_map/ppermute | solution.py:18
  392.4 7.2 %shard_map.142 = f32[512,768]{1,0:T(8,128)} custom-call(bf16[512,3072]{1,0:T(8,128)(2,1)} %broadcast_select_fusion.rows_ref, bf16[3072,1920]{1,0:T(8,128)(2,1)} %bitcast.173), custom_call_target="tpu_custom_call" | custom-call | flops 2415919104 | bytes 9437184 | tf_op jit(solution)/shard_map/pallas_call | solution.py:89
  408.5 5.5 %all-reduce.1 = (f32[2,256,1]{1,0,2:T(2,128)S(1)}, f32[2,256,1]{1,0,2:T(2,128)S(1)}) all-reduce(f32[2,256,1]{1,0,2:T(2,128)S(1)} %broadcast_in_dim.53, f32[2,256,1]{1,0,2:T(2,128)S(1)} %broadcast_in_dim.52), channel_id=1, replica_groups=mesh['ctl'=32,'side'=2,'tp'=2] {'tp'}, use_global_device_ids=true, to_apply=%region_13.16 | all-reduce | flops 1024 | bytes 8192 | tf_op jit(solution)/shard_map/psum | solution.py:251
  423.5 5.3 all-reduce
  432.7 6.4 %collective-permute-start.40 = (bf16[512,1536]{1,0:T(8,128)(2,1)}, bf16[512,1536]{1,0:T(8,128)(2,1)}, u32[]{:S(2)}, u32[]{:S(2)}) collective-permute-start(bf16[512,1536]{1,0:T(8,128)(2,1)} %multiply_convert_fusion), channel_id=1, source_target_pairs={{2,0},{3,1},{6,4},{7,5},{10,8},{11,9},{14,12},{15,13},{18,16},{19,... | collective-permute-start | bytes 4718600 | tf_op jit(solution)/shard_map/ppermute | solution.py:18
  442.4 5.8 %convolution_convert_fusion = bf16[1536,1536]{1,0:T(8,128)(2,1)} fusion(bf16[512,1536]{0,1:T(8,128)(2,1)S(1)} %bitcast.208, bf16[512,1536]{1,0:T(8,128)(2,1)} %collective-permute-done.40, bf16[512,1536]{1,0:T(8,128)(2,1)} %multiply_convert_fusion, pred[]{:T(512)S(6)} %eq.19), kind=kOutput, calls=%fused_computation.46 | convolution fusion | flops 2419064832 | bytes 9437185 | tf_op jit(solution)/shard_map/dot_general | solution.py:292
  448.2 10.1 %all-to-all-start = ((bf16[32,48,1536]{2,1,0:T(8,128)(2,1)}), bf16[32,48,1536]{2,1,0:T(8,128)(2,1)}, u32[]{:S(2)}, u32[]{:S(2)}) async-start(bf16[32,48,1536]{2,1,0:T(8,128)(2,1)} %bitcast.189), calls=%async_computation | async-start | bytes 9437184 | tf_op jit(solution)/shard_map/all_to_all | solution.py:296
  463.0 71.2 %all-to-all-done = bf16[32,48,1536]{2,1,0:T(8,128)(2,1)} async-done(((bf16[32,48,1536]{2,1,0:T(8,128)(2,1)}), bf16[32,48,1536]{2,1,0:T(8,128)(2,1)}, u32[]{:S(2)}, u32[]{:S(2)}) %all-to-all-start) | async-done | bytes 4718624 | tf_op jit(solution)/shard_map/all_to_all | solution.py:296
  (294 shorter events, 225.6 us)
Async XLA Ops:
  3.8 36.1 %collective-permute-start = (bf16[96,1920]{1,0:T(8,128)(2,1)}, bf16[96,1920]{1,0:T(8,128)(2,1)}, u32[]{:S(2)}, u32[]{:S(2)}) collective-permute-start(bf16[96,1920]{1,0:T(8,128)(2,1)} %get-tuple-element.42), channel_id=1, source_target_pairs={{0,12},{4,0},{8,4},{12,8},{16,28},{20,16},{24,20},{28,24},{32,44},... | collective-permute-start | bytes 1105928 | tf_op jit(solution)/shard_map/ppermute | solution.py:42
  4.1 39.2 %collective-permute-start.2 = (bf16[96,1920]{1,0:T(8,128)(2,1)}, bf16[96,1920]{1,0:T(8,128)(2,1)}, u32[]{:S(2)}, u32[]{:S(2)}) collective-permute-start(bf16[96,1920]{1,0:T(8,128)(2,1)} %get-tuple-element.42), channel_id=1, source_target_pairs={{0,4},{4,8},{8,12},{12,0},{16,20},{20,24},{24,28},{28,16},{32,36},... | collective-permute-start | bytes 1105928 | tf_op jit(solution)/shard_map/ppermute | solution.py:42
  8.3 50.5 %collective-permute-start.8 = (bf16[96,3840]{1,0:T(8,128)(2,1)}, bf16[96,3840]{1,0:T(8,128)(2,1)}, u32[]{:S(2)}, u32[]{:S(2)}) collective-permute-start(bf16[96,3840]{1,0:T(8,128)(2,1)} %pad_maximum_fusion.5), channel_id=1, source_target_pairs={{0,16},{4,20},{8,24},{12,28},{16,0},{20,4},{24,8},{28,12},{32,48},... | collective-permute-start | bytes 2211848 | tf_op jit(solution)/shard_map/ppermute | solution.py:42
  11.9 37.5 %collective-permute-start.17 = (bf16[96,1920]{1,0:T(8,128)(2,1)}, bf16[96,1920]{1,0:T(8,128)(2,1)}, u32[]{:S(2)}, u32[]{:S(2)}) collective-permute-start(bf16[96,1920]{1,0:T(8,128)(2,1)} %get-tuple-element.40), channel_id=1, source_target_pairs={{0,96},{4,100},{8,104},{12,108},{16,112},{20,116},{24,120},{28,124... | collective-permute-start | bytes 1105928 | tf_op jit(solution)/shard_map/ppermute | solution.py:42
  12.0 38.5 %collective-permute-start.19 = (bf16[96,1920]{1,0:T(8,128)(2,1)}, bf16[96,1920]{1,0:T(8,128)(2,1)}, u32[]{:S(2)}, u32[]{:S(2)}) collective-permute-start(bf16[96,1920]{1,0:T(8,128)(2,1)} %get-tuple-element.40), channel_id=1, source_target_pairs={{0,32},{4,36},{8,40},{12,44},{16,48},{20,52},{24,56},{28,60},{32,6... | collective-permute-start | bytes 1105928 | tf_op jit(solution)/shard_map/ppermute | solution.py:42
  58.7 65.6 %collective-permute-start.4 = (bf16[4,96,1920]{2,1,0:T(8,128)(2,1)}, bf16[4,96,1920]{2,1,0:T(8,128)(2,1)S(1)}, u32[]{:S(2)}, u32[]{:S(2)}) collective-permute-start(bf16[4,96,1920]{2,1,0:T(8,128)(2,1)} %fusion.73), channel_id=1, source_target_pairs={{0,96},{4,100},{8,104},{12,108},{16,112},{20,116},{24,120},{28,124... | collective-permute-start | bytes 4423688 | tf_op jit(solution)/shard_map/ppermute | solution.py:42
  63.7 35.3 %collective-permute-start.25 = (bf16[96,1920]{1,0:T(8,128)(2,1)S(1)}, bf16[96,1920]{1,0:T(8,128)(2,1)}, u32[]{:S(2)}, u32[]{:S(2)}) collective-permute-start(bf16[96,1920]{1,0:T(8,128)(2,1)S(1)} %get-tuple-element.39), channel_id=1, source_target_pairs={{0,96},{4,100},{8,104},{12,108},{16,112},{20,116},{24,120},{28,124... | collective-permute-start | bytes 1105928 | tf_op jit(solution)/shard_map/ppermute | solution.py:42
  65.7 36.1 %collective-permute-start.27 = (bf16[96,1920]{1,0:T(8,128)(2,1)S(1)}, bf16[96,1920]{1,0:T(8,128)(2,1)}, u32[]{:S(2)}, u32[]{:S(2)}) collective-permute-start(bf16[96,1920]{1,0:T(8,128)(2,1)S(1)} %get-tuple-element.39), channel_id=1, source_target_pairs={{0,32},{4,36},{8,40},{12,44},{16,48},{20,52},{24,56},{28,60},{32,6... | collective-permute-start | bytes 1105928 | tf_op jit(solution)/shard_map/ppermute | solution.py:42
  70.2 59.3 %collective-permute-start.6 = (bf16[4,96,1920]{2,1,0:T(8,128)(2,1)}, bf16[4,96,1920]{2,1,0:T(8,128)(2,1)}, u32[]{:S(2)}, u32[]{:S(2)}) collective-permute-start(bf16[4,96,1920]{2,1,0:T(8,128)(2,1)} %fusion.73), channel_id=1, source_target_pairs={{0,32},{4,36},{8,40},{12,44},{16,48},{20,52},{24,56},{28,60},{32,6... | collective-permute-start | bytes 4423688 | tf_op jit(solution)/shard_map/ppermute | solution.py:42
  73.6 56.7 %collective-permute-start.21 = (bf16[4,96,1920]{2,1,0:T(8,128)(2,1)}, bf16[4,96,1920]{2,1,0:T(8,128)(2,1)S(1)}, u32[]{:S(2)}, u32[]{:S(2)}) collective-permute-start(bf16[4,96,1920]{2,1,0:T(8,128)(2,1)} %fusion.59), channel_id=1, source_target_pairs={{0,12},{4,0},{8,4},{12,8},{16,28},{20,16},{24,20},{28,24},{32,44},... | collective-permute-start | bytes 4423688 | tf_op jit(solution)/shard_map/ppermute | solution.py:42
  111.9 31.3 %collective-permute-start.23 = (bf16[4,96,1920]{2,1,0:T(8,128)(2,1)}, bf16[4,96,1920]{2,1,0:T(8,128)(2,1)S(1)}, u32[]{:S(2)}, u32[]{:S(2)}) collective-permute-start(bf16[4,96,1920]{2,1,0:T(8,128)(2,1)} %fusion.59), channel_id=1, source_target_pairs={{0,4},{4,8},{8,12},{12,0},{16,20},{20,24},{24,28},{28,16},{32,36},... | collective-permute-start | bytes 4423688 | tf_op jit(solution)/shard_map/ppermute | solution.py:42
  124.2 26.8 %collective-permute-start.13 = (bf16[4,96,1920]{2,1,0:T(8,128)(2,1)S(1)}, bf16[4,96,1920]{2,1,0:T(8,128)(2,1)S(1)}, u32[]{:S(2)}, u32[]{:S(2)}) collective-permute-start(bf16[4,96,1920]{2,1,0:T(8,128)(2,1)S(1)} %fusion.66), channel_id=1, source_target_pairs={{0,96},{4,100},{8,104},{12,108},{16,112},{20,116},{24,120},{28,124... | collective-permute-start | bytes 4423688 | tf_op jit(solution)/shard_map/ppermute | solution.py:42
  124.3 30.6 %collective-permute-start.15 = (bf16[4,96,1920]{2,1,0:T(8,128)(2,1)S(1)}, bf16[4,96,1920]{2,1,0:T(8,128)(2,1)S(1)}, u32[]{:S(2)}, u32[]{:S(2)}) collective-permute-start(bf16[4,96,1920]{2,1,0:T(8,128)(2,1)S(1)} %fusion.66), channel_id=1, source_target_pairs={{0,32},{4,36},{8,40},{12,44},{16,48},{20,52},{24,56},{28,60},{32,6... | collective-permute-start | bytes 4423688 | tf_op jit(solution)/shard_map/ppermute | solution.py:42
  129.6 41.1 %collective-permute-start.29 = (bf16[4,96,1920]{2,1,0:T(8,128)(2,1)S(1)}, bf16[4,96,1920]{2,1,0:T(8,128)(2,1)S(1)}, u32[]{:S(2)}, u32[]{:S(2)}) collective-permute-start(bf16[4,96,1920]{2,1,0:T(8,128)(2,1)S(1)} %fusion.52), channel_id=1, source_target_pairs={{0,12},{4,0},{8,4},{12,8},{16,28},{20,16},{24,20},{28,24},{32,44},... | collective-permute-start | bytes 4423688 | tf_op jit(solution)/shard_map/ppermute | solution.py:42
  130.3 44.4 %collective-permute-start.31 = (bf16[4,96,1920]{2,1,0:T(8,128)(2,1)S(1)}, bf16[4,96,1920]{2,1,0:T(8,128)(2,1)S(1)}, u32[]{:S(2)}, u32[]{:S(2)}) collective-permute-start(bf16[4,96,1920]{2,1,0:T(8,128)(2,1)S(1)} %fusion.52), channel_id=1, source_target_pairs={{0,4},{4,8},{8,12},{12,0},{16,20},{20,24},{24,28},{28,16},{32,36},... | collective-permute-start | bytes 4423688 | tf_op jit(solution)/shard_map/ppermute | solution.py:42
  143.2 23.1 %collective-permute-start.5 = (bf16[2,96,1920]{2,1,0:T(8,128)(2,1)S(1)}, bf16[2,96,1920]{2,1,0:T(8,128)(2,1)S(1)}, u32[]{:S(2)}, u32[]{:S(2)}) collective-permute-start(bf16[2,96,1920]{2,1,0:T(8,128)(2,1)S(1)} %slice.179), channel_id=1, source_target_pairs={{0,96},{4,100},{8,104},{12,108},{16,112},{20,116},{24,120},{28,124... | collective-permute-start | bytes 2211848 | tf_op jit(solution)/shard_map/ppermute | solution.py:42
  151.0 31.5 %collective-permute-start.7 = (bf16[2,96,1920]{2,1,0:T(8,128)(2,1)S(1)}, bf16[2,96,1920]{2,1,0:T(8,128)(2,1)S(1)}, u32[]{:S(2)}, u32[]{:S(2)}) collective-permute-start(bf16[2,96,1920]{2,1,0:T(8,128)(2,1)S(1)} %slice.180), channel_id=1, source_target_pairs={{0,32},{4,36},{8,40},{12,44},{16,48},{20,52},{24,56},{28,60},{32,6... | collective-permute-start | bytes 2211848 | tf_op jit(solution)/shard_map/ppermute | solution.py:42
  154.9 30.3 %collective-permute-start.22 = (bf16[2,96,1920]{2,1,0:T(8,128)(2,1)S(1)}, bf16[2,96,1920]{2,1,0:T(8,128)(2,1)S(1)}, u32[]{:S(2)}, u32[]{:S(2)}) collective-permute-start(bf16[2,96,1920]{2,1,0:T(8,128)(2,1)S(1)} %slice.190), channel_id=1, source_target_pairs={{0,12},{4,0},{8,4},{12,8},{16,28},{20,16},{24,20},{28,24},{32,44},... | collective-permute-start | bytes 2211848 | tf_op jit(solution)/shard_map/ppermute | solution.py:42
  166.3 24.3 %collective-permute-start.24 = (bf16[2,96,1920]{2,1,0:T(8,128)(2,1)S(1)}, bf16[2,96,1920]{2,1,0:T(8,128)(2,1)S(1)}, u32[]{:S(2)}, u32[]{:S(2)}) collective-permute-start(bf16[2,96,1920]{2,1,0:T(8,128)(2,1)S(1)} %slice.191), channel_id=1, source_target_pairs={{0,4},{4,8},{8,12},{12,0},{16,20},{20,24},{24,28},{28,16},{32,36},... | collective-permute-start | bytes 2211848 | tf_op jit(solution)/shard_map/ppermute | solution.py:42
  182.6 68.4 %collective-permute-start.30 = (bf16[2,96,1920]{2,1,0:T(8,128)(2,1)}, bf16[2,96,1920]{2,1,0:T(8,128)(2,1)}, u32[]{:S(2)}, u32[]{:S(2)}) collective-permute-start(bf16[2,96,1920]{2,1,0:T(8,128)(2,1)} %slice.195), channel_id=1, source_target_pairs={{0,12},{4,0},{8,4},{12,8},{16,28},{20,16},{24,20},{28,24},{32,44},... | collective-permute-start | bytes 2211848 | tf_op jit(solution)/shard_map/ppermute | solution.py:42
  185.2 65.7 %collective-permute-start.32 = (bf16[2,96,1920]{2,1,0:T(8,128)(2,1)}, bf16[2,96,1920]{2,1,0:T(8,128)(2,1)}, u32[]{:S(2)}, u32[]{:S(2)}) collective-permute-start(bf16[2,96,1920]{2,1,0:T(8,128)(2,1)} %slice.196), channel_id=1, source_target_pairs={{0,4},{4,8},{8,12},{12,0},{16,20},{20,24},{24,28},{28,16},{32,36},... | collective-permute-start | bytes 2211848 | tf_op jit(solution)/shard_map/ppermute | solution.py:42
  312.3 21.3 %collective-permute-start.35 = (bf16[256,1536]{1,0:T(8,128)(2,1)}, bf16[256,1536]{1,0:T(8,128)(2,1)}, u32[]{:S(2)}, u32[]{:S(2)}) collective-permute-start(bf16[256,1536]{1,0:T(8,128)(2,1)} %convolution_convert_fusion.1), channel_id=1, source_target_pairs={{0,1},{1,0},{2,3},{3,2},{4,5},{5,4},{6,7},{7,6},{8,9},{9,8},{10,11... | collective-permute-start | bytes 2359304 | tf_op jit(solution)/shard_map/ppermute | solution.py:80
  357.9 31.6 %collective-permute-start.37 = (bf16[512,3072]{1,0:T(8,128)(2,1)S(1)}, bf16[512,3072]{1,0:T(8,128)(2,1)S(1)}, u32[]{:S(2)}, u32[]{:S(2)}) collective-permute-start(bf16[512,3072]{1,0:T(8,128)(2,1)S(1)} %pad_maximum_fusion.3), channel_id=1, source_target_pairs={{0,2},{1,3},{4,6},{5,7},{8,10},{9,11},{12,14},{13,15},{16,18},{17,... | collective-permute-start | bytes 9437192 | tf_op jit(solution)/shard_map/ppermute | solution.py:18
  448.2 86.0 %all-to-all-start = ((bf16[32,48,1536]{2,1,0:T(8,128)(2,1)}), bf16[32,48,1536]{2,1,0:T(8,128)(2,1)}, u32[]{:S(2)}, u32[]{:S(2)}) async-start(bf16[32,48,1536]{2,1,0:T(8,128)(2,1)} %bitcast.189), calls=%async_computation | async-start | bytes 9437184 | tf_op jit(solution)/shard_map/all_to_all | solution.py:296
  (69 other events, 632.5 us)

commit v10 on v7

--- a/solution.py
+++ b/solution.py
@@ -141,9 +141,11 @@
     quarter_width = half_width // 2
     flat_rows = micro_count * img_rows
     block_rows = width_full // (2 * ctl_count)
-    aligned = jax.vmap(lambda latent, order_row: jnp.take(latent, order_row, axis=0))(
-        control_latent, control_order
-    )
+    token_ids = lax.broadcasted_iota(jnp.int32, (micro_count, img_rows, img_rows), 2)
+    picks = (control_order[:, :, None] == token_ids).astype(jnp.bfloat16)
+    aligned = jnp.einsum(
+        "bij,bjd->bid", picks, control_latent, preferred_element_type=jnp.float32
+    ).astype(jnp.bfloat16)
     plain_rows = image_latent.astype(jnp.float32)
     hidden = plain_rows + jnp.where(is_control, 1.0, 0.0) * aligned.astype(jnp.float32)
     chosen = jnp.take(captions, caption_ids, axis=0).astype(jnp.float32)

time: 519 us -> 506 us (0.975)
  local copies, waits for them, and re-layouts: 113 us -> 94.8 us
    gather x1 -> x0, local copies, waits for them, and re-layouts: 14.7 us -> none  [local(): jnp.take(latent, order_row, axis=0)]
    ppermute x17, waiting for transfers between devices: 74.4 us -> 79.8 us  [ctl_shift(): return lax.ppermute(value, 'ctl', pairs)]
    unnamed x94 -> x87, local copies, waits for them, and re-layouts: 32.8 us -> 30.6 us
    unnamed x10 -> x9, other arithmetic: 28.3 us -> 28.4 us
  transfers between devices with their start and end apart: 26 -> 26, of which waited for: 10 -> 10; matrix products, arithmetic and copies ran while one was open for 25% -> 22% of each run, Pallas kernels for 3% -> 3%
where the time goes in v10:
time: 506 us; the launch traced here: 497 us
  waiting for transfers between devices  197 us (39%)
  local copies, waits for them, and re-layouts  94.8 us (19%)
  other arithmetic  79.7 us (16%)
  starting transfers between devices  46.8 us (9%)
  matrix products  34.6 us (7%)
  Pallas kernels  31 us (6%)
  blocking collectives  10.7 us (2%)
    ppermute x17, waiting for transfers between devices, ctl_shift(): return lax.ppermute(value, 'ctl', pairs)  79.8 us
    all_to_all x1, waiting for transfers between devices, local(): received = lax.all_to_all(group_parts, 'ctl', 0, 0, tiled=True)  70.9 us
    pallas_call x3, Pallas kernels, block_matmul(): pl.pallas_call(kernel, grid=(block_count,), in_specs=[pl.BlockSpec((row_c...  31 us
    unnamed x87, local copies, waits for them, and re-layouts  30.6 us
    ppermute x2, waiting for transfers between devices, passed_along(): return lax.ppermute(shard, axis, pairs)  28.8 us
    unnamed x9, other arithmetic  28.4 us
    ppermute x17, starting transfers between devices, ctl_shift(): return lax.ppermute(value, 'ctl', pairs)  22.7 us
    ppermute x3, waiting for transfers between devices, swap(): return lax.ppermute(value, axis, [(0, 1), (1, 0)])  15.6 us
  transfers between devices with their start and end apart: 26, of which 10 were waited for; matrix products, arithmetic and copies ran while one was open for 22% of the time, Pallas kernels for 3%

profile of v10, /device:TPU:5, one launch (start us, length us, event | category | flops | bytes accessed | tf_op | source)
XLA Modules:
  0.0 496.5 jit_solution(15840305272132927760)
XLA Ops:
  7.9 16.4 %collective-permute-done = bf16[96,3840]{1,0:T(8,128)(2,1)} collective-permute-done((bf16[96,3840]{1,0:T(8,128)(2,1)}, bf16[96,3840]{1,0:T(8,128)(2,1)}, u32[]{:S(2)}, u32[]{:S(2)}) %collective-permute-start) | collective-permute-done | bytes 737312 | tf_op jit(solution)/shard_map/ppermute | solution.py:42
  36.1 9.0 %collective-permute-done.1 = bf16[2,96,1920]{2,1,0:T(8,128)(2,1)} collective-permute-done((bf16[2,96,1920]{2,1,0:T(8,128)(2,1)}, bf16[2,96,1920]{2,1,0:T(8,128)(2,1)}, u32[]{:S(2)}, u32[]{:S(2)}) %collective-permute-start.1) | collective-permute-done | bytes 737312 | tf_op jit(solution)/shard_map/ppermute | solution.py:42
  58.0 6.7 %bitcast_dynamic-update-slice_fusion = (bf16[8,2,4,96,1920]{4,3,1,2,0:T(8,128)(2,1)}, bf16[4,2,96,1920]{3,2,1,0:T(8,128)(2,1)S(1)}) fusion(s32[]{:T(128)S(6)} %select_n.175, bf16[1,2,96,1920]{3,2,1,0:T(8,128)(2,1)} %bitcast.14, bf16[1,2,96,1920]{3,2,1,0:T(8,128)(2,1)S(1)} %maximum_bitcast_fusion.2, bf16[1,2,96,1920]{3,2,1,0:T(8,128)(2,1)} %bitcast.12, ...), kind=kLoop, calls=%fused_computation.60 | loop fusion | flops 23592960 | bytes 8847364
  67.5 7.2 %bitcast_dynamic-update-slice_fusion.6 = (bf16[8,4,2,96,1920]{4,3,2,1,0:T(8,128)(2,1)}, bf16[4,2,96,1920]{3,2,1,0:T(8,128)(2,1)}) fusion(s32[]{:T(128)S(6)} %select_n.159, bf16[1,2,96,1920]{3,2,1,0:T(8,128)(2,1)} %bitcast.25, bf16[1,2,96,1920]{3,2,1,0:T(8,128)(2,1)S(1)} %maximum_bitcast_fusion.3, bf16[1,2,96,1920]{3,2,1,0:T(8,128)(2,1)} %bitcast.23, ...), kind=kLoop, calls=%fused_computation.66 | loop fusion | flops 23592960 | bytes 8847364
  83.0 44.6 %collective-permute-done.5 = bf16[2,4,96,1920]{3,2,0,1:T(8,128)(2,1)S(1)} collective-permute-done((bf16[2,4,96,1920]{3,2,0,1:T(8,128)(2,1)S(1)}, bf16[2,4,96,1920]{3,2,0,1:T(8,128)(2,1)S(1)}, u32[]{:S(2)}, u32[]{:S(2)}) %collective-permute-start.5) | collective-permute-done | bytes 2949152 | tf_op jit(solution)/shard_map/ppermute | solution.py:42
  135.3 8.0 %fusion.2.rows_ref = bf16[768,3072]{1,0:T(8,128)(2,1)} fusion(f32[2,384,3072]{2,1,0:T(8,128)} %get-tuple-element.23, f32[2,3072]{1,0:T(2,128)S(1)} %get-tuple-element.40, f32[2,3072]{1,0:T(2,128)S(1)} %get-tuple-element.41, f32[768]{0:T(1024)S(1)} %rsqrt.47, f32[768]{0:T(1024)S(1)} %div.70), kind=kLoop, calls=%fused_computation.6 | loop fusion | flops 11796480 | bytes 14211072 | tf_op jit(solution)/shard_map/convert_element_type | solution.py:154
  160.3 6.1 %collective-permute-done.8 = bf16[1,4,96,1920]{3,2,0,1:T(8,128)(2,1)} collective-permute-done((bf16[1,4,96,1920]{3,2,0,1:T(8,128)(2,1)}, bf16[1,4,96,1920]{3,2,0,1:T(8,128)(2,1)}, u32[]{:S(2)}, u32[]{:S(2)}) %collective-permute-start.8) | collective-permute-done | bytes 1474592 | tf_op jit(solution)/shard_map/ppermute | solution.py:42
  182.1 6.3 %constant_dynamic-slice_fusion.3 = bf16[4,2,4,96,1920]{4,3,1,2,0:T(8,128)(2,1)S(1)} fusion(bf16[8,2,4,96,1920]{4,3,1,2,0:T(8,128)(2,1)} %bitcast_dynamic-update-slice_fusion.9, s32[]{:T(128)S(6)} %select_n.159), kind=kLoop, calls=%fused_computation.152 | loop fusion | bytes 23592964 | tf_op jit(solution)/shard_map/jit(_roll_dynamic)/dynamic_slice | solution.py:54
  188.4 5.3 %copy.24 = bf16[4,2,4,96,1920]{4,3,2,1,0:T(8,128)(2,1)} copy(bf16[4,2,4,96,1920]{4,3,1,2,0:T(8,128)(2,1)S(1)} %constant_dynamic-slice_fusion.3) | data formatting | bytes 23592960 | tf_op jit(solution)/shard_map/jit(_roll_dynamic)/dynamic_slice | solution.py:54
  193.7 17.2 %shard_map.140 = f32[768,1920]{1,0:T(8,128)} custom-call(bf16[768,3072]{1,0:T(8,128)(2,1)} %fusion.2.rows_ref, bf16[3072,1920]{1,0:T(8,128)(2,1)} %bitcast.156), custom_call_target="tpu_custom_call" | custom-call | flops 9059696640 | bytes 22413312 | tf_op jit(solution)/shard_map/pallas_call | solution.py:81
  240.1 6.1 %dynamic-slice_bitcast_fusion = bf16[4,2,4,96,1920]{4,3,1,0,2:T(8,128)(2,1)S(1)} fusion(bf16[8,4,2,96,1920]{4,3,2,1,0:T(8,128)(2,1)} %bitcast_dynamic-update-slice_fusion.3, s32[]{:T(128)S(6)} %select_n.175), kind=kLoop, calls=%fused_computation.3 | loop fusion | bytes 23592964 | tf_op jit(solution)/shard_map/transpose | solution.py:67
  246.2 5.2 %copy.25 = bf16[4,2,4,96,1920]{4,3,2,1,0:T(8,128)(2,1)} copy(bf16[4,2,4,96,1920]{4,3,1,0,2:T(8,128)(2,1)S(1)} %dynamic-slice_bitcast_fusion) | data formatting | bytes 23592960 | tf_op jit(solution)/shard_map/transpose | solution.py:67
  251.5 6.7 %shard_map.141 = f32[768,384]{1,0:T(8,128)} custom-call(bf16[768,3072]{1,0:T(8,128)(2,1)} %fusion.2.rows_ref, bf16[3072,1920]{1,0:T(8,128)(2,1)} %bitcast.152), custom_call_target="tpu_custom_call" | custom-call | flops 1811939328 | bytes 8257536 | tf_op jit(solution)/shard_map/pallas_call | solution.py:81
  266.6 5.3 %convolution_convert_fusion.6 = bf16[6,128,256]{2,1,0:T(8,128)(2,1)S(1)} fusion(bf16[384,6,128]{0,2,1:T(8,128)(2,1)S(1)} %bitcast.178, f32[6,256]{1,0:T(8,128)S(1)} %fusion.92, f32[6,256,384]{2,1,0:T(8,128)} %copy-done.19), kind=kOutput, calls=%fused_computation.106 | convolution fusion | flops 154142592 | bytes 3348480 | tf_op jit(solution)/shard_map/hij,jhd->ihd/dot_general | solution.py:206
  282.4 5.3 %convolution_convert_fusion.7 = bf16[6,128,256]{2,1,0:T(8,128)(2,1)S(1)} fusion(bf16[384,6,128]{0,2,1:T(8,128)(2,1)S(1)} %bitcast.179, f32[6,256]{1,0:T(8,128)S(1)} %fusion.91, f32[6,256,384]{2,1,0:T(8,128)} %copy-done.20), kind=kOutput, calls=%fused_computation.107 | convolution fusion | flops 154142592 | bytes 3348480 | tf_op jit(solution)/shard_map/hij,jhd->ihd/dot_general | solution.py:206
  296.4 13.0 %collective-permute-done.17 = bf16[256,1536]{1,0:T(8,128)(2,1)S(1)} collective-permute-done((bf16[256,1536]{1,0:T(8,128)(2,1)S(1)}, bf16[256,1536]{1,0:T(8,128)(2,1)S(1)}, u32[]{:S(2)}, u32[]{:S(2)}) %collective-permute-start.17) | collective-permute-done | bytes 786464 | tf_op jit(solution)/shard_map/ppermute | solution.py:72
  323.0 28.8 %collective-permute-done.21 = bf16[512,3072]{1,0:T(8,128)(2,1)S(1)} collective-permute-done((bf16[512,3072]{1,0:T(8,128)(2,1)S(1)}, bf16[512,3072]{1,0:T(8,128)(2,1)S(1)}, u32[]{:S(2)}, u32[]{:S(2)}) %collective-permute-start.21) | collective-permute-done | bytes 3145760 | tf_op jit(solution)/shard_map/ppermute | solution.py:18
  354.6 7.1 %shard_map.142 = f32[512,768]{1,0:T(8,128)} custom-call(bf16[512,3072]{1,0:T(8,128)(2,1)} %broadcast_select_fusion.rows_ref, bf16[3072,1920]{1,0:T(8,128)(2,1)} %bitcast.154), custom_call_target="tpu_custom_call" | custom-call | flops 2415919104 | bytes 9437184 | tf_op jit(solution)/shard_map/pallas_call | solution.py:81
  370.5 5.4 %all-reduce.1 = (f32[2,256,1]{1,0,2:T(2,128)S(1)}, f32[2,256,1]{1,0,2:T(2,128)S(1)}) all-reduce(f32[2,256,1]{1,0,2:T(2,128)S(1)} %broadcast_in_dim.39, f32[2,256,1]{1,0,2:T(2,128)S(1)} %broadcast_in_dim.38), channel_id=1, replica_groups=mesh['ctl'=32,'side'=2,'tp'=2] {'tp'}, use_global_device_ids=true, to_apply=%region_13.15 | all-reduce | flops 1024 | bytes 8192 | tf_op jit(solution)/shard_map/psum | solution.py:245
  385.4 5.3 %all-reduce = (f32[2,256,1]{1,0,2:T(2,128)S(1)}, f32[2,256,1]{1,0,2:T(2,128)S(1)}) all-reduce(f32[2,256,1]{1,0,2:T(2,128)S(1)} %broadcast_in_dim.41, f32[2,256,1]{1,0,2:T(2,128)S(1)} %broadcast_in_dim.40), channel_id=1, replica_groups=mesh['ctl'=32,'side'=2,'tp'=2] {'tp'}, use_global_device_ids=true, to_apply=%region_17.19 | all-reduce | flops 1024 | bytes 8192 | tf_op jit(solution)/shard_map/psum | solution.py:269
  394.6 6.7 %collective-permute-start.24 = (bf16[512,1536]{1,0:T(8,128)(2,1)}, bf16[512,1536]{1,0:T(8,128)(2,1)}, u32[]{:S(2)}, u32[]{:S(2)}) collective-permute-start(bf16[512,1536]{1,0:T(8,128)(2,1)} %multiply_convert_fusion), channel_id=1, source_target_pairs={{2,0},{3,1},{6,4},{7,5},{10,8},{11,9},{14,12},{15,13},{18,16},{19,... | collective-permute-start | bytes 4718600 | tf_op jit(solution)/shard_map/ppermute | solution.py:18
  404.6 5.7 %convolution_convert_fusion = bf16[1536,1536]{1,0:T(8,128)(2,1)} fusion(bf16[512,1536]{0,1:T(8,128)(2,1)S(1)} %bitcast.177, bf16[512,1536]{1,0:T(8,128)(2,1)} %collective-permute-done.24, bf16[512,1536]{1,0:T(8,128)(2,1)} %multiply_convert_fusion, pred[]{:T(512)S(6)} %eq.27), kind=kOutput, calls=%fused_computation.12 | convolution fusion | flops 2419064832 | bytes 9437185 | tf_op jit(solution)/shard_map/dot_general | solution.py:286
  410.3 6.4 %all-to-all-start = ((bf16[32,48,1536]{2,1,0:T(8,128)(2,1)}), bf16[32,48,1536]{2,1,0:T(8,128)(2,1)}, u32[]{:S(2)}, u32[]{:S(2)}) async-start(bf16[32,48,1536]{2,1,0:T(8,128)(2,1)} %bitcast.170), calls=%async_computation | async-start | bytes 9437184 | tf_op jit(solution)/shard_map/all_to_all | solution.py:290
  421.4 70.9 %all-to-all-done = bf16[32,48,1536]{2,1,0:T(8,128)(2,1)} async-done(((bf16[32,48,1536]{2,1,0:T(8,128)(2,1)}), bf16[32,48,1536]{2,1,0:T(8,128)(2,1)}, u32[]{:S(2)}, u32[]{:S(2)}) %all-to-all-start) | async-done | bytes 4718624 | tf_op jit(solution)/shard_map/all_to_all | solution.py:290
  (213 shorter events, 190.0 us)
Async XLA Ops:
  6.2 18.0 %collective-permute-start = (bf16[96,3840]{1,0:T(8,128)(2,1)}, bf16[96,3840]{1,0:T(8,128)(2,1)}, u32[]{:S(2)}, u32[]{:S(2)}) collective-permute-start(bf16[96,3840]{1,0:T(8,128)(2,1)} %get-tuple-element.38), channel_id=1, source_target_pairs={{0,16},{4,20},{8,24},{12,28},{16,0},{20,4},{24,8},{28,12},{32,48},... | collective-permute-start | bytes 2211848 | tf_op jit(solution)/shard_map/ppermute | solution.py:42
  28.2 17.0 %collective-permute-start.1 = (bf16[2,96,1920]{2,1,0:T(8,128)(2,1)}, bf16[2,96,1920]{2,1,0:T(8,128)(2,1)}, u32[]{:S(2)}, u32[]{:S(2)}) collective-permute-start(bf16[2,96,1920]{2,1,0:T(8,128)(2,1)} %get-tuple-element.34), channel_id=1, source_target_pairs={{0,12},{4,0},{8,4},{12,8},{16,28},{20,16},{24,20},{28,24},{32,44},... | collective-permute-start | bytes 2211848 | tf_op jit(solution)/shard_map/ppermute | solution.py:42
  28.4 18.1 %collective-permute-start.3 = (bf16[2,96,1920]{2,1,0:T(8,128)(2,1)}, bf16[2,96,1920]{2,1,0:T(8,128)(2,1)}, u32[]{:S(2)}, u32[]{:S(2)}) collective-permute-start(bf16[2,96,1920]{2,1,0:T(8,128)(2,1)} %get-tuple-element.34), channel_id=1, source_target_pairs={{0,4},{4,8},{8,12},{12,0},{16,20},{20,24},{24,28},{28,16},{32,36},... | collective-permute-start | bytes 2211848 | tf_op jit(solution)/shard_map/ppermute | solution.py:42
  29.6 22.9 %collective-permute-start.9 = (bf16[2,96,1920]{2,1,0:T(8,128)(2,1)}, bf16[2,96,1920]{2,1,0:T(8,128)(2,1)}, u32[]{:S(2)}, u32[]{:S(2)}) collective-permute-start(bf16[2,96,1920]{2,1,0:T(8,128)(2,1)} %get-tuple-element.33), channel_id=1, source_target_pairs={{0,96},{4,100},{8,104},{12,108},{16,112},{20,116},{24,120},{28,124... | collective-permute-start | bytes 2211848 | tf_op jit(solution)/shard_map/ppermute | solution.py:42
  32.4 24.4 %collective-permute-start.11 = (bf16[2,96,1920]{2,1,0:T(8,128)(2,1)}, bf16[2,96,1920]{2,1,0:T(8,128)(2,1)}, u32[]{:S(2)}, u32[]{:S(2)}) collective-permute-start(bf16[2,96,1920]{2,1,0:T(8,128)(2,1)} %get-tuple-element.33), channel_id=1, source_target_pairs={{0,32},{4,36},{8,40},{12,44},{16,48},{20,52},{24,56},{28,60},{32,6... | collective-permute-start | bytes 2211848 | tf_op jit(solution)/shard_map/ppermute | solution.py:42
  46.2 11.7 %collective-permute-start.2 = (bf16[1,96,1920]{2,1,0:T(8,128)(2,1)S(1)}, bf16[1,96,1920]{2,1,0:T(8,128)(2,1)S(1)}, u32[]{:S(2)}, u32[]{:S(2)}) collective-permute-start(bf16[1,96,1920]{2,1,0:T(8,128)(2,1)S(1)} %slice.135), channel_id=1, source_target_pairs={{0,12},{4,0},{8,4},{12,8},{16,28},{20,16},{24,20},{28,24},{32,44},... | collective-permute-start | bytes 1105928 | tf_op jit(solution)/shard_map/ppermute | solution.py:42
  47.5 10.4 %collective-permute-start.4 = (bf16[1,96,1920]{2,1,0:T(8,128)(2,1)S(1)}, bf16[1,96,1920]{2,1,0:T(8,128)(2,1)S(1)}, u32[]{:S(2)}, u32[]{:S(2)}) collective-permute-start(bf16[1,96,1920]{2,1,0:T(8,128)(2,1)S(1)} %slice.136), channel_id=1, source_target_pairs={{0,4},{4,8},{8,12},{12,0},{16,20},{20,24},{24,28},{28,16},{32,36},... | collective-permute-start | bytes 1105928 | tf_op jit(solution)/shard_map/ppermute | solution.py:42
  54.0 13.4 %collective-permute-start.10 = (bf16[1,96,1920]{2,1,0:T(8,128)(2,1)S(1)}, bf16[1,96,1920]{2,1,0:T(8,128)(2,1)S(1)}, u32[]{:S(2)}, u32[]{:S(2)}) collective-permute-start(bf16[1,96,1920]{2,1,0:T(8,128)(2,1)S(1)} %slice.141), channel_id=1, source_target_pairs={{0,96},{4,100},{8,104},{12,108},{16,112},{20,116},{24,120},{28,124... | collective-permute-start | bytes 1105928 | tf_op jit(solution)/shard_map/ppermute | solution.py:42
  57.8 9.6 %collective-permute-start.12 = (bf16[1,96,1920]{2,1,0:T(8,128)(2,1)S(1)}, bf16[1,96,1920]{2,1,0:T(8,128)(2,1)S(1)}, u32[]{:S(2)}, u32[]{:S(2)}) collective-permute-start(bf16[1,96,1920]{2,1,0:T(8,128)(2,1)S(1)} %slice.142), channel_id=1, source_target_pairs={{0,32},{4,36},{8,40},{12,44},{16,48},{20,52},{24,56},{28,60},{32,6... | collective-permute-start | bytes 1105928 | tf_op jit(solution)/shard_map/ppermute | solution.py:42
  64.7 62.8 %collective-permute-start.5 = (bf16[2,4,96,1920]{3,2,0,1:T(8,128)(2,1)S(1)}, bf16[2,4,96,1920]{3,2,0,1:T(8,128)(2,1)S(1)}, u32[]{:S(2)}, u32[]{:S(2)}) collective-permute-start(bf16[2,4,96,1920]{3,2,0,1:T(8,128)(2,1)S(1)} %bitcast.157), channel_id=1, source_target_pairs={{0,96},{4,100},{8,104},{12,108},{16,112},{20,116},{24,120},{28,124... | collective-permute-start | bytes 8847368 | tf_op jit(solution)/shard_map/ppermute | solution.py:42
  67.4 64.9 %collective-permute-start.7 = (bf16[2,4,96,1920]{3,2,0,1:T(8,128)(2,1)S(1)}, bf16[2,4,96,1920]{3,2,0,1:T(8,128)(2,1)S(1)}, u32[]{:S(2)}, u32[]{:S(2)}) collective-permute-start(bf16[2,4,96,1920]{3,2,0,1:T(8,128)(2,1)S(1)} %bitcast.158), channel_id=1, source_target_pairs={{0,32},{4,36},{8,40},{12,44},{16,48},{20,52},{24,56},{28,60},{32,6... | collective-permute-start | bytes 8847368 | tf_op jit(solution)/shard_map/ppermute | solution.py:42
  74.6 68.7 %collective-permute-start.13 = (bf16[4,2,96,1920]{3,2,1,0:T(8,128)(2,1)}, bf16[4,2,96,1920]{3,2,1,0:T(8,128)(2,1)}, u32[]{:S(2)}, u32[]{:S(2)}) collective-permute-start(bf16[4,2,96,1920]{3,2,1,0:T(8,128)(2,1)} %get-tuple-element.21), channel_id=1, source_target_pairs={{0,12},{4,0},{8,4},{12,8},{16,28},{20,16},{24,20},{28,24},{32,44},... | collective-permute-start | bytes 8847368 | tf_op jit(solution)/shard_map/ppermute | solution.py:42
  74.9 71.5 %collective-permute-start.15 = (bf16[4,2,96,1920]{3,2,1,0:T(8,128)(2,1)}, bf16[4,2,96,1920]{3,2,1,0:T(8,128)(2,1)}, u32[]{:S(2)}, u32[]{:S(2)}) collective-permute-start(bf16[4,2,96,1920]{3,2,1,0:T(8,128)(2,1)} %get-tuple-element.21), channel_id=1, source_target_pairs={{0,4},{4,8},{8,12},{12,0},{16,20},{20,24},{24,28},{28,16},{32,36},... | collective-permute-start | bytes 8847368 | tf_op jit(solution)/shard_map/ppermute | solution.py:42
  128.9 31.5 %collective-permute-start.6 = (bf16[1,4,96,1920]{3,2,0,1:T(8,128)(2,1)}, bf16[1,4,96,1920]{3,2,0,1:T(8,128)(2,1)}, u32[]{:S(2)}, u32[]{:S(2)}) collective-permute-start(bf16[1,4,96,1920]{3,2,0,1:T(8,128)(2,1)} %slice.137), channel_id=1, source_target_pairs={{0,96},{4,100},{8,104},{12,108},{16,112},{20,116},{24,120},{28,124... | collective-permute-start | bytes 4423688 | tf_op jit(solution)/shard_map/ppermute | solution.py:42
  135.2 31.2 %collective-permute-start.8 = (bf16[1,4,96,1920]{3,2,0,1:T(8,128)(2,1)}, bf16[1,4,96,1920]{3,2,0,1:T(8,128)(2,1)}, u32[]{:S(2)}, u32[]{:S(2)}) collective-permute-start(bf16[1,4,96,1920]{3,2,0,1:T(8,128)(2,1)} %slice.138), channel_id=1, source_target_pairs={{0,32},{4,36},{8,40},{12,44},{16,48},{20,52},{24,56},{28,60},{32,6... | collective-permute-start | bytes 4423688 | tf_op jit(solution)/shard_map/ppermute | solution.py:42
  146.1 72.0 %collective-permute-start.14 = (bf16[2,2,96,1920]{3,2,1,0:T(8,128)(2,1)}, bf16[2,2,96,1920]{3,2,1,0:T(8,128)(2,1)}, u32[]{:S(2)}, u32[]{:S(2)}) collective-permute-start(bf16[2,2,96,1920]{3,2,1,0:T(8,128)(2,1)} %slice.143), channel_id=1, source_target_pairs={{0,12},{4,0},{8,4},{12,8},{16,28},{20,16},{24,20},{28,24},{32,44},... | collective-permute-start | bytes 4423688 | tf_op jit(solution)/shard_map/ppermute | solution.py:42
  148.9 69.3 %collective-permute-start.16 = (bf16[2,2,96,1920]{3,2,1,0:T(8,128)(2,1)}, bf16[2,2,96,1920]{3,2,1,0:T(8,128)(2,1)}, u32[]{:S(2)}, u32[]{:S(2)}) collective-permute-start(bf16[2,2,96,1920]{3,2,1,0:T(8,128)(2,1)} %slice.144), channel_id=1, source_target_pairs={{0,4},{4,8},{8,12},{12,0},{16,20},{20,24},{24,28},{28,16},{32,36},... | collective-permute-start | bytes 4423688 | tf_op jit(solution)/shard_map/ppermute | solution.py:42
  275.4 21.0 %collective-permute-start.19 = (bf16[256,1536]{1,0:T(8,128)(2,1)}, bf16[256,1536]{1,0:T(8,128)(2,1)}, u32[]{:S(2)}, u32[]{:S(2)}) collective-permute-start(bf16[256,1536]{1,0:T(8,128)(2,1)} %convolution_convert_fusion.2), channel_id=1, source_target_pairs={{0,1},{1,0},{2,3},{3,2},{4,5},{5,4},{6,7},{7,6},{8,9},{9,8},{10,11... | collective-permute-start | bytes 2359304 | tf_op jit(solution)/shard_map/ppermute | solution.py:72
  291.0 18.5 %collective-permute-start.17 = (bf16[256,1536]{1,0:T(8,128)(2,1)S(1)}, bf16[256,1536]{1,0:T(8,128)(2,1)S(1)}, u32[]{:S(2)}, u32[]{:S(2)}) collective-permute-start(bf16[256,1536]{1,0:T(8,128)(2,1)S(1)} %convolution_convert_fusion.4), channel_id=1, source_target_pairs={{0,1},{1,0},{2,3},{3,2},{4,5},{5,4},{6,7},{7,6},{8,9},{9,8},{10,11... | collective-permute-start | bytes 2359304 | tf_op jit(solution)/shard_map/ppermute | solution.py:72
  315.5 3.4 collective-permute-start.20
  321.7 30.1 %collective-permute-start.21 = (bf16[512,3072]{1,0:T(8,128)(2,1)S(1)}, bf16[512,3072]{1,0:T(8,128)(2,1)S(1)}, u32[]{:S(2)}, u32[]{:S(2)}) collective-permute-start(bf16[512,3072]{1,0:T(8,128)(2,1)S(1)} %pad_maximum_fusion.1), channel_id=1, source_target_pairs={{0,2},{1,3},{4,6},{5,7},{8,10},{9,11},{12,14},{13,15},{16,18},{17,... | collective-permute-start | bytes 9437192 | tf_op jit(solution)/shard_map/ppermute | solution.py:18
  377.4 5.4 %collective-permute-start.23 = (f32[512,64]{0,1:T(8,128)S(1)}, f32[512,64]{0,1:T(8,128)S(1)}, u32[]{:S(2)}, u32[]{:S(2)}) collective-permute-start(f32[512,64]{0,1:T(8,128)S(1)} %fusion.93), channel_id=1, source_target_pairs={{0,1},{1,0},{2,3},{3,2},{4,5},{5,4},{6,7},{7,6},{8,9},{9,8},{10,11... | collective-permute-start | bytes 393224 | tf_op jit(solution)/shard_map/ppermute | solution.py:72
  394.6 10.0 %collective-permute-start.24 = (bf16[512,1536]{1,0:T(8,128)(2,1)}, bf16[512,1536]{1,0:T(8,128)(2,1)}, u32[]{:S(2)}, u32[]{:S(2)}) collective-permute-start(bf16[512,1536]{1,0:T(8,128)(2,1)} %multiply_convert_fusion), channel_id=1, source_target_pairs={{2,0},{3,1},{6,4},{7,5},{10,8},{11,9},{14,12},{15,13},{18,16},{19,... | collective-permute-start | bytes 4718600 | tf_op jit(solution)/shard_map/ppermute | solution.py:18
  410.3 82.0 %all-to-all-start = ((bf16[32,48,1536]{2,1,0:T(8,128)(2,1)}), bf16[32,48,1536]{2,1,0:T(8,128)(2,1)}, u32[]{:S(2)}, u32[]{:S(2)}) async-start(bf16[32,48,1536]{2,1,0:T(8,128)(2,1)} %bitcast.170), calls=%async_computation | async-start | bytes 9437184 | tf_op jit(solution)/shard_map/all_to_all | solution.py:290
  (36 other events, 347.9 us)

commit v11 on v10

--- a/solution.py
+++ b/solution.py
@@ -148,7 +148,11 @@
     ).astype(jnp.bfloat16)
     plain_rows = image_latent.astype(jnp.float32)
     hidden = plain_rows + jnp.where(is_control, 1.0, 0.0) * aligned.astype(jnp.float32)
-    chosen = jnp.take(captions, caption_ids, axis=0).astype(jnp.float32)
+    caption_slots = lax.broadcasted_iota(jnp.int32, (micro_count, captions.shape[0]), 1)
+    caption_picks = (caption_ids[:, None] == caption_slots).astype(jnp.bfloat16)
+    chosen = jnp.einsum(
+        "bc,ctd->btd", caption_picks, captions, preferred_element_type=jnp.float32
+    )
     sequence = jnp.concatenate([chosen, hidden], axis=1)
     modulate = modulation[0]
     normed = (layer_norm(sequence) * (1.0 + modulate[:, 1:2]) + modulate[:, 0:1]).astype(

time: 506 us -> 510 us (level)
  local copies, waits for them, and re-layouts: 94.8 us -> 106 us
  waiting for transfers between devices: 197 us -> 189 us
    unnamed x87 -> x85, local copies, waits for them, and re-layouts: 30.6 us -> 38.9 us
    ppermute x17, waiting for transfers between devices: 79.8 us -> 71.6 us  [ctl_shift(): return lax.ppermute(value, 'ctl', pairs)]
  transfers between devices with their start and end apart: 26 -> 26, of which waited for: 10 -> 12; matrix products, arithmetic and copies ran while one was open for 22% -> 24% of each run, Pallas kernels for 3% -> 3%
where the time goes in v11:
time: 510 us; the launch traced here: 501 us
  waiting for transfers between devices  189 us (37%)
  local copies, waits for them, and re-layouts  106 us (21%)
  other arithmetic  75.3 us (15%)
  starting transfers between devices  50.2 us (10%)
  matrix products  37.8 us (7%)
  Pallas kernels  31 us (6%)
  blocking collectives  10.7 us (2%)
    ppermute x17, waiting for transfers between devices, ctl_shift(): return lax.ppermute(value, 'ctl', pairs)  71.6 us
    all_to_all x1, waiting for transfers between devices, local(): received = lax.all_to_all(group_parts, 'ctl', 0, 0, tiled=True)  70.9 us
    unnamed x85, local copies, waits for them, and re-layouts  38.9 us
    pallas_call x3, Pallas kernels, block_matmul(): pl.pallas_call(kernel, grid=(block_count,), in_specs=[pl.BlockSpec((row_c...  31 us
    ppermute x2, waiting for transfers between devices, passed_along(): return lax.ppermute(shard, axis, pairs)  28.8 us
    unnamed x9, other arithmetic  23.6 us
    ppermute x17, starting transfers between devices, ctl_shift(): return lax.ppermute(value, 'ctl', pairs)  23.3 us
    ppermute x3, waiting for transfers between devices, swap(): return lax.ppermute(value, axis, [(0, 1), (1, 0)])  15.7 us
  transfers between devices with their start and end apart: 26, of which 12 were waited for; matrix products, arithmetic and copies ran while one was open for 24% of the time, Pallas kernels for 3%

profile of v11, /device:TPU:5, one launch (start us, length us, event | category | flops | bytes accessed | tf_op | source)
XLA Modules:
  0.0 501.3 jit_solution(5618602141259605913)
XLA Ops:
  7.9 16.4 %collective-permute-done = bf16[96,3840]{1,0:T(8,128)(2,1)} collective-permute-done((bf16[96,3840]{1,0:T(8,128)(2,1)}, bf16[96,3840]{1,0:T(8,128)(2,1)}, u32[]{:S(2)}, u32[]{:S(2)}) %collective-permute-start) | collective-permute-done | bytes 737312 | tf_op jit(solution)/shard_map/ppermute | solution.py:42
  32.0 12.6 %collective-permute-done.1 = bf16[2,96,1920]{2,1,0:T(8,128)(2,1)S(1)} collective-permute-done((bf16[2,96,1920]{2,1,0:T(8,128)(2,1)S(1)}, bf16[2,96,1920]{2,1,0:T(8,128)(2,1)S(1)}, u32[]{:S(2)}, u32[]{:S(2)}) %collective-permute-start.1) | collective-permute-done | bytes 737312 | tf_op jit(solution)/shard_map/ppermute | solution.py:42
  57.3 5.5 %bitcast_dynamic-update-slice_fusion = (bf16[8,2,4,96,1920]{4,3,1,2,0:T(8,128)(2,1)}, bf16[4,2,96,1920]{3,2,1,0:T(8,128)(2,1)}) fusion(s32[]{:T(128)S(6)} %select_n.164, bf16[1,2,96,1920]{3,2,1,0:T(8,128)(2,1)S(1)} %bitcast.179, bf16[1,2,96,1920]{3,2,1,0:T(8,128)(2,1)S(1)} %maximum_bitcast_fusion.2, bf16[1,2,96,1920]{3,2,1,0:T(8,128)(2,1)S(1)} %bitcast.178, ...), kind=kLoop, calls=%fused_computation.61 | loop fusion | flops 23592960 | bytes 8847364
  65.7 7.1 %bitcast_dynamic-update-slice_fusion.6 = (bf16[8,4,2,96,1920]{4,3,2,1,0:T(8,128)(2,1)}, bf16[4,2,96,1920]{3,2,1,0:T(8,128)(2,1)}) fusion(s32[]{:T(128)S(6)} %select_n.148, bf16[1,2,96,1920]{3,2,1,0:T(8,128)(2,1)} %bitcast.26, bf16[1,2,96,1920]{3,2,1,0:T(8,128)(2,1)S(1)} %maximum_bitcast_fusion.3, bf16[1,2,96,1920]{3,2,1,0:T(8,128)(2,1)} %bitcast.24, ...), kind=kLoop, calls=%fused_computation.67 | loop fusion | flops 23592960 | bytes 8847364
  91.6 34.3 %collective-permute-done.5 = bf16[2,4,96,1920]{3,2,0,1:T(8,128)(2,1)} collective-permute-done((bf16[2,4,96,1920]{3,2,0,1:T(8,128)(2,1)}, bf16[2,4,96,1920]{3,2,0,1:T(8,128)(2,1)}, u32[]{:S(2)}, u32[]{:S(2)}) %collective-permute-start.5) | collective-permute-done | bytes 2949152 | tf_op jit(solution)/shard_map/ppermute | solution.py:42
  134.6 8.0 %fusion.2.rows_ref = bf16[768,3072]{1,0:T(8,128)(2,1)} fusion(f32[2,384,3072]{2,1,0:T(8,128)} %get-tuple-element.23, f32[2,3072]{1,0:T(2,128)S(1)} %get-tuple-element.40, f32[2,3072]{1,0:T(2,128)S(1)} %get-tuple-element.41, f32[768]{0:T(1024)S(1)} %rsqrt.47, f32[768]{0:T(1024)S(1)} %div.70), kind=kLoop, calls=%fused_computation.5 | loop fusion | flops 11796480 | bytes 14211072 | tf_op jit(solution)/shard_map/convert_element_type | solution.py:158
  159.8 5.6 %collective-permute-done.8 = bf16[1,4,96,1920]{3,2,0,1:T(8,128)(2,1)S(1)} collective-permute-done((bf16[1,4,96,1920]{3,2,0,1:T(8,128)(2,1)}, bf16[1,4,96,1920]{3,2,0,1:T(8,128)(2,1)S(1)}, u32[]{:S(2)}, u32[]{:S(2)}) %collective-permute-start.8) | collective-permute-done | bytes 1474592 | tf_op jit(solution)/shard_map/ppermute | solution.py:42
  183.6 6.3 %constant_dynamic-slice_fusion.3 = bf16[4,2,4,96,1920]{4,3,1,2,0:T(8,128)(2,1)S(1)} fusion(bf16[8,2,4,96,1920]{4,3,1,2,0:T(8,128)(2,1)} %bitcast_dynamic-update-slice_fusion.9, s32[]{:T(128)S(6)} %select_n.148), kind=kLoop, calls=%fused_computation.152 | loop fusion | bytes 23592964 | tf_op jit(solution)/shard_map/jit(_roll_dynamic)/dynamic_slice | solution.py:54
  190.0 5.3 %copy.28 = bf16[4,2,4,96,1920]{4,3,2,1,0:T(8,128)(2,1)} copy(bf16[4,2,4,96,1920]{4,3,1,2,0:T(8,128)(2,1)S(1)} %constant_dynamic-slice_fusion.3) | data formatting | bytes 23592960 | tf_op jit(solution)/shard_map/jit(_roll_dynamic)/dynamic_slice | solution.py:54
  195.3 17.2 %shard_map.140 = f32[768,1920]{1,0:T(8,128)} custom-call(bf16[768,3072]{1,0:T(8,128)(2,1)} %fusion.2.rows_ref, bf16[3072,1920]{1,0:T(8,128)(2,1)} %bitcast.159), custom_call_target="tpu_custom_call" | custom-call | flops 9059696640 | bytes 22413312 | tf_op jit(solution)/shard_map/pallas_call | solution.py:81
  241.7 6.1 %dynamic-slice_bitcast_fusion = bf16[4,2,4,96,1920]{4,3,1,0,2:T(8,128)(2,1)S(1)} fusion(bf16[8,4,2,96,1920]{4,3,2,1,0:T(8,128)(2,1)} %bitcast_dynamic-update-slice_fusion.3, s32[]{:T(128)S(6)} %select_n.164), kind=kLoop, calls=%fused_computation.2 | loop fusion | bytes 23592964 | tf_op jit(solution)/shard_map/transpose | solution.py:67
  247.9 5.3 %copy.29 = bf16[4,2,4,96,1920]{4,3,2,1,0:T(8,128)(2,1)} copy(bf16[4,2,4,96,1920]{4,3,1,0,2:T(8,128)(2,1)S(1)} %dynamic-slice_bitcast_fusion) | data formatting | bytes 23592960 | tf_op jit(solution)/shard_map/transpose | solution.py:67
  253.2 6.7 %shard_map.141 = f32[768,384]{1,0:T(8,128)} custom-call(bf16[768,3072]{1,0:T(8,128)(2,1)} %fusion.2.rows_ref, bf16[3072,1920]{1,0:T(8,128)(2,1)} %bitcast.155), custom_call_target="tpu_custom_call" | custom-call | flops 1811939328 | bytes 8257536 | tf_op jit(solution)/shard_map/pallas_call | solution.py:81
  268.3 5.3 %convolution_convert_fusion.6 = bf16[6,128,256]{2,1,0:T(8,128)(2,1)S(1)} fusion(bf16[384,6,128]{0,2,1:T(8,128)(2,1)S(1)} %bitcast.181, f32[6,256]{1,0:T(8,128)S(1)} %fusion.98, f32[6,256,384]{2,1,0:T(8,128)} %copy-done.14), kind=kOutput, calls=%fused_computation.106 | convolution fusion | flops 154142592 | bytes 3348480 | tf_op jit(solution)/shard_map/hij,jhd->ihd/dot_general | solution.py:210
  284.0 5.3 %convolution_convert_fusion.7 = bf16[6,128,256]{2,1,0:T(8,128)(2,1)S(1)} fusion(bf16[384,6,128]{0,2,1:T(8,128)(2,1)S(1)} %bitcast.182, f32[6,256]{1,0:T(8,128)S(1)} %fusion.97, f32[6,256,384]{2,1,0:T(8,128)} %copy-done.15), kind=kOutput, calls=%fused_computation.107 | convolution fusion | flops 154142592 | bytes 3348480 | tf_op jit(solution)/shard_map/hij,jhd->ihd/dot_general | solution.py:210
  298.1 13.0 %collective-permute-done.17 = bf16[256,1536]{1,0:T(8,128)(2,1)S(1)} collective-permute-done((bf16[256,1536]{1,0:T(8,128)(2,1)S(1)}, bf16[256,1536]{1,0:T(8,128)(2,1)S(1)}, u32[]{:S(2)}, u32[]{:S(2)}) %collective-permute-start.17) | collective-permute-done | bytes 786464 | tf_op jit(solution)/shard_map/ppermute | solution.py:72
  324.7 28.8 %collective-permute-done.21 = bf16[512,3072]{1,0:T(8,128)(2,1)S(1)} collective-permute-done((bf16[512,3072]{1,0:T(8,128)(2,1)S(1)}, bf16[512,3072]{1,0:T(8,128)(2,1)S(1)}, u32[]{:S(2)}, u32[]{:S(2)}) %collective-permute-start.21) | collective-permute-done | bytes 3145760 | tf_op jit(solution)/shard_map/ppermute | solution.py:18
  356.4 7.1 %shard_map.142 = f32[512,768]{1,0:T(8,128)} custom-call(bf16[512,3072]{1,0:T(8,128)(2,1)} %broadcast_select_fusion.rows_ref, bf16[3072,1920]{1,0:T(8,128)(2,1)} %bitcast.157), custom_call_target="tpu_custom_call" | custom-call | flops 2415919104 | bytes 9437184 | tf_op jit(solution)/shard_map/pallas_call | solution.py:81
  372.2 5.4 %all-reduce.1 = (f32[2,256,1]{1,0,2:T(2,128)S(1)}, f32[2,256,1]{1,0,2:T(2,128)S(1)}) all-reduce(f32[2,256,1]{1,0,2:T(2,128)S(1)} %broadcast_in_dim.9, f32[2,256,1]{1,0,2:T(2,128)S(1)} %broadcast_in_dim.8), channel_id=1, replica_groups=mesh['ctl'=32,'side'=2,'tp'=2] {'tp'}, use_global_device_ids=true, to_apply=%region_13.15 | all-reduce | flops 1024 | bytes 8192 | tf_op jit(solution)/shard_map/psum | solution.py:249
  387.2 5.3 %all-reduce = (f32[2,256,1]{1,0,2:T(2,128)S(1)}, f32[2,256,1]{1,0,2:T(2,128)S(1)}) all-reduce(f32[2,256,1]{1,0,2:T(2,128)S(1)} %broadcast_in_dim.11, f32[2,256,1]{1,0,2:T(2,128)S(1)} %broadcast_in_dim.10), channel_id=1, replica_groups=mesh['ctl'=32,'side'=2,'tp'=2] {'tp'}, use_global_device_ids=true, to_apply=%region_17.19 | all-reduce | flops 1024 | bytes 8192 | tf_op jit(solution)/shard_map/psum | solution.py:273
  396.3 6.7 %collective-permute-start.24 = (bf16[512,1536]{1,0:T(8,128)(2,1)}, bf16[512,1536]{1,0:T(8,128)(2,1)}, u32[]{:S(2)}, u32[]{:S(2)}) collective-permute-start(bf16[512,1536]{1,0:T(8,128)(2,1)} %multiply_convert_fusion), channel_id=1, source_target_pairs={{2,0},{3,1},{6,4},{7,5},{10,8},{11,9},{14,12},{15,13},{18,16},{19,... | collective-permute-start | bytes 4718600 | tf_op jit(solution)/shard_map/ppermute | solution.py:18
  406.3 5.7 %convolution_convert_fusion = bf16[1536,1536]{1,0:T(8,128)(2,1)} fusion(bf16[512,1536]{0,1:T(8,128)(2,1)S(1)} %bitcast.180, bf16[512,1536]{1,0:T(8,128)(2,1)} %collective-permute-done.24, bf16[512,1536]{1,0:T(8,128)(2,1)} %multiply_convert_fusion, pred[]{:T(512)S(6)} %eq.35), kind=kOutput, calls=%fused_computation.11 | convolution fusion | flops 2419064832 | bytes 9437185 | tf_op jit(solution)/shard_map/dot_general | solution.py:290
  412.1 9.4 %all-to-all-start = ((bf16[32,48,1536]{2,1,0:T(8,128)(2,1)}), bf16[32,48,1536]{2,1,0:T(8,128)(2,1)}, u32[]{:S(2)}, u32[]{:S(2)}) async-start(bf16[32,48,1536]{2,1,0:T(8,128)(2,1)} %bitcast.171), calls=%async_computation | async-start | bytes 9437184 | tf_op jit(solution)/shard_map/all_to_all | solution.py:294
  426.2 70.9 %all-to-all-done = bf16[32,48,1536]{2,1,0:T(8,128)(2,1)} async-done(((bf16[32,48,1536]{2,1,0:T(8,128)(2,1)}), bf16[32,48,1536]{2,1,0:T(8,128)(2,1)}, u32[]{:S(2)}, u32[]{:S(2)}) %all-to-all-start) | async-done | bytes 4718624 | tf_op jit(solution)/shard_map/all_to_all | solution.py:294
  (208 shorter events, 200.1 us)
Async XLA Ops:
  6.2 18.0 %collective-permute-start = (bf16[96,3840]{1,0:T(8,128)(2,1)}, bf16[96,3840]{1,0:T(8,128)(2,1)}, u32[]{:S(2)}, u32[]{:S(2)}) collective-permute-start(bf16[96,3840]{1,0:T(8,128)(2,1)} %get-tuple-element.38), channel_id=1, source_target_pairs={{0,16},{4,20},{8,24},{12,28},{16,0},{20,4},{24,8},{28,12},{32,48},... | collective-permute-start | bytes 2211848 | tf_op jit(solution)/shard_map/ppermute | solution.py:42
  27.8 16.8 %collective-permute-start.1 = (bf16[2,96,1920]{2,1,0:T(8,128)(2,1)S(1)}, bf16[2,96,1920]{2,1,0:T(8,128)(2,1)S(1)}, u32[]{:S(2)}, u32[]{:S(2)}) collective-permute-start(bf16[2,96,1920]{2,1,0:T(8,128)(2,1)S(1)} %get-tuple-element.34), channel_id=1, source_target_pairs={{0,12},{4,0},{8,4},{12,8},{16,28},{20,16},{24,20},{28,24},{32,44},... | collective-permute-start | bytes 2211848 | tf_op jit(solution)/shard_map/ppermute | solution.py:42
  28.0 18.5 %collective-permute-start.3 = (bf16[2,96,1920]{2,1,0:T(8,128)(2,1)S(1)}, bf16[2,96,1920]{2,1,0:T(8,128)(2,1)S(1)}, u32[]{:S(2)}, u32[]{:S(2)}) collective-permute-start(bf16[2,96,1920]{2,1,0:T(8,128)(2,1)S(1)} %get-tuple-element.34), channel_id=1, source_target_pairs={{0,4},{4,8},{8,12},{12,0},{16,20},{20,24},{24,28},{28,16},{32,36},... | collective-permute-start | bytes 2211848 | tf_op jit(solution)/shard_map/ppermute | solution.py:42
  29.2 20.8 %collective-permute-start.9 = (bf16[2,96,1920]{2,1,0:T(8,128)(2,1)}, bf16[2,96,1920]{2,1,0:T(8,128)(2,1)}, u32[]{:S(2)}, u32[]{:S(2)}) collective-permute-start(bf16[2,96,1920]{2,1,0:T(8,128)(2,1)} %get-tuple-element.33), channel_id=1, source_target_pairs={{0,96},{4,100},{8,104},{12,108},{16,112},{20,116},{24,120},{28,124... | collective-permute-start | bytes 2211848 | tf_op jit(solution)/shard_map/ppermute | solution.py:42
  32.0 22.0 %collective-permute-start.11 = (bf16[2,96,1920]{2,1,0:T(8,128)(2,1)}, bf16[2,96,1920]{2,1,0:T(8,128)(2,1)}, u32[]{:S(2)}, u32[]{:S(2)}) collective-permute-start(bf16[2,96,1920]{2,1,0:T(8,128)(2,1)} %get-tuple-element.33), channel_id=1, source_target_pairs={{0,32},{4,36},{8,40},{12,44},{16,48},{20,52},{24,56},{28,60},{32,6... | collective-permute-start | bytes 2211848 | tf_op jit(solution)/shard_map/ppermute | solution.py:42
  46.2 9.3 %collective-permute-start.2 = (bf16[1,96,1920]{2,1,0:T(8,128)(2,1)}, bf16[1,96,1920]{2,1,0:T(8,128)(2,1)S(1)}, u32[]{:S(2)}, u32[]{:S(2)}) collective-permute-start(bf16[1,96,1920]{2,1,0:T(8,128)(2,1)} %slice.133), channel_id=1, source_target_pairs={{0,12},{4,0},{8,4},{12,8},{16,28},{20,16},{24,20},{28,24},{32,44},... | collective-permute-start | bytes 1105928 | tf_op jit(solution)/shard_map/ppermute | solution.py:42
  48.1 8.1 %collective-permute-start.4 = (bf16[1,96,1920]{2,1,0:T(8,128)(2,1)}, bf16[1,96,1920]{2,1,0:T(8,128)(2,1)}, u32[]{:S(2)}, u32[]{:S(2)}) collective-permute-start(bf16[1,96,1920]{2,1,0:T(8,128)(2,1)} %slice.134), channel_id=1, source_target_pairs={{0,4},{4,8},{8,12},{12,0},{16,20},{20,24},{24,28},{28,16},{32,36},... | collective-permute-start | bytes 1105928 | tf_op jit(solution)/shard_map/ppermute | solution.py:42
  51.2 14.4 %collective-permute-start.10 = (bf16[1,96,1920]{2,1,0:T(8,128)(2,1)S(1)}, bf16[1,96,1920]{2,1,0:T(8,128)(2,1)S(1)}, u32[]{:S(2)}, u32[]{:S(2)}) collective-permute-start(bf16[1,96,1920]{2,1,0:T(8,128)(2,1)S(1)} %slice.139), channel_id=1, source_target_pairs={{0,96},{4,100},{8,104},{12,108},{16,112},{20,116},{24,120},{28,124... | collective-permute-start | bytes 1105928 | tf_op jit(solution)/shard_map/ppermute | solution.py:42
  55.0 10.6 %collective-permute-start.12 = (bf16[1,96,1920]{2,1,0:T(8,128)(2,1)S(1)}, bf16[1,96,1920]{2,1,0:T(8,128)(2,1)S(1)}, u32[]{:S(2)}, u32[]{:S(2)}) collective-permute-start(bf16[1,96,1920]{2,1,0:T(8,128)(2,1)S(1)} %slice.140), channel_id=1, source_target_pairs={{0,32},{4,36},{8,40},{12,44},{16,48},{20,52},{24,56},{28,60},{32,6... | collective-permute-start | bytes 1105928 | tf_op jit(solution)/shard_map/ppermute | solution.py:42
  62.8 63.0 %collective-permute-start.5 = (bf16[2,4,96,1920]{3,2,0,1:T(8,128)(2,1)}, bf16[2,4,96,1920]{3,2,0,1:T(8,128)(2,1)}, u32[]{:S(2)}, u32[]{:S(2)}) collective-permute-start(bf16[2,4,96,1920]{3,2,0,1:T(8,128)(2,1)} %bitcast.16), channel_id=1, source_target_pairs={{0,96},{4,100},{8,104},{12,108},{16,112},{20,116},{24,120},{28,124... | collective-permute-start | bytes 8847368 | tf_op jit(solution)/shard_map/ppermute | solution.py:42
  65.6 66.3 %collective-permute-start.7 = (bf16[2,4,96,1920]{3,2,0,1:T(8,128)(2,1)}, bf16[2,4,96,1920]{3,2,0,1:T(8,128)(2,1)}, u32[]{:S(2)}, u32[]{:S(2)}) collective-permute-start(bf16[2,4,96,1920]{3,2,0,1:T(8,128)(2,1)} %bitcast.16), channel_id=1, source_target_pairs={{0,32},{4,36},{8,40},{12,44},{16,48},{20,52},{24,56},{28,60},{32,6... | collective-permute-start | bytes 8847368 | tf_op jit(solution)/shard_map/ppermute | solution.py:42
  72.8 69.8 %collective-permute-start.13 = (bf16[4,2,96,1920]{3,2,1,0:T(8,128)(2,1)}, bf16[4,2,96,1920]{3,2,1,0:T(8,128)(2,1)}, u32[]{:S(2)}, u32[]{:S(2)}) collective-permute-start(bf16[4,2,96,1920]{3,2,1,0:T(8,128)(2,1)} %get-tuple-element.21), channel_id=1, source_target_pairs={{0,12},{4,0},{8,4},{12,8},{16,28},{20,16},{24,20},{28,24},{32,44},... | collective-permute-start | bytes 8847368 | tf_op jit(solution)/shard_map/ppermute | solution.py:42
  75.6 72.7 %collective-permute-start.15 = (bf16[4,2,96,1920]{3,2,1,0:T(8,128)(2,1)}, bf16[4,2,96,1920]{3,2,1,0:T(8,128)(2,1)}, u32[]{:S(2)}, u32[]{:S(2)}) collective-permute-start(bf16[4,2,96,1920]{3,2,1,0:T(8,128)(2,1)} %get-tuple-element.21), channel_id=1, source_target_pairs={{0,4},{4,8},{8,12},{12,0},{16,20},{20,24},{24,28},{28,16},{32,36},... | collective-permute-start | bytes 8847368 | tf_op jit(solution)/shard_map/ppermute | solution.py:42
  128.5 31.3 %collective-permute-start.6 = (bf16[1,4,96,1920]{3,2,0,1:T(8,128)(2,1)}, bf16[1,4,96,1920]{3,2,0,1:T(8,128)(2,1)S(1)}, u32[]{:S(2)}, u32[]{:S(2)}) collective-permute-start(bf16[1,4,96,1920]{3,2,0,1:T(8,128)(2,1)} %slice.135), channel_id=1, source_target_pairs={{0,96},{4,100},{8,104},{12,108},{16,112},{20,116},{24,120},{28,124... | collective-permute-start | bytes 4423688 | tf_op jit(solution)/shard_map/ppermute | solution.py:42
  134.5 30.9 %collective-permute-start.8 = (bf16[1,4,96,1920]{3,2,0,1:T(8,128)(2,1)}, bf16[1,4,96,1920]{3,2,0,1:T(8,128)(2,1)S(1)}, u32[]{:S(2)}, u32[]{:S(2)}) collective-permute-start(bf16[1,4,96,1920]{3,2,0,1:T(8,128)(2,1)} %slice.136), channel_id=1, source_target_pairs={{0,32},{4,36},{8,40},{12,44},{16,48},{20,52},{24,56},{28,60},{32,6... | collective-permute-start | bytes 4423688 | tf_op jit(solution)/shard_map/ppermute | solution.py:42
  145.2 74.5 %collective-permute-start.14 = (bf16[2,2,96,1920]{3,2,1,0:T(8,128)(2,1)}, bf16[2,2,96,1920]{3,2,1,0:T(8,128)(2,1)}, u32[]{:S(2)}, u32[]{:S(2)}) collective-permute-start(bf16[2,2,96,1920]{3,2,1,0:T(8,128)(2,1)} %slice.141), channel_id=1, source_target_pairs={{0,12},{4,0},{8,4},{12,8},{16,28},{20,16},{24,20},{28,24},{32,44},... | collective-permute-start | bytes 4423688 | tf_op jit(solution)/shard_map/ppermute | solution.py:42
  150.9 68.9 %collective-permute-start.16 = (bf16[2,2,96,1920]{3,2,1,0:T(8,128)(2,1)}, bf16[2,2,96,1920]{3,2,1,0:T(8,128)(2,1)}, u32[]{:S(2)}, u32[]{:S(2)}) collective-permute-start(bf16[2,2,96,1920]{3,2,1,0:T(8,128)(2,1)} %slice.142), channel_id=1, source_target_pairs={{0,4},{4,8},{8,12},{12,0},{16,20},{20,24},{24,28},{28,16},{32,36},... | collective-permute-start | bytes 4423688 | tf_op jit(solution)/shard_map/ppermute | solution.py:42
  277.2 21.0 %collective-permute-start.19 = (bf16[256,1536]{1,0:T(8,128)(2,1)}, bf16[256,1536]{1,0:T(8,128)(2,1)}, u32[]{:S(2)}, u32[]{:S(2)}) collective-permute-start(bf16[256,1536]{1,0:T(8,128)(2,1)} %convolution_convert_fusion.2), channel_id=1, source_target_pairs={{0,1},{1,0},{2,3},{3,2},{4,5},{5,4},{6,7},{7,6},{8,9},{9,8},{10,11... | collective-permute-start | bytes 2359304 | tf_op jit(solution)/shard_map/ppermute | solution.py:72
  292.5 18.6 %collective-permute-start.17 = (bf16[256,1536]{1,0:T(8,128)(2,1)S(1)}, bf16[256,1536]{1,0:T(8,128)(2,1)S(1)}, u32[]{:S(2)}, u32[]{:S(2)}) collective-permute-start(bf16[256,1536]{1,0:T(8,128)(2,1)S(1)} %convolution_convert_fusion.4), channel_id=1, source_target_pairs={{0,1},{1,0},{2,3},{3,2},{4,5},{5,4},{6,7},{7,6},{8,9},{9,8},{10,11... | collective-permute-start | bytes 2359304 | tf_op jit(solution)/shard_map/ppermute | solution.py:72
  317.2 3.4 collective-permute-start.20
  323.4 30.1 %collective-permute-start.21 = (bf16[512,3072]{1,0:T(8,128)(2,1)S(1)}, bf16[512,3072]{1,0:T(8,128)(2,1)S(1)}, u32[]{:S(2)}, u32[]{:S(2)}) collective-permute-start(bf16[512,3072]{1,0:T(8,128)(2,1)S(1)} %pad_maximum_fusion.1), channel_id=1, source_target_pairs={{0,2},{1,3},{4,6},{5,7},{8,10},{9,11},{12,14},{13,15},{16,18},{17,... | collective-permute-start | bytes 9437192 | tf_op jit(solution)/shard_map/ppermute | solution.py:18
  379.2 5.4 %collective-permute-start.23 = (f32[512,64]{0,1:T(8,128)S(1)}, f32[512,64]{0,1:T(8,128)S(1)}, u32[]{:S(2)}, u32[]{:S(2)}) collective-permute-start(f32[512,64]{0,1:T(8,128)S(1)} %fusion.99), channel_id=1, source_target_pairs={{0,1},{1,0},{2,3},{3,2},{4,5},{5,4},{6,7},{7,6},{8,9},{9,8},{10,11... | collective-permute-start | bytes 393224 | tf_op jit(solution)/shard_map/ppermute | solution.py:72
  396.3 10.0 %collective-permute-start.24 = (bf16[512,1536]{1,0:T(8,128)(2,1)}, bf16[512,1536]{1,0:T(8,128)(2,1)}, u32[]{:S(2)}, u32[]{:S(2)}) collective-permute-start(bf16[512,1536]{1,0:T(8,128)(2,1)} %multiply_convert_fusion), channel_id=1, source_target_pairs={{2,0},{3,1},{6,4},{7,5},{10,8},{11,9},{14,12},{15,13},{18,16},{19,... | collective-permute-start | bytes 4718600 | tf_op jit(solution)/shard_map/ppermute | solution.py:18
  412.1 85.1 %all-to-all-start = ((bf16[32,48,1536]{2,1,0:T(8,128)(2,1)}), bf16[32,48,1536]{2,1,0:T(8,128)(2,1)}, u32[]{:S(2)}, u32[]{:S(2)}) async-start(bf16[32,48,1536]{2,1,0:T(8,128)(2,1)} %bitcast.171), calls=%async_computation | async-start | bytes 9437184 | tf_op jit(solution)/shard_map/all_to_all | solution.py:294
  (35 other events, 316.3 us)

commit v12 on v10

--- a/solution.py
+++ b/solution.py
@@ -283,12 +283,20 @@
         control_rows.reshape(flat_rows, ctl_count, 2, block_rows), side_index, 2, keepdims=False
     )
     own_act = own_act.reshape(flat_rows, ctl_count * block_rows)
-    product = lax.dot_general(
-        own_act, grad_rows_all, (((0,), (0,)), ((), ())), preferred_element_type=jnp.float32
-    )
-    group_parts = rounded(product).astype(jnp.bfloat16).reshape(ctl_count, block_rows, half_width)
-    received = lax.all_to_all(group_parts, "ctl", 0, 0, tiled=True)
-    zero_grad = jnp.sum(received.astype(jnp.float32), axis=0)
+    column_half = half_width // 2
+    sums = []
+    for part in range(2):
+        product = lax.dot_general(
+            own_act,
+            grad_rows_all[:, part * column_half : (part + 1) * column_half],
+            (((0,), (0,)), ((), ())),
+            preferred_element_type=jnp.float32,
+        )
+        group_parts = rounded(product).astype(jnp.bfloat16)
+        group_parts = group_parts.reshape(ctl_count, block_rows, column_half)
+        received = lax.all_to_all(group_parts, "ctl", 0, 0, tiled=True)
+        sums.append(jnp.sum(received.astype(jnp.float32), axis=0))
+    zero_grad = jnp.concatenate(sums, axis=1)
     return (section_out.reshape(1, micro_count, img_rows, half_width), zero_grad)
 
 

time: 506 us -> 501 us (level)
  the two profiles are of different devices: /device:TPU:5 before, /device:TPU:66 now
where the time goes in v12:
time: 501 us; the launch traced here: 491 us
  waiting for transfers between devices  179 us (36%)
  local copies, waits for them, and re-layouts  95.2 us (19%)
  other arithmetic  82.3 us (16%)
  starting transfers between devices  53.8 us (11%)
  matrix products  34.6 us (7%)
  Pallas kernels  31.1 us (6%)
  blocking collectives  13 us (3%)
    ppermute x17, waiting for transfers between devices, ctl_shift(): return lax.ppermute(value, 'ctl', pairs)  81.2 us
    all_to_all x2, waiting for transfers between devices, local(): received = lax.all_to_all(group_parts, 'ctl', 0, 0, tiled=True)  57.4 us
    pallas_call x3, Pallas kernels, block_matmul(): pl.pallas_call(kernel, grid=(block_count,), in_specs=[pl.BlockSpec((row_c...  31.1 us
    unnamed x91, local copies, waits for them, and re-layouts  31 us
    unnamed x9, other arithmetic  28.4 us
    ppermute x17, starting transfers between devices, ctl_shift(): return lax.ppermute(value, 'ctl', pairs)  24.8 us
    ppermute x3, waiting for transfers between devices, swap(): return lax.ppermute(value, axis, [(0, 1), (1, 0)])  17.7 us
    ppermute x2, waiting for transfers between devices, local(): act_got = lax.ppermute(act_own, ('side', 'tp'), [(0, 1), (1, 0)])  14.7 us
  transfers between devices with their start and end apart: 27, of which 15 were waited for; matrix products, arithmetic and copies ran while one was open for 23% of the time, Pallas kernels for 4%

profile of v12, /device:TPU:66, one launch (start us, length us, event | category | flops | bytes accessed | tf_op | source)
XLA Modules:
  0.0 490.7 jit_solution(8230808044210815335)
XLA Ops:
  7.9 16.9 %collective-permute-done = bf16[96,3840]{1,0:T(8,128)(2,1)} collective-permute-done((bf16[96,3840]{1,0:T(8,128)(2,1)}, bf16[96,3840]{1,0:T(8,128)(2,1)}, u32[]{:S(2)}, u32[]{:S(2)}) %collective-permute-start) | collective-permute-done | bytes 737312 | tf_op jit(solution)/shard_map/ppermute | solution.py:42
  37.5 8.9 %collective-permute-done.1 = bf16[2,96,1920]{2,1,0:T(8,128)(2,1)} collective-permute-done((bf16[2,96,1920]{2,1,0:T(8,128)(2,1)}, bf16[2,96,1920]{2,1,0:T(8,128)(2,1)}, u32[]{:S(2)}, u32[]{:S(2)}) %collective-permute-start.1) | collective-permute-done | bytes 737312 | tf_op jit(solution)/shard_map/ppermute | solution.py:42
  59.7 6.7 %bitcast_dynamic-update-slice_fusion = (bf16[8,2,4,96,1920]{4,3,1,2,0:T(8,128)(2,1)}, bf16[4,2,96,1920]{3,2,1,0:T(8,128)(2,1)S(1)}) fusion(s32[]{:T(128)S(6)} %select_n.175, bf16[1,2,96,1920]{3,2,1,0:T(8,128)(2,1)} %bitcast.14, bf16[1,2,96,1920]{3,2,1,0:T(8,128)(2,1)S(1)} %maximum_bitcast_fusion.2, bf16[1,2,96,1920]{3,2,1,0:T(8,128)(2,1)} %bitcast.12, ...), kind=kLoop, calls=%fused_computation.62 | loop fusion | flops 23592960 | bytes 8847364
  69.6 7.1 %bitcast_dynamic-update-slice_fusion.6 = (bf16[8,4,2,96,1920]{4,3,2,1,0:T(8,128)(2,1)}, bf16[4,2,96,1920]{3,2,1,0:T(8,128)(2,1)}) fusion(s32[]{:T(128)S(6)} %select_n.159, bf16[1,2,96,1920]{3,2,1,0:T(8,128)(2,1)} %bitcast.25, bf16[1,2,96,1920]{3,2,1,0:T(8,128)(2,1)S(1)} %maximum_bitcast_fusion.3, bf16[1,2,96,1920]{3,2,1,0:T(8,128)(2,1)} %bitcast.23, ...), kind=kLoop, calls=%fused_computation.68 | loop fusion | flops 23592960 | bytes 8847364
  85.3 44.8 %collective-permute-done.5 = bf16[2,4,96,1920]{3,2,0,1:T(8,128)(2,1)S(1)} collective-permute-done((bf16[2,4,96,1920]{3,2,0,1:T(8,128)(2,1)S(1)}, bf16[2,4,96,1920]{3,2,0,1:T(8,128)(2,1)S(1)}, u32[]{:S(2)}, u32[]{:S(2)}) %collective-permute-start.5) | collective-permute-done | bytes 2949152 | tf_op jit(solution)/shard_map/ppermute | solution.py:42
  138.1 8.0 %fusion.2.rows_ref = bf16[768,3072]{1,0:T(8,128)(2,1)} fusion(f32[2,384,3072]{2,1,0:T(8,128)} %get-tuple-element.23, f32[2,3072]{1,0:T(2,128)S(1)} %get-tuple-element.40, f32[2,3072]{1,0:T(2,128)S(1)} %get-tuple-element.41, f32[768]{0:T(1024)S(1)} %rsqrt.47, f32[768]{0:T(1024)S(1)} %div.70), kind=kLoop, calls=%fused_computation.6 | loop fusion | flops 11796480 | bytes 14211072 | tf_op jit(solution)/shard_map/convert_element_type | solution.py:154
  163.5 6.4 %collective-permute-done.8 = bf16[1,4,96,1920]{3,2,0,1:T(8,128)(2,1)} collective-permute-done((bf16[1,4,96,1920]{3,2,0,1:T(8,128)(2,1)}, bf16[1,4,96,1920]{3,2,0,1:T(8,128)(2,1)}, u32[]{:S(2)}, u32[]{:S(2)}) %collective-permute-start.8) | collective-permute-done | bytes 1474592 | tf_op jit(solution)/shard_map/ppermute | solution.py:42
  185.5 6.3 %constant_dynamic-slice_fusion.3 = bf16[4,2,4,96,1920]{4,3,1,2,0:T(8,128)(2,1)S(1)} fusion(bf16[8,2,4,96,1920]{4,3,1,2,0:T(8,128)(2,1)} %bitcast_dynamic-update-slice_fusion.9, s32[]{:T(128)S(6)} %select_n.159), kind=kLoop, calls=%fused_computation.156 | loop fusion | bytes 23592964 | tf_op jit(solution)/shard_map/jit(_roll_dynamic)/dynamic_slice | solution.py:54
  197.0 17.2 %shard_map.140 = f32[768,1920]{1,0:T(8,128)} custom-call(bf16[768,3072]{1,0:T(8,128)(2,1)} %fusion.2.rows_ref, bf16[3072,1920]{1,0:T(8,128)(2,1)} %bitcast.158), custom_call_target="tpu_custom_call" | custom-call | flops 9059696640 | bytes 22413312 | tf_op jit(solution)/shard_map/pallas_call | solution.py:81
  243.5 6.1 %dynamic-slice_bitcast_fusion = bf16[4,2,4,96,1920]{4,3,1,0,2:T(8,128)(2,1)S(1)} fusion(bf16[8,4,2,96,1920]{4,3,2,1,0:T(8,128)(2,1)} %bitcast_dynamic-update-slice_fusion.3, s32[]{:T(128)S(6)} %select_n.175), kind=kLoop, calls=%fused_computation.3 | loop fusion | bytes 23592964 | tf_op jit(solution)/shard_map/transpose | solution.py:67
  254.8 6.7 %shard_map.141 = f32[768,384]{1,0:T(8,128)} custom-call(bf16[768,3072]{1,0:T(8,128)(2,1)} %fusion.2.rows_ref, bf16[3072,1920]{1,0:T(8,128)(2,1)} %bitcast.154), custom_call_target="tpu_custom_call" | custom-call | flops 1811939328 | bytes 8257536 | tf_op jit(solution)/shard_map/pallas_call | solution.py:81
  270.4 5.3 %convolution_convert_fusion.7 = bf16[6,128,256]{2,1,0:T(8,128)(2,1)S(1)} fusion(bf16[384,6,128]{0,2,1:T(8,128)(2,1)S(1)} %bitcast.180, f32[6,256]{1,0:T(8,128)S(1)} %fusion.92, f32[6,256,384]{2,1,0:T(8,128)} %copy-done.19), kind=kOutput, calls=%fused_computation.107 | convolution fusion | flops 154142592 | bytes 3348480 | tf_op jit(solution)/shard_map/hij,jhd->ihd/dot_general | solution.py:206
  284.0 5.3 %convolution_convert_fusion.8 = bf16[6,128,256]{2,1,0:T(8,128)(2,1)S(1)} fusion(bf16[384,6,128]{0,2,1:T(8,128)(2,1)S(1)} %bitcast.181, f32[6,256]{1,0:T(8,128)S(1)} %fusion.91, f32[6,256,384]{2,1,0:T(8,128)} %copy-done.20), kind=kOutput, calls=%fused_computation.108 | convolution fusion | flops 154142592 | bytes 3348480 | tf_op jit(solution)/shard_map/hij,jhd->ihd/dot_general | solution.py:206
  300.7 11.9 %collective-permute-done.17 = bf16[256,1536]{1,0:T(8,128)(2,1)S(1)} collective-permute-done((bf16[256,1536]{1,0:T(8,128)(2,1)S(1)}, bf16[256,1536]{1,0:T(8,128)(2,1)S(1)}, u32[]{:S(2)}, u32[]{:S(2)}) %collective-permute-start.17) | collective-permute-done | bytes 786464 | tf_op jit(solution)/shard_map/ppermute | solution.py:72
  324.6 8.1 %collective-permute-done.18 = bf16[256,1536]{1,0:T(8,128)(2,1)} collective-permute-done((bf16[256,1536]{1,0:T(8,128)(2,1)S(1)}, bf16[256,1536]{1,0:T(8,128)(2,1)}, u32[]{:S(2)}, u32[]{:S(2)}) %collective-permute-start.18) | collective-permute-done | bytes 786464 | tf_op jit(solution)/shard_map/ppermute | solution.py:220
  334.6 6.5 %collective-permute-done.20 = bf16[256,1536]{1,0:T(8,128)(2,1)} collective-permute-done((bf16[256,1536]{1,0:T(8,128)(2,1)S(1)}, bf16[256,1536]{1,0:T(8,128)(2,1)}, u32[]{:S(2)}, u32[]{:S(2)}) %collective-permute-start.20) | collective-permute-done | bytes 786464 | tf_op jit(solution)/shard_map/ppermute | solution.py:220
  353.4 7.2 %shard_map.142 = f32[512,768]{1,0:T(8,128)} custom-call(bf16[512,3072]{1,0:T(8,128)(2,1)} %broadcast_select_fusion.rows_ref, bf16[3072,1920]{1,0:T(8,128)(2,1)} %bitcast.156), custom_call_target="tpu_custom_call" | custom-call | flops 2415919104 | bytes 9437184 | tf_op jit(solution)/shard_map/pallas_call | solution.py:81
  369.2 6.6 %all-reduce.1 = (f32[2,256,1]{1,0,2:T(2,128)S(1)}, f32[2,256,1]{1,0,2:T(2,128)S(1)}) all-reduce(f32[2,256,1]{1,0,2:T(2,128)S(1)} %broadcast_in_dim.39, f32[2,256,1]{1,0,2:T(2,128)S(1)} %broadcast_in_dim.38), channel_id=1, replica_groups=mesh['ctl'=32,'side'=2,'tp'=2] {'tp'}, use_global_device_ids=true, to_apply=%region_13.15 | all-reduce | flops 1024 | bytes 8192 | tf_op jit(solution)/shard_map/psum | solution.py:245
  378.1 5.8 %collective-permute-done.23 = f32[512,64]{0,1:T(8,128)S(1)} collective-permute-done((f32[512,64]{0,1:T(8,128)S(1)}, f32[512,64]{0,1:T(8,128)S(1)}, u32[]{:S(2)}, u32[]{:S(2)}) %collective-permute-start.23) | collective-permute-done | bytes 131104 | tf_op jit(solution)/shard_map/ppermute | solution.py:72
  386.5 6.4 %all-reduce = (f32[2,256,1]{1,0,2:T(2,128)S(1)}, f32[2,256,1]{1,0,2:T(2,128)S(1)}) all-reduce(f32[2,256,1]{1,0,2:T(2,128)S(1)} %broadcast_in_dim.41, f32[2,256,1]{1,0,2:T(2,128)S(1)} %broadcast_in_dim.40), channel_id=1, replica_groups=mesh['ctl'=32,'side'=2,'tp'=2] {'tp'}, use_global_device_ids=true, to_apply=%region_17.19 | all-reduce | flops 1024 | bytes 8192 | tf_op jit(solution)/shard_map/psum | solution.py:269
  406.9 7.6 %all-to-all-start = ((bf16[32,48,768]{2,1,0:T(8,128)(2,1)}), bf16[32,48,768]{2,1,0:T(8,128)(2,1)}, u32[]{:S(2)}, u32[]{:S(2)}) async-start(bf16[32,48,768]{2,1,0:T(8,128)(2,1)} %bitcast.55), calls=%async_computation | async-start | bytes 4718592 | tf_op jit(solution)/shard_map/all_to_all | solution.py:297
  417.3 31.0 %all-to-all-done = bf16[32,48,768]{2,1,0:T(8,128)(2,1)} async-done(((bf16[32,48,768]{2,1,0:T(8,128)(2,1)}), bf16[32,48,768]{2,1,0:T(8,128)(2,1)}, u32[]{:S(2)}, u32[]{:S(2)}) %all-to-all-start) | async-done | bytes 2359328 | tf_op jit(solution)/shard_map/all_to_all | solution.py:297
  448.3 6.0 %all-to-all-start.1 = ((bf16[32,48,768]{2,1,0:T(8,128)(2,1)}), bf16[32,48,768]{2,1,0:T(8,128)(2,1)}, u32[]{:S(2)}, u32[]{:S(2)}) async-start(bf16[32,48,768]{2,1,0:T(8,128)(2,1)} %bitcast.56), calls=%async_computation.1 | async-start | bytes 4718592 | tf_op jit(solution)/shard_map/all_to_all | solution.py:297
  461.1 26.4 %all-to-all-done.1 = bf16[32,48,768]{2,1,0:T(8,128)(2,1)} async-done(((bf16[32,48,768]{2,1,0:T(8,128)(2,1)}), bf16[32,48,768]{2,1,0:T(8,128)(2,1)}, u32[]{:S(2)}, u32[]{:S(2)}) %all-to-all-start.1) | async-done | bytes 2359328 | tf_op jit(solution)/shard_map/all_to_all | solution.py:297
  (223 shorter events, 219.4 us)
Async XLA Ops:
  6.2 18.5 %collective-permute-start = (bf16[96,3840]{1,0:T(8,128)(2,1)}, bf16[96,3840]{1,0:T(8,128)(2,1)}, u32[]{:S(2)}, u32[]{:S(2)}) collective-permute-start(bf16[96,3840]{1,0:T(8,128)(2,1)} %get-tuple-element.38), channel_id=1, source_target_pairs={{0,16},{4,20},{8,24},{12,28},{16,0},{20,4},{24,8},{28,12},{32,48},... | collective-permute-start | bytes 2211848 | tf_op jit(solution)/shard_map/ppermute | solution.py:42
  28.7 17.7 %collective-permute-start.1 = (bf16[2,96,1920]{2,1,0:T(8,128)(2,1)}, bf16[2,96,1920]{2,1,0:T(8,128)(2,1)}, u32[]{:S(2)}, u32[]{:S(2)}) collective-permute-start(bf16[2,96,1920]{2,1,0:T(8,128)(2,1)} %get-tuple-element.34), channel_id=1, source_target_pairs={{0,12},{4,0},{8,4},{12,8},{16,28},{20,16},{24,20},{28,24},{32,44},... | collective-permute-start | bytes 2211848 | tf_op jit(solution)/shard_map/ppermute | solution.py:42
  29.2 19.1 %collective-permute-start.3 = (bf16[2,96,1920]{2,1,0:T(8,128)(2,1)}, bf16[2,96,1920]{2,1,0:T(8,128)(2,1)}, u32[]{:S(2)}, u32[]{:S(2)}) collective-permute-start(bf16[2,96,1920]{2,1,0:T(8,128)(2,1)} %get-tuple-element.34), channel_id=1, source_target_pairs={{0,4},{4,8},{8,12},{12,0},{16,20},{20,24},{24,28},{28,16},{32,36},... | collective-permute-start | bytes 2211848 | tf_op jit(solution)/shard_map/ppermute | solution.py:42
  30.7 22.9 %collective-permute-start.9 = (bf16[2,96,1920]{2,1,0:T(8,128)(2,1)}, bf16[2,96,1920]{2,1,0:T(8,128)(2,1)}, u32[]{:S(2)}, u32[]{:S(2)}) collective-permute-start(bf16[2,96,1920]{2,1,0:T(8,128)(2,1)} %get-tuple-element.33), channel_id=1, source_target_pairs={{0,96},{4,100},{8,104},{12,108},{16,112},{20,116},{24,120},{28,124... | collective-permute-start | bytes 2211848 | tf_op jit(solution)/shard_map/ppermute | solution.py:42
  33.7 24.4 %collective-permute-start.11 = (bf16[2,96,1920]{2,1,0:T(8,128)(2,1)}, bf16[2,96,1920]{2,1,0:T(8,128)(2,1)}, u32[]{:S(2)}, u32[]{:S(2)}) collective-permute-start(bf16[2,96,1920]{2,1,0:T(8,128)(2,1)} %get-tuple-element.33), channel_id=1, source_target_pairs={{0,32},{4,36},{8,40},{12,44},{16,48},{20,52},{24,56},{28,60},{32,6... | collective-permute-start | bytes 2211848 | tf_op jit(solution)/shard_map/ppermute | solution.py:42
  47.4 11.8 %collective-permute-start.2 = (bf16[1,96,1920]{2,1,0:T(8,128)(2,1)S(1)}, bf16[1,96,1920]{2,1,0:T(8,128)(2,1)S(1)}, u32[]{:S(2)}, u32[]{:S(2)}) collective-permute-start(bf16[1,96,1920]{2,1,0:T(8,128)(2,1)S(1)} %slice.143), channel_id=1, source_target_pairs={{0,12},{4,0},{8,4},{12,8},{16,28},{20,16},{24,20},{28,24},{32,44},... | collective-permute-start | bytes 1105928 | tf_op jit(solution)/shard_map/ppermute | solution.py:42
  49.3 10.4 %collective-permute-start.4 = (bf16[1,96,1920]{2,1,0:T(8,128)(2,1)S(1)}, bf16[1,96,1920]{2,1,0:T(8,128)(2,1)S(1)}, u32[]{:S(2)}, u32[]{:S(2)}) collective-permute-start(bf16[1,96,1920]{2,1,0:T(8,128)(2,1)S(1)} %slice.144), channel_id=1, source_target_pairs={{0,4},{4,8},{8,12},{12,0},{16,20},{20,24},{24,28},{28,16},{32,36},... | collective-permute-start | bytes 1105928 | tf_op jit(solution)/shard_map/ppermute | solution.py:42
  55.0 14.5 %collective-permute-start.10 = (bf16[1,96,1920]{2,1,0:T(8,128)(2,1)S(1)}, bf16[1,96,1920]{2,1,0:T(8,128)(2,1)S(1)}, u32[]{:S(2)}, u32[]{:S(2)}) collective-permute-start(bf16[1,96,1920]{2,1,0:T(8,128)(2,1)S(1)} %slice.149), channel_id=1, source_target_pairs={{0,96},{4,100},{8,104},{12,108},{16,112},{20,116},{24,120},{28,124... | collective-permute-start | bytes 1105928 | tf_op jit(solution)/shard_map/ppermute | solution.py:42
  59.1 10.4 %collective-permute-start.12 = (bf16[1,96,1920]{2,1,0:T(8,128)(2,1)S(1)}, bf16[1,96,1920]{2,1,0:T(8,128)(2,1)S(1)}, u32[]{:S(2)}, u32[]{:S(2)}) collective-permute-start(bf16[1,96,1920]{2,1,0:T(8,128)(2,1)S(1)} %slice.150), channel_id=1, source_target_pairs={{0,32},{4,36},{8,40},{12,44},{16,48},{20,52},{24,56},{28,60},{32,6... | collective-permute-start | bytes 1105928 | tf_op jit(solution)/shard_map/ppermute | solution.py:42
  66.5 63.6 %collective-permute-start.5 = (bf16[2,4,96,1920]{3,2,0,1:T(8,128)(2,1)S(1)}, bf16[2,4,96,1920]{3,2,0,1:T(8,128)(2,1)S(1)}, u32[]{:S(2)}, u32[]{:S(2)}) collective-permute-start(bf16[2,4,96,1920]{3,2,0,1:T(8,128)(2,1)S(1)} %bitcast.159), channel_id=1, source_target_pairs={{0,96},{4,100},{8,104},{12,108},{16,112},{20,116},{24,120},{28,124... | collective-permute-start | bytes 8847368 | tf_op jit(solution)/shard_map/ppermute | solution.py:42
  69.5 65.6 %collective-permute-start.7 = (bf16[2,4,96,1920]{3,2,0,1:T(8,128)(2,1)S(1)}, bf16[2,4,96,1920]{3,2,0,1:T(8,128)(2,1)S(1)}, u32[]{:S(2)}, u32[]{:S(2)}) collective-permute-start(bf16[2,4,96,1920]{3,2,0,1:T(8,128)(2,1)S(1)} %bitcast.160), channel_id=1, source_target_pairs={{0,32},{4,36},{8,40},{12,44},{16,48},{20,52},{24,56},{28,60},{32,6... | collective-permute-start | bytes 8847368 | tf_op jit(solution)/shard_map/ppermute | solution.py:42
  76.8 69.4 %collective-permute-start.13 = (bf16[4,2,96,1920]{3,2,1,0:T(8,128)(2,1)}, bf16[4,2,96,1920]{3,2,1,0:T(8,128)(2,1)}, u32[]{:S(2)}, u32[]{:S(2)}) collective-permute-start(bf16[4,2,96,1920]{3,2,1,0:T(8,128)(2,1)} %get-tuple-element.21), channel_id=1, source_target_pairs={{0,12},{4,0},{8,4},{12,8},{16,28},{20,16},{24,20},{28,24},{32,44},... | collective-permute-start | bytes 8847368 | tf_op jit(solution)/shard_map/ppermute | solution.py:42
  79.7 71.9 %collective-permute-start.15 = (bf16[4,2,96,1920]{3,2,1,0:T(8,128)(2,1)}, bf16[4,2,96,1920]{3,2,1,0:T(8,128)(2,1)}, u32[]{:S(2)}, u32[]{:S(2)}) collective-permute-start(bf16[4,2,96,1920]{3,2,1,0:T(8,128)(2,1)} %get-tuple-element.21), channel_id=1, source_target_pairs={{0,4},{4,8},{8,12},{12,0},{16,20},{20,24},{24,28},{28,16},{32,36},... | collective-permute-start | bytes 8847368 | tf_op jit(solution)/shard_map/ppermute | solution.py:42
  131.4 32.1 %collective-permute-start.6 = (bf16[1,4,96,1920]{3,2,0,1:T(8,128)(2,1)}, bf16[1,4,96,1920]{3,2,0,1:T(8,128)(2,1)}, u32[]{:S(2)}, u32[]{:S(2)}) collective-permute-start(bf16[1,4,96,1920]{3,2,0,1:T(8,128)(2,1)} %slice.145), channel_id=1, source_target_pairs={{0,96},{4,100},{8,104},{12,108},{16,112},{20,116},{24,120},{28,124... | collective-permute-start | bytes 4423688 | tf_op jit(solution)/shard_map/ppermute | solution.py:42
  138.0 31.9 %collective-permute-start.8 = (bf16[1,4,96,1920]{3,2,0,1:T(8,128)(2,1)}, bf16[1,4,96,1920]{3,2,0,1:T(8,128)(2,1)}, u32[]{:S(2)}, u32[]{:S(2)}) collective-permute-start(bf16[1,4,96,1920]{3,2,0,1:T(8,128)(2,1)} %slice.146), channel_id=1, source_target_pairs={{0,32},{4,36},{8,40},{12,44},{16,48},{20,52},{24,56},{28,60},{32,6... | collective-permute-start | bytes 4423688 | tf_op jit(solution)/shard_map/ppermute | solution.py:42
  148.9 72.6 %collective-permute-start.14 = (bf16[2,2,96,1920]{3,2,1,0:T(8,128)(2,1)}, bf16[2,2,96,1920]{3,2,1,0:T(8,128)(2,1)}, u32[]{:S(2)}, u32[]{:S(2)}) collective-permute-start(bf16[2,2,96,1920]{3,2,1,0:T(8,128)(2,1)} %slice.151), channel_id=1, source_target_pairs={{0,12},{4,0},{8,4},{12,8},{16,28},{20,16},{24,20},{28,24},{32,44},... | collective-permute-start | bytes 4423688 | tf_op jit(solution)/shard_map/ppermute | solution.py:42
  154.2 67.4 %collective-permute-start.16 = (bf16[2,2,96,1920]{3,2,1,0:T(8,128)(2,1)}, bf16[2,2,96,1920]{3,2,1,0:T(8,128)(2,1)}, u32[]{:S(2)}, u32[]{:S(2)}) collective-permute-start(bf16[2,2,96,1920]{3,2,1,0:T(8,128)(2,1)} %slice.152), channel_id=1, source_target_pairs={{0,4},{4,8},{8,12},{12,0},{16,20},{20,24},{24,28},{28,16},{32,36},... | collective-permute-start | bytes 4423688 | tf_op jit(solution)/shard_map/ppermute | solution.py:42
  279.2 21.5 %collective-permute-start.19 = (bf16[256,1536]{1,0:T(8,128)(2,1)}, bf16[256,1536]{1,0:T(8,128)(2,1)}, u32[]{:S(2)}, u32[]{:S(2)}) collective-permute-start(bf16[256,1536]{1,0:T(8,128)(2,1)} %convolution_convert_fusion.3), channel_id=1, source_target_pairs={{0,1},{1,0},{2,3},{3,2},{4,5},{5,4},{6,7},{7,6},{8,9},{9,8},{10,11... | collective-permute-start | bytes 2359304 | tf_op jit(solution)/shard_map/ppermute | solution.py:72
  292.5 20.2 %collective-permute-start.17 = (bf16[256,1536]{1,0:T(8,128)(2,1)S(1)}, bf16[256,1536]{1,0:T(8,128)(2,1)S(1)}, u32[]{:S(2)}, u32[]{:S(2)}) collective-permute-start(bf16[256,1536]{1,0:T(8,128)(2,1)S(1)} %convolution_convert_fusion.5), channel_id=1, source_target_pairs={{0,1},{1,0},{2,3},{3,2},{4,5},{5,4},{6,7},{7,6},{8,9},{9,8},{10,11... | collective-permute-start | bytes 2359304 | tf_op jit(solution)/shard_map/ppermute | solution.py:72
  317.2 15.5 %collective-permute-start.18 = (bf16[256,1536]{1,0:T(8,128)(2,1)S(1)}, bf16[256,1536]{1,0:T(8,128)(2,1)}, u32[]{:S(2)}, u32[]{:S(2)}) collective-permute-start(bf16[256,1536]{1,0:T(8,128)(2,1)S(1)} %get-tuple-element.14), channel_id=1, source_target_pairs={{0,1},{1,0},{4,5},{5,4},{8,9},{9,8},{12,13},{13,12},{16,17},{17,16... | collective-permute-start | bytes 2359304 | tf_op jit(solution)/shard_map/ppermute | solution.py:220
  319.8 21.3 %collective-permute-start.20 = (bf16[256,1536]{1,0:T(8,128)(2,1)S(1)}, bf16[256,1536]{1,0:T(8,128)(2,1)}, u32[]{:S(2)}, u32[]{:S(2)}) collective-permute-start(bf16[256,1536]{1,0:T(8,128)(2,1)S(1)} %get-tuple-element.24), channel_id=1, source_target_pairs={{0,1},{1,0},{4,5},{5,4},{8,9},{9,8},{12,13},{13,12},{16,17},{17,16... | collective-permute-start | bytes 2359304 | tf_op jit(solution)/shard_map/ppermute | solution.py:220
  343.9 6.6 %collective-permute-start.21 = (bf16[512,3072]{1,0:T(8,128)(2,1)S(1)}, bf16[512,3072]{1,0:T(8,128)(2,1)S(1)}, u32[]{:S(2)}, u32[]{:S(2)}) collective-permute-start(bf16[512,3072]{1,0:T(8,128)(2,1)S(1)} %pad_maximum_fusion.1), channel_id=1, source_target_pairs={{0,2},{1,3},{4,6},{5,7},{8,10},{9,11},{12,14},{13,15},{16,18},{17,... | collective-permute-start | bytes 9437192 | tf_op jit(solution)/shard_map/ppermute | solution.py:18
  406.9 41.5 %all-to-all-start = ((bf16[32,48,768]{2,1,0:T(8,128)(2,1)}), bf16[32,48,768]{2,1,0:T(8,128)(2,1)}, u32[]{:S(2)}, u32[]{:S(2)}) async-start(bf16[32,48,768]{2,1,0:T(8,128)(2,1)} %bitcast.55), calls=%async_computation | async-start | bytes 4718592 | tf_op jit(solution)/shard_map/all_to_all | solution.py:297
  448.3 39.1 %all-to-all-start.1 = ((bf16[32,48,768]{2,1,0:T(8,128)(2,1)}), bf16[32,48,768]{2,1,0:T(8,128)(2,1)}, u32[]{:S(2)}, u32[]{:S(2)}) async-start(bf16[32,48,768]{2,1,0:T(8,128)(2,1)} %bitcast.56), calls=%async_computation.1 | async-start | bytes 4718592 | tf_op jit(solution)/shard_map/all_to_all | solution.py:297
  (39 other events, 340.5 us)
